TPU v7x, 128 devices: a whole 4x4x4 slice. The times are simulated.
128 devices in a mesh: pp: 8 (over x, y_hi), ep: 16 (over z, y_lo, core).
Axes of the slice: x: 4, y: 4 (y_hi: 2, y_lo: 2; y = y_hi * 2 + y_lo), z: 4, core: 2. Of those that a mesh axis runs over, the one named last changes fastest.
Arguments:
- prev_out: bfloat16 [8, 2048, 7168], P('pp', 'ep'), may hold values from -6 to 6
- fwd_experts: int32 [8, 2048, 2], P('pp', 'ep'), may hold values from 0 to 7, all different within a row; in each aligned block of 128 rows (0 to 127, 128 to 255, ..., all dimensions but the last counted through in order) at most 48 rows name the same one
- expert_weights: bfloat16 [8, 16, 7168, 1024], P('pp', 'ep'), may hold values from -0.0625 to 0.0625
- bwd_experts: int32 [8, 2048, 2], P('pp', 'ep'), may hold values from 0 to 7, all different within a row; in each aligned block of 128 rows (0 to 127, 128 to 255, ..., all dimensions but the last counted through in order) at most 48 rows name the same one
- grad_hidden: bfloat16 [8, 16, 16, 48, 512], P('pp', 'ep'), may hold values from -6 to 6
- saved_pre: bfloat16 [8, 16, 16, 48, 1024], P('pp', 'ep'), may hold values from -6 to 6
Outputs:
- hidden_out: bfloat16 [8, 16, 16, 48, 512], P('pp', 'ep')
- grad_rows: bfloat16 [8, 2048, 7168], P('pp', 'ep')
Inputs may be any that keep to these rules, and one draw needn't show every extreme that they name: `fwd_experts`: each row names 2 different experts, and within the 128 rows of one device no expert is named more than 48 times. `bwd_experts`: each row names 2 different experts, and within the 128 rows of one device no expert is named more than 48 times.
All inputs are finite; a program needn't handle non-finite values.
Results may differ from a plain program's by a relative error of at most 0.0066.
Values may be sent and summed in bfloat16 or wider, within the bound.
No kernel may reach another device: no remote copies, remote signals or barrier semaphores. Data moves between devices by JAX's collectives and lax.ppermute only.
A program may use at most 128 MiB of HBM per device.

v0:
```python
import jax
import jax.numpy as jnp
from jax import lax
from jax.sharding import PartitionSpec as P


def shifted(block, axis, distance):
    devices = range(lax.axis_size(axis))
    route = [((i - distance) % len(devices), i) for i in devices]
    return lax.ppermute(block, axis, route)


def slot_table(route_ids, expert_count, capacity):
    token_count, choice_count = route_ids.shape
    flattened = route_ids.reshape(token_count * choice_count)
    onehot = (flattened[:, None] == jnp.arange(expert_count, dtype=jnp.int32)[None, :]).astype(
        jnp.int32
    )
    earlier = jnp.cumsum(onehot, axis=0) - onehot
    slot_index = jnp.sum(earlier * onehot, axis=1)
    slot_match = (slot_index[:, None] == jnp.arange(capacity, dtype=jnp.int32)[None, :]).astype(
        jnp.float32
    )
    expert_match = onehot.astype(jnp.float32)
    joined = jnp.einsum("re,rc->rec", expert_match, slot_match).reshape(
        token_count, choice_count, expert_count, capacity
    )
    return jnp.transpose(jnp.sum(joined, axis=1), (1, 2, 0))


def swiglu_backward(upstream, saved):
    hid_units = upstream.shape[-1]
    pre_float = saved.astype(jnp.float32)
    gate_pre = pre_float[..., :hid_units]
    up_pre = pre_float[..., hid_units:]
    sigmoid_gate = jax.nn.sigmoid(gate_pre)
    upstream_float = upstream.astype(jnp.float32)
    grad_gate = upstream_float * up_pre * sigmoid_gate * (1.0 + gate_pre * (1.0 - sigmoid_gate))
    grad_up = upstream_float * gate_pre * sigmoid_gate
    return jnp.concatenate([grad_gate, grad_up], axis=-1).astype(jnp.bfloat16)


def shards(prev_out, fwd_experts, expert_weights, bwd_experts, grad_hidden, saved_pre):
    groups = lax.axis_size("ep")
    experts = groups // 2
    capacity = grad_hidden.shape[3]
    hid_units = grad_hidden.shape[4]
    model_width = prev_out.shape[2]
    weights = expert_weights[0, 0]
    section_rows = shifted(prev_out[0], "pp", 1)
    fwd_table = slot_table(fwd_experts[0], experts, capacity).astype(jnp.bfloat16)
    picked = jnp.einsum(
        "ect,td->ecd", fwd_table, section_rows, preferred_element_type=jnp.float32
    ).astype(jnp.bfloat16)
    outgoing = jnp.broadcast_to(picked[:, None], (experts, 2, capacity, model_width)).reshape(
        groups, capacity, model_width
    )
    projected = jnp.einsum(
        "scd,dh->sch",
        lax.all_to_all(outgoing, "ep", split_axis=0, concat_axis=0, tiled=True),
        weights,
        preferred_element_type=jnp.float32,
    )
    hidden = (jax.nn.silu(projected[..., :hid_units]) * projected[..., hid_units:]).astype(
        jnp.bfloat16
    )
    grad_pre = swiglu_backward(grad_hidden[0, 0], saved_pre[0, 0])
    partial_rows = jnp.einsum(
        "sch,dh->scd", grad_pre, weights, preferred_element_type=jnp.float32
    ).astype(jnp.bfloat16)
    bwd_table = slot_table(bwd_experts[0], experts, capacity).astype(jnp.bfloat16)
    returned = lax.all_to_all(partial_rows, "ep", split_axis=0, concat_axis=0, tiled=True)
    paired = returned.reshape(experts, 2, capacity, model_width).astype(jnp.float32)
    summed = (paired[:, 0] + paired[:, 1]).astype(jnp.bfloat16)
    grad_in = jnp.einsum(
        "ect,ecd->td", bwd_table, summed, preferred_element_type=jnp.float32
    ).astype(jnp.bfloat16)
    grad_rows = shifted(grad_in, "pp", -1)
    return (hidden[None, None], grad_rows[None])


def solution(mesh):
    placed = (
        P("pp", "ep", None),
        P("pp", "ep", None),
        P("pp", "ep", None, None),
        P("pp", "ep", None),
        P("pp", "ep", None, None, None),
        P("pp", "ep", None, None, None),
    )
    return jax.shard_map(
        shards,
        mesh=mesh,
        in_specs=placed,
        out_specs=(P("pp", "ep", None, None, None), P("pp", "ep", None)),
        check_vma=False,
    )
```

profile of v0, /device:TPU:30, one launch (start us, length us, event | category | flops | bytes accessed | tf_op | source)
XLA Modules:
  0.0 387.3 jit_solution(2584681451831286190)
XLA Ops:
  0.6 1.9 bitcast_convert_fusion
  2.5 0.8 fusion.15
  3.3 19.2 %fusion.4 = bf16[16,48,7168]{2,1,0:T(8,128)(2,1)} fusion(bf16[1,1,7168,1024]{3,2,1,0:T(8,128)(2,1)} %param.8, bf16[16,48,512]{2,1,0:T(8,128)(2,1)S(1)} %get-tuple-element.3, bf16[16,48,512]{2,1,0:T(8,128)(2,1)S(1)} %get-tuple-element.2), kind=kOutput, calls=%fused_computation.4 | convolution fusion | flops 11282939904 | bytes 27262976 | tf_op jit(solution)/shard_map/sch,dh->scd/dot_general | solution.py:68
  22.5 6.9 %all-to-all-start.1 = ((bf16[16,48,7168]{2,1,0:T(8,128)(2,1)}), bf16[16,48,7168]{2,1,0:T(8,128)(2,1)}, u32[]{:S(2)}, u32[]{:S(2)}) async-start(bf16[16,48,7168]{2,1,0:T(8,128)(2,1)} %fusion.4), calls=%async_computation.1 | async-start | bytes 22020096 | tf_op jit(solution)/shard_map/all_to_all | solution.py:72
  29.4 1.2 collective-permute-start
  30.7 0.1 eq.80
  30.8 0.1 eq.76
  31.0 0.6 reduce-window.14
  31.6 0.2 slice_reduce_fusion.1
  31.8 0.1 copy.27
  32.2 0.3 bitcast_reduce_fusion.1
  32.5 0.2 copy.36
  32.7 157.6 %collective-permute-done = bf16[128,7168]{1,0:T(8,128)(2,1)S(1)} collective-permute-done((bf16[128,7168]{1,0:T(8,128)(2,1)}, bf16[128,7168]{1,0:T(8,128)(2,1)S(1)}, u32[]{:S(2)}, u32[]{:S(2)}) %collective-permute-start) | collective-permute-done | bytes 1835040 | tf_op jit(solution)/shard_map/ppermute | solution.py:10
  190.3 4.0 %convolution_convert_fusion = bf16[8,48,7168]{2,1,0:T(8,128)(2,1)} fusion(bf16[128,7168]{1,0:T(8,128)(2,1)S(1)} %collective-permute-done, bf16[128,8,48]{0,2,1:T(8,128)(2,1)S(1)} %copy.36), kind=kOutput, calls=%fused_computation.9 | convolution fusion | flops 707395584 | bytes 7438336 | tf_op jit(solution)/shard_map/ect,td->ecd/dot_general | solution.py:52
  194.3 7.8 %broadcast_in_dim.6 = bf16[8,2,48,7168]{3,2,1,0:T(8,128)(2,1)} broadcast(bf16[8,48,7168]{2,1,0:T(8,128)(2,1)} %convolution_convert_fusion), dimensions={0,2,3} | broadcast | bytes 16515072 | tf_op jit(solution)/shard_map/broadcast_in_dim | solution.py:55
  202.1 5.5 %all-to-all-start = ((bf16[16,48,7168]{2,1,0:T(8,128)(2,1)}), bf16[16,48,7168]{2,1,0:T(8,128)(2,1)}, u32[]{:S(2)}, u32[]{:S(2)}) async-start(bf16[16,48,7168]{2,1,0:T(8,128)(2,1)} %bitcast.68), calls=%async_computation | async-start | bytes 22020096 | tf_op jit(solution)/shard_map/all_to_all | solution.py:60
  207.8 0.1 eq.91
  207.9 0.1 eq.87
  208.0 0.6 reduce-window.16
  208.6 0.2 slice_reduce_fusion
  208.9 0.1 copy.31
  209.2 0.3 bitcast_reduce_fusion
  209.6 0.2 copy.37
  209.8 5.8 %convert.21 = f32[8,2,48,7168]{3,2,1,0:T(8,128)S(1)} convert(bf16[8,2,48,7168]{3,2,1,0:T(8,128)(2,1)} %bitcast.20) | non-fusion elementwise | flops 5505024 | bytes 33030144 | tf_op jit(solution)/shard_map/convert_element_type | solution.py:73
  215.6 1.7 fusion.9
  217.3 0.3 collective-permute-start.1
  217.6 149.3 %collective-permute-done.1 = bf16[128,7168]{1,0:T(8,128)(2,1)S(1)} collective-permute-done((bf16[128,7168]{1,0:T(8,128)(2,1)S(1)}, bf16[128,7168]{1,0:T(8,128)(2,1)S(1)}, u32[]{:S(2)}, u32[]{:S(2)}) %collective-permute-start.1) | collective-permute-done | bytes 1835040 | tf_op jit(solution)/shard_map/ppermute | solution.py:10
  366.9 1.2 copy-done
  368.1 16.5 %fusion.2 = f32[16,48,1024]{2,1,0:T(8,128)S(1)} fusion(bf16[16,48,7168]{2,1,0:T(8,128)(2,1)} %all-to-all-done, bf16[1,1,7168,1024]{3,2,1,0:T(8,128)(2,1)} %param.8), kind=kOutput, calls=%fused_computation.2 | convolution fusion | flops 11274289152 | bytes 28835840 | tf_op jit(solution)/shard_map/scd,dh->sch/dot_general | solution.py:58
  384.6 1.4 fusion.22
  386.0 0.1 copy-done.1
  386.1 1.2 copy.41
  (24 shorter events, 0.7 us)
Async XLA Ops:
  0.6 1.9 copy-start.2
  22.5 8.1 %copy-start.3 = (s32[1,128,2]{1,2,0:T(2,128)S(1)}, s32[1,128,2]{1,2,0:T(2,128)}, u32[]{:S(2)}) copy-start(s32[1,128,2]{1,2,0:T(2,128)} %param.7) | copy-start | bytes 3076
  22.5 171.8 %all-to-all-start.1 = ((bf16[16,48,7168]{2,1,0:T(8,128)(2,1)}), bf16[16,48,7168]{2,1,0:T(8,128)(2,1)}, u32[]{:S(2)}, u32[]{:S(2)}) async-start(bf16[16,48,7168]{2,1,0:T(8,128)(2,1)} %fusion.4), calls=%async_computation.1 | async-start | bytes 22020096 | tf_op jit(solution)/shard_map/all_to_all | solution.py:72
  29.4 160.9 %collective-permute-start = (bf16[128,7168]{1,0:T(8,128)(2,1)}, bf16[128,7168]{1,0:T(8,128)(2,1)S(1)}, u32[]{:S(2)}, u32[]{:S(2)}) collective-permute-start(bf16[128,7168]{1,0:T(8,128)(2,1)} %bitcast.70), channel_id=1, source_target_pairs={{112,0},{0,16},{16,32},{32,48},{48,64},{64,80},{80,96},{96,112},{1... | collective-permute-start | bytes 5505032 | tf_op jit(solution)/shard_map/ppermute | solution.py:10
  202.1 5.5 %copy-start.4 = (s32[1,128,2]{1,2,0:T(2,128)S(1)}, s32[1,128,2]{1,2,0:T(2,128)}, u32[]{:S(2)}) copy-start(s32[1,128,2]{1,2,0:T(2,128)} %param.9) | copy-start | bytes 3076
  202.1 166.0 %all-to-all-start = ((bf16[16,48,7168]{2,1,0:T(8,128)(2,1)}), bf16[16,48,7168]{2,1,0:T(8,128)(2,1)}, u32[]{:S(2)}, u32[]{:S(2)}) async-start(bf16[16,48,7168]{2,1,0:T(8,128)(2,1)} %bitcast.68), calls=%async_computation | async-start | bytes 22020096 | tf_op jit(solution)/shard_map/all_to_all | solution.py:60
  217.3 149.6 %collective-permute-start.1 = (bf16[128,7168]{1,0:T(8,128)(2,1)S(1)}, bf16[128,7168]{1,0:T(8,128)(2,1)S(1)}, u32[]{:S(2)}, u32[]{:S(2)}) collective-permute-start(bf16[128,7168]{1,0:T(8,128)(2,1)S(1)} %fusion.9), channel_id=1, source_target_pairs={{16,0},{32,16},{48,32},{64,48},{80,64},{96,80},{112,96},{0,112},{1... | collective-permute-start | bytes 5505032 | tf_op jit(solution)/shard_map/ppermute | solution.py:10
  366.9 1.2 copy-start
  384.6 1.5 copy-start.1
where the time goes:
time: 392 us; the launch traced here: 387 us
  waiting for transfers between devices  307 us (78%)
  matrix products  41.3 us (11%)
  starting transfers between devices  13.8 us (4%)
  local copies, waits for them, and re-layouts  12.3 us (3%)
  other arithmetic  12.2 us (3%)
    ppermute x2, waiting for transfers between devices, shifted(): return lax.ppermute(block, axis, route)  307 us
    dot_general x1, matrix products, shards(): jnp.einsum('sch,dh->scd', grad_pre, weights, preferred_element_type=jnp.f...  19.2 us
    dot_general x1, matrix products, shards(): jnp.einsum('scd,dh->sch', lax.all_to_all(outgoing, 'ep', split_axis=0, co...  16.5 us
  transfers between devices with their start and end apart: 4, of which 2 were waited for; matrix products, arithmetic and copies ran while one was open for 4% of the time, Pallas kernels for 0%

commit v1 on v0

v1 whole, which is shorter than its diff:
```python
import numpy as np
import jax
import jax.numpy as jnp
from jax import lax
from jax.sharding import Mesh
from jax.sharding import PartitionSpec as P

PP = ("x", "yhi")
EP = ("z", "ylo", "core")
CHIPS = ("z", "ylo")
RING = ("x", "yhi", "ylo")


def ring_route(sections, distance):
    route = []
    for p in range(sections):
        for lo in range(2):
            route.append((p * 2 + lo, ((p + distance) % sections) * 2 + (1 - lo)))
    return route


def swap_ylo(block):
    return lax.ppermute(block, "ylo", [(0, 1), (1, 0)])


def slot_table(route_ids, expert_count, capacity):
    token_count, choice_count = route_ids.shape
    flattened = route_ids.reshape(token_count * choice_count)
    onehot = (flattened[:, None] == jnp.arange(expert_count, dtype=jnp.int32)[None, :]).astype(
        jnp.int32
    )
    earlier = jnp.cumsum(onehot, axis=0) - onehot
    slot_index = jnp.sum(earlier * onehot, axis=1)
    slot_match = (slot_index[:, None] == jnp.arange(capacity, dtype=jnp.int32)[None, :]).astype(
        jnp.float32
    )
    expert_match = onehot.astype(jnp.float32)
    joined = jnp.einsum("re,rc->rec", expert_match, slot_match).reshape(
        token_count, choice_count, expert_count, capacity
    )
    return jnp.transpose(jnp.sum(joined, axis=1), (1, 2, 0))


def swiglu_backward(upstream, saved):
    hid_units = upstream.shape[-1]
    pre_float = saved.astype(jnp.float32)
    gate_pre = pre_float[..., :hid_units]
    up_pre = pre_float[..., hid_units:]
    sigmoid_gate = jax.nn.sigmoid(gate_pre)
    upstream_float = upstream.astype(jnp.float32)
    grad_gate = upstream_float * up_pre * sigmoid_gate * (1.0 + gate_pre * (1.0 - sigmoid_gate))
    grad_up = upstream_float * gate_pre * sigmoid_gate
    return jnp.concatenate([grad_gate, grad_up], axis=-1).astype(jnp.bfloat16)


def make_shards(sections, zs):
    def shards(prev_out, fwd_experts, expert_weights, bwd_experts, grad_hidden, saved_pre):
        experts = 2 * zs
        capacity = grad_hidden.shape[3]
        hid_units = grad_hidden.shape[4]
        model_width = prev_out.shape[2]
        weights = expert_weights[0, 0]
        core = lax.axis_index("core")

        rows = lax.ppermute(prev_out[0], RING, ring_route(sections, 1))
        fwd_ids = swap_ylo(fwd_experts[0])
        fwd_table = slot_table(fwd_ids, experts, capacity).astype(jnp.bfloat16)
        picked = jnp.einsum(
            "ect,td->ecd", fwd_table, rows, preferred_element_type=jnp.float32
        ).astype(jnp.bfloat16)
        arrived = lax.all_to_all(picked, CHIPS, split_axis=0, concat_axis=0, tiled=True)
        both = lax.all_gather(arrived, "core", axis=0, tiled=False)
        projected = jnp.einsum(
            "scd,dh->sch",
            both.reshape(2 * experts, capacity, model_width),
            weights,
            preferred_element_type=jnp.float32,
        )
        hidden = (jax.nn.silu(projected[..., :hid_units]) * projected[..., hid_units:]).astype(
            jnp.bfloat16
        )
        hidden = hidden.reshape(2, zs, 2, capacity, hid_units)[:, :, ::-1]
        hidden = jnp.transpose(hidden, (1, 2, 0, 3, 4)).reshape(2 * experts, capacity, hid_units)

        upstream = grad_hidden[0, 0].reshape(zs, 2, 2, capacity, hid_units)
        saved = saved_pre[0, 0].reshape(zs, 2, 2, capacity, 2 * hid_units)
        keep_pre = swiglu_backward(
            lax.dynamic_index_in_dim(upstream, core, axis=2, keepdims=False),
            lax.dynamic_index_in_dim(saved, core, axis=2, keepdims=False),
        )
        send_pre = swiglu_backward(
            lax.dynamic_index_in_dim(upstream, 1 - core, axis=2, keepdims=False),
            lax.dynamic_index_in_dim(saved, 1 - core, axis=2, keepdims=False),
        )
        send_part = jnp.einsum(
            "zych,dh->zycd", send_pre, weights, preferred_element_type=jnp.float32
        ).astype(jnp.bfloat16)
        other_part = lax.ppermute(send_part, "core", [(0, 1), (1, 0)])
        keep_part = jnp.einsum(
            "zych,dh->zycd", keep_pre, weights, preferred_element_type=jnp.float32
        ).astype(jnp.bfloat16)
        pair_sum = (keep_part.astype(jnp.float32) + other_part.astype(jnp.float32)).astype(
            jnp.bfloat16
        )
        outgoing = pair_sum[:, ::-1].reshape(experts, capacity, model_width)
        returned = lax.all_to_all(outgoing, CHIPS, split_axis=0, concat_axis=0, tiled=True)
        bwd_ids = swap_ylo(bwd_experts[0])
        bwd_table = slot_table(bwd_ids, experts, capacity).astype(jnp.bfloat16)
        grad_in = jnp.einsum(
            "ect,ecd->td", bwd_table, returned, preferred_element_type=jnp.float32
        ).astype(jnp.bfloat16)
        grad_rows = lax.ppermute(grad_in, RING, ring_route(sections, -1))
        return (hidden[None, None], grad_rows[None])

    return shards


def solution(mesh):
    sections = mesh.shape["pp"]
    groups = mesh.shape["ep"]
    zs = groups // 4
    devices = np.asarray(mesh.devices).reshape(sections // 2, 2, zs, 2, 2)
    fine = Mesh(devices, PP + EP)
    placed = (
        P(PP, EP, None),
        P(PP, EP, None),
        P(PP, EP, None, None),
        P(PP, EP, None),
        P(PP, EP, None, None, None),
        P(PP, EP, None, None, None),
    )
    return jax.shard_map(
        make_shards(sections, zs),
        mesh=fine,
        in_specs=placed,
        out_specs=(P(PP, EP, None, None, None), P(PP, EP, None)),
        check_vma=False,
    )
```

time: 392 us -> 291 us (0.74)
  waiting for transfers between devices: 307 us -> 176 us
  matrix products: 41.3 us -> 67.5 us
  between operations: 0.79 us -> 14.2 us
  other arithmetic: 12.2 us -> 6.24 us
    ppermute x2 -> x5, waiting for transfers between devices: 307 us -> 135 us  [the longest x2 58.3 us: swap_ylo(): return lax.ppermute(block, 'ylo', [(0, 1), (1, 0)])]
    all_to_all x2, waiting for transfers between devices: 0.01 us -> 40.3 us  [the longest x1 40.1 us: shards(): lax.all_to_all(picked, CHIPS, split_axis=0, concat_axis=0, tiled=True)]
    dot_general x4 -> x5, matrix products: 41.3 us -> 67.5 us  [the longest x1 22 us: shards(): jnp.einsum('zych,dh->zycd', keep_pre, weights, preferred_element_type=jnp...]
    broadcast_in_dim x1 -> x0, local copies, waits for them, and re-layouts: 7.8 us -> none  [shards(): jnp.broadcast_to(picked[:, None], (experts, 2, capacity, model_width))]
    convert_element_type x1, other arithmetic: 5.84 us -> 0.51 us  [shards(): (jax.nn.silu(projected[..., :hid_units]) * projected[..., hid_units:]).as...]
    rev x0 -> x1, local copies, waits for them, and re-layouts: none -> 5.31 us  [shards(): outgoing = pair_sum[:, ::-1].reshape(experts, capacity, model_width)]
  transfers between devices with their start and end apart: 4 -> 8, of which waited for: 2 -> 5; matrix products, arithmetic and copies ran while one was open for 4% -> 21% of each run, Pallas kernels for 0% -> 0%
where the time goes in v1:
time: 291 us; the launch traced here: 289 us
  waiting for transfers between devices  176 us (60%)
  matrix products  67.5 us (23%)
  starting transfers between devices  16.3 us (6%)
  between operations  14.2 us (5%)
  local copies, waits for them, and re-layouts  9.41 us (3%)
  other arithmetic  6.24 us (2%)
    ppermute x2, waiting for transfers between devices, swap_ylo(): return lax.ppermute(block, 'ylo', [(0, 1), (1, 0)])  58.3 us
    ppermute x1, waiting for transfers between devices, shards(): grad_rows = lax.ppermute(grad_in, RING, ring_route(sections, -1))  40.5 us
    all_to_all x1, waiting for transfers between devices, shards(): lax.all_to_all(picked, CHIPS, split_axis=0, concat_axis=0, tiled=True)  40.1 us
    ppermute x1, waiting for transfers between devices, shards(): rows = lax.ppermute(prev_out[0], RING, ring_route(sections, 1))  36.5 us
    dot_general x1, matrix products, shards(): jnp.einsum('zych,dh->zycd', keep_pre, weights, preferred_element_type=jnp...  22 us
    dot_general x1, matrix products, shards(): jnp.einsum('zych,dh->zycd', send_pre, weights, preferred_element_type=jnp...  21.4 us
    dot_general x1, matrix products, shards(): jnp.einsum('scd,dh->sch', both.reshape(2 * experts, capacity, model_width...  16.5 us
    all_to_all x1, starting transfers between devices, shards(): lax.all_to_all(picked, CHIPS, split_axis=0, concat_axis=0, tiled=True)  6.9 us
  transfers between devices with their start and end apart: 8, of which 5 were waited for; matrix products, arithmetic and copies ran while one was open for 21% of the time, Pallas kernels for 0%

profile of v1, /device:TPU:30, one launch (start us, length us, event | category | flops | bytes accessed | tf_op | source)
XLA Modules:
  0.0 289.2 jit_solution(14322601096663883309)
XLA Ops:
  7.3 1.1 collective-permute-start
  8.4 1.8 bitcast_convert_fusion.1
  10.1 1.6 fusion.19
  11.9 0.1 eq.80
  12.0 0.1 eq.76
  12.2 0.6 reduce-window.14
  12.8 0.2 slice_reduce_fusion.1
  13.4 0.3 bitcast_reduce_fusion.1
  13.7 0.2 copy.56
  13.9 36.5 %collective-permute-done.1 = bf16[128,7168]{1,0:T(8,128)(2,1)S(1)} collective-permute-done((bf16[128,7168]{1,0:T(8,128)(2,1)}, bf16[128,7168]{1,0:T(8,128)(2,1)S(1)}, u32[]{:S(2)}, u32[]{:S(2)}) %collective-permute-start.1) | collective-permute-done | bytes 1835040 | tf_op jit(solution)/shard_map/ppermute | solution.py:65
  50.4 4.0 %convolution_convert_fusion = bf16[8,48,7168]{2,1,0:T(8,128)(2,1)} fusion(bf16[128,7168]{1,0:T(8,128)(2,1)S(1)} %collective-permute-done.1, bf16[128,8,48]{0,2,1:T(8,128)(2,1)S(1)} %copy.56), kind=kOutput, calls=%fused_computation.9 | convolution fusion | flops 707395584 | bytes 7438336 | tf_op jit(solution)/shard_map/ect,td->ecd/dot_general | solution.py:68
  54.4 6.9 %all-to-all-start = ((bf16[8,48,7168]{2,1,0:T(8,128)(2,1)}), bf16[8,48,7168]{2,1,0:T(8,128)(2,1)}, u32[]{:S(2)}, u32[]{:S(2)}) async-start(bf16[8,48,7168]{2,1,0:T(8,128)(2,1)} %convolution_convert_fusion), calls=%async_computation | async-start | bytes 11010048 | tf_op jit(solution)/shard_map/all_to_all | solution.py:71
  61.3 21.4 %fusion.9 = bf16[4,2,48,7168]{3,2,1,0:T(8,128)(2,1)} fusion(bf16[1,1,7168,1024]{3,2,1,0:T(8,128)(2,1)} %param.8, bf16[4,2,48,512]{3,2,1,0:T(8,128)(2,1)S(1)} %copy-done.1, bf16[4,2,48,512]{3,2,1,0:T(8,128)(2,1)S(1)} %copy-done.2), kind=kOutput, calls=%fused_computation.8 | convolution fusion | flops 5641469952 | bytes 20971520 | tf_op jit(solution)/shard_map/zych,dh->zycd/dot_general | solution.py:95
  82.7 40.1 %all-to-all-done = bf16[8,48,7168]{2,1,0:T(8,128)(2,1)} async-done(((bf16[8,48,7168]{2,1,0:T(8,128)(2,1)}), bf16[8,48,7168]{2,1,0:T(8,128)(2,1)}, u32[]{:S(2)}, u32[]{:S(2)}) %all-to-all-start) | async-done | bytes 5505056 | tf_op jit(solution)/shard_map/all_to_all | solution.py:71
  122.8 22.0 %add_convert_fusion = bf16[4,2,48,7168]{3,2,1,0:T(8,128)(2,1)} fusion(bf16[4,2,48,7168]{3,2,1,0:T(8,128)(2,1)} %collective-permute-done.3, bf16[1,1,7168,1024]{3,2,1,0:T(8,128)(2,1)} %param.8, bf16[4,2,48,512]{3,2,1,0:T(8,128)(2,1)S(1)} %get-tuple-element.3, bf16[4,2,48,512]{3,2,1,0:T(8,128)(2,1)S(1)} %get-tuple-element.2), kind=kOutput, calls=%fused_computation.6 | convolution fusion | flops 5652480000 | bytes 26476544 | tf_op jit(solution)/shard_map/zych,dh->zycd/dot_general | solution.py:99
  144.8 5.3 %rev.7 = bf16[4,2,48,7168]{3,2,1,0:T(8,128)(2,1)} reverse(bf16[4,2,48,7168]{3,2,1,0:T(8,128)(2,1)} %add_convert_fusion), dimensions={1} | reverse | bytes 11010048 | tf_op jit(solution)/shard_map/rev | solution.py:105
  150.1 5.9 %all-to-all-start.1 = ((bf16[8,48,7168]{2,1,0:T(8,128)(2,1)}), bf16[8,48,7168]{2,1,0:T(8,128)(2,1)}, u32[]{:S(2)}, u32[]{:S(2)}) async-start(bf16[8,48,7168]{2,1,0:T(8,128)(2,1)} %bitcast.79), calls=%async_computation.1 | async-start | bytes 11010048 | tf_op jit(solution)/shard_map/all_to_all | solution.py:106
  156.0 0.2 collective-permute-start.2
  156.3 58.3 %collective-permute-done.2 = s32[128,2]{0,1:T(2,128)S(1)} collective-permute-done((s32[128,2]{0,1:T(2,128)S(1)}, s32[128,2]{0,1:T(2,128)S(1)}, u32[]{:S(2)}, u32[]{:S(2)}) %collective-permute-start.2) | collective-permute-done | bytes 1056 | tf_op jit(solution)/shard_map/ppermute | solution.py:23
  214.8 0.1 eq.87
  215.0 0.6 reduce-window.16
  215.6 0.2 slice_reduce_fusion
  216.2 0.3 bitcast_reduce_fusion
  216.5 0.2 copy.57
  216.7 0.2 all-to-all-done.1
  216.9 3.7 %fusion.14 = bf16[128,7168]{1,0:T(8,128)(2,1)S(1)} fusion(bf16[8,48,7168]{2,1,0:T(8,128)(2,1)} %all-to-all-done.1, bf16[128,8,48]{0,2,1:T(8,128)(2,1)S(1)} %copy.57), kind=kOutput, calls=%fused_computation.11 | convolution fusion | flops 705560576 | bytes 7438336 | tf_op jit(solution)/shard_map/ect,ecd->td/dot_general | solution.py:109
  220.6 2.1 collective-permute-start.4
  222.7 40.5 %collective-permute-done.4 = bf16[128,7168]{1,0:T(8,128)(2,1)S(1)} collective-permute-done((bf16[128,7168]{1,0:T(8,128)(2,1)S(1)}, bf16[128,7168]{1,0:T(8,128)(2,1)S(1)}, u32[]{:S(2)}, u32[]{:S(2)}) %collective-permute-start.4) | collective-permute-done | bytes 1835040 | tf_op jit(solution)/shard_map/ppermute | solution.py:112
  263.2 16.5 %fusion = f32[16,48,1024]{2,1,0:T(8,128)S(1)} fusion(bf16[16,48,7168]{2,1,0:T(8,128)(2,1)} %all-gather.3.cloned.1.call-done, bf16[1,1,7168,1024]{3,2,1,0:T(8,128)(2,1)} %param.8), kind=kOutput, calls=%fused_computation | convolution fusion | flops 11274289152 | bytes 28835840 | tf_op jit(solution)/shard_map/scd,dh->sch/dot_general | solution.py:73
  279.6 0.5 fusion.16
  280.2 0.9 copy.46
  281.2 1.2 copy.63
  (33 shorter events, 1.3 us)
Async XLA Ops:
  7.2 3.0 %copy-start = (bf16[1,1,16,48,512]{4,3,2,1,0:T(8,128)(2,1)S(1)}, bf16[1,1,16,48,512]{4,3,2,1,0:T(8,128)(2,1)}, u32[]{:S(2)}) copy-start(bf16[1,1,16,48,512]{4,3,2,1,0:T(8,128)(2,1)} %param.10) | copy-start | bytes 2359300
  7.2 43.2 %collective-permute-start.1 = (bf16[128,7168]{1,0:T(8,128)(2,1)}, bf16[128,7168]{1,0:T(8,128)(2,1)S(1)}, u32[]{:S(2)}, u32[]{:S(2)}) collective-permute-start(bf16[128,7168]{1,0:T(8,128)(2,1)} %bitcast.85), channel_id=1, source_target_pairs={{0,18},{2,16},{16,34},{18,32},{32,50},{34,48},{48,66},{50,64},{64,... | collective-permute-start | bytes 5505032 | tf_op jit(solution)/shard_map/ppermute | solution.py:65
  7.3 4.5 %collective-permute-start = (s32[128,2]{0,1:T(2,128)}, s32[128,2]{0,1:T(2,128)S(1)}, u32[]{:S(2)}, u32[]{:S(2)}) collective-permute-start(s32[128,2]{0,1:T(2,128)} %bitcast.86), channel_id=1, source_target_pairs={{0,2},{2,0},{1,3},{3,1},{4,6},{6,4},{5,7},{7,5},{8,10},{10,8},{9,1... | collective-permute-start | bytes 3080 | tf_op jit(solution)/shard_map/ppermute | solution.py:23
  54.4 6.9 %copy-start.1 = (bf16[4,2,48,512]{3,2,1,0:T(8,128)(2,1)S(1)}, bf16[4,2,48,512]{3,2,1,0:T(8,128)(2,1)}, u32[]{:S(2)}) copy-start(bf16[4,2,48,512]{3,2,1,0:T(8,128)(2,1)} %get-tuple-element.8) | copy-start | bytes 1179652
  54.4 6.9 %copy-start.2 = (bf16[4,2,48,512]{3,2,1,0:T(8,128)(2,1)S(1)}, bf16[4,2,48,512]{3,2,1,0:T(8,128)(2,1)}, u32[]{:S(2)}) copy-start(bf16[4,2,48,512]{3,2,1,0:T(8,128)(2,1)} %get-tuple-element.9) | copy-start | bytes 1179652
  54.4 68.4 %all-to-all-start = ((bf16[8,48,7168]{2,1,0:T(8,128)(2,1)}), bf16[8,48,7168]{2,1,0:T(8,128)(2,1)}, u32[]{:S(2)}, u32[]{:S(2)}) async-start(bf16[8,48,7168]{2,1,0:T(8,128)(2,1)} %convolution_convert_fusion), calls=%async_computation | async-start | bytes 11010048 | tf_op jit(solution)/shard_map/all_to_all | solution.py:71
  61.3 201.9 %all-gather.3.cloned.1.call-start = ((), (), s32[]{:S(2)}) async-start(), calls=%async_computation.2 | async-start | bytes 16515072 | tf_op jit(solution)/shard_map/all_gather | solution.py:72
  82.7 40.2 %collective-permute-start.3 = (bf16[4,2,48,7168]{3,2,1,0:T(8,128)(2,1)}, bf16[4,2,48,7168]{3,2,1,0:T(8,128)(2,1)}, u32[]{:S(2)}, u32[]{:S(2)}) collective-permute-start(bf16[4,2,48,7168]{3,2,1,0:T(8,128)(2,1)} %fusion.9), channel_id=1, source_target_pairs={{0,1},{1,0},{2,3},{3,2},{4,5},{5,4},{6,7},{7,6},{8,9},{9,8},{10,11... | collective-permute-start | bytes 16515080 | tf_op jit(solution)/shard_map/ppermute | solution.py:98
  150.1 5.9 %copy-start.3 = (s32[1,128,2]{1,2,0:T(2,128)S(1)}, s32[1,128,2]{1,2,0:T(2,128)}, u32[]{:S(2)}) copy-start(s32[1,128,2]{1,2,0:T(2,128)} %param.9) | copy-start | bytes 3076
  150.1 66.8 %all-to-all-start.1 = ((bf16[8,48,7168]{2,1,0:T(8,128)(2,1)}), bf16[8,48,7168]{2,1,0:T(8,128)(2,1)}, u32[]{:S(2)}, u32[]{:S(2)}) async-start(bf16[8,48,7168]{2,1,0:T(8,128)(2,1)} %bitcast.79), calls=%async_computation.1 | async-start | bytes 11010048 | tf_op jit(solution)/shard_map/all_to_all | solution.py:106
  156.0 58.5 %collective-permute-start.2 = (s32[128,2]{0,1:T(2,128)S(1)}, s32[128,2]{0,1:T(2,128)S(1)}, u32[]{:S(2)}, u32[]{:S(2)}) collective-permute-start(s32[128,2]{0,1:T(2,128)S(1)} %bitcast.87), channel_id=1, source_target_pairs={{0,2},{2,0},{1,3},{3,1},{4,6},{6,4},{5,7},{7,5},{8,10},{10,8},{9,1... | collective-permute-start | bytes 3080 | tf_op jit(solution)/shard_map/ppermute | solution.py:23
  220.6 42.5 %collective-permute-start.4 = (bf16[128,7168]{1,0:T(8,128)(2,1)S(1)}, bf16[128,7168]{1,0:T(8,128)(2,1)S(1)}, u32[]{:S(2)}, u32[]{:S(2)}) collective-permute-start(bf16[128,7168]{1,0:T(8,128)(2,1)S(1)} %fusion.14), channel_id=1, source_target_pairs={{0,114},{2,112},{16,2},{18,0},{32,18},{34,16},{48,34},{50,32},{64,... | collective-permute-start | bytes 5505032 | tf_op jit(solution)/shard_map/ppermute | solution.py:112
Sparse Core Ops, SparseCore 0:
  123.0 26.1 all-gather.2

commit v2 on v1

--- a/solution.py
+++ b/solution.py
@@ -53,22 +53,55 @@
     return jnp.concatenate([grad_gate, grad_up], axis=-1).astype(jnp.bfloat16)
 
 
+def chip_route(chips, k):
+    return [(j, j ^ k) for j in range(chips)]
+
+
 def make_shards(sections, zs):
+    chips = 2 * zs
+
     def shards(prev_out, fwd_experts, expert_weights, bwd_experts, grad_hidden, saved_pre):
-        experts = 2 * zs
+        experts = chips
         capacity = grad_hidden.shape[3]
         hid_units = grad_hidden.shape[4]
         model_width = prev_out.shape[2]
         weights = expert_weights[0, 0]
         core = lax.axis_index("core")
+        me = lax.axis_index("z") * 2 + lax.axis_index("ylo")
+        peer = me ^ jnp.arange(chips, dtype=jnp.int32)
+        worked = (peer // 2) * 4 + (1 - peer % 2) * 2
+
+        ids = swap_ylo(jnp.concatenate([fwd_experts[0], bwd_experts[0]], axis=1))
+        fwd_ids = ids[:, : fwd_experts.shape[2]]
+        bwd_ids = ids[:, fwd_experts.shape[2] :]
 
         rows = lax.ppermute(prev_out[0], RING, ring_route(sections, 1))
-        fwd_ids = swap_ylo(fwd_experts[0])
+
+        order = jnp.concatenate([worked + core, worked + 1 - core])
+        upstream = jnp.take(grad_hidden[0, 0], order, axis=0)
+        saved = jnp.take(saved_pre[0, 0], order, axis=0)
+        grad_pre = swiglu_backward(upstream, saved).reshape(2, chips, capacity, 2 * hid_units)
+        partial_rows = jnp.einsum(
+            "kech,dh->kecd", grad_pre, weights, preferred_element_type=jnp.float32
+        ).astype(jnp.bfloat16)
+        other_part = lax.ppermute(partial_rows[1], "core", [(0, 1), (1, 0)])
+        pair_sum = (partial_rows[0].astype(jnp.float32) + other_part.astype(jnp.float32)).astype(
+            jnp.bfloat16
+        )
+        returned = [pair_sum[0]] + [
+            lax.ppermute(pair_sum[k], CHIPS, chip_route(chips, k)) for k in range(1, chips)
+        ]
+        rows, _ = lax.optimization_barrier((rows, pair_sum))
+
         fwd_table = slot_table(fwd_ids, experts, capacity).astype(jnp.bfloat16)
+        fwd_table = jnp.take(fwd_table, peer, axis=0)
         picked = jnp.einsum(
             "ect,td->ecd", fwd_table, rows, preferred_element_type=jnp.float32
         ).astype(jnp.bfloat16)
-        arrived = lax.all_to_all(picked, CHIPS, split_axis=0, concat_axis=0, tiled=True)
+        arrived = jnp.stack(
+            [picked[0]]
+            + [lax.ppermute(picked[k], CHIPS, chip_route(chips, k)) for k in range(1, chips)]
+        )
         both = lax.all_gather(arrived, "core", axis=0, tiled=False)
         projected = jnp.einsum(
             "scd,dh->sch",
@@ -79,35 +112,14 @@
         hidden = (jax.nn.silu(projected[..., :hid_units]) * projected[..., hid_units:]).astype(
             jnp.bfloat16
         )
-        hidden = hidden.reshape(2, zs, 2, capacity, hid_units)[:, :, ::-1]
-        hidden = jnp.transpose(hidden, (1, 2, 0, 3, 4)).reshape(2 * experts, capacity, hid_units)
+        blocks = jnp.arange(2 * experts, dtype=jnp.int32)
+        chip_of = (blocks // 4) * 2 + (1 - (blocks // 2) % 2)
+        hidden = jnp.take(hidden, (blocks % 2) * chips + (chip_of ^ me), axis=0)
 
-        upstream = grad_hidden[0, 0].reshape(zs, 2, 2, capacity, hid_units)
-        saved = saved_pre[0, 0].reshape(zs, 2, 2, capacity, 2 * hid_units)
-        keep_pre = swiglu_backward(
-            lax.dynamic_index_in_dim(upstream, core, axis=2, keepdims=False),
-            lax.dynamic_index_in_dim(saved, core, axis=2, keepdims=False),
-        )
-        send_pre = swiglu_backward(
-            lax.dynamic_index_in_dim(upstream, 1 - core, axis=2, keepdims=False),
-            lax.dynamic_index_in_dim(saved, 1 - core, axis=2, keepdims=False),
-        )
-        send_part = jnp.einsum(
-            "zych,dh->zycd", send_pre, weights, preferred_element_type=jnp.float32
-        ).astype(jnp.bfloat16)
-        other_part = lax.ppermute(send_part, "core", [(0, 1), (1, 0)])
-        keep_part = jnp.einsum(
-            "zych,dh->zycd", keep_pre, weights, preferred_element_type=jnp.float32
-        ).astype(jnp.bfloat16)
-        pair_sum = (keep_part.astype(jnp.float32) + other_part.astype(jnp.float32)).astype(
-            jnp.bfloat16
-        )
-        outgoing = pair_sum[:, ::-1].reshape(experts, capacity, model_width)
-        returned = lax.all_to_all(outgoing, CHIPS, split_axis=0, concat_axis=0, tiled=True)
-        bwd_ids = swap_ylo(bwd_experts[0])
         bwd_table = slot_table(bwd_ids, experts, capacity).astype(jnp.bfloat16)
+        bwd_table = jnp.take(bwd_table, peer, axis=0)
         grad_in = jnp.einsum(
-            "ect,ecd->td", bwd_table, returned, preferred_element_type=jnp.float32
+            "ect,ecd->td", bwd_table, jnp.stack(returned), preferred_element_type=jnp.float32
         ).astype(jnp.bfloat16)
         grad_rows = lax.ppermute(grad_in, RING, ring_route(sections, -1))
         return (hidden[None, None], grad_rows[None])

time: 291 us -> 363 us (1.25)
  waiting for transfers between devices: 176 us -> 233 us
  matrix products: 67.5 us -> 39.7 us
  local copies, waits for them, and re-layouts: 9.41 us -> 33.8 us
  starting transfers between devices: 16.3 us -> 25.8 us
  other arithmetic: 6.24 us -> 15.2 us
    ppermute x1 -> x15, waiting for transfers between devices: 0.01 us -> 159 us  [the longest x7 128 us: shards(): lax.ppermute(picked[k], CHIPS, chip_route(chips, k))]
    ppermute x2 -> x1, waiting for transfers between devices: 58.3 us -> 1.85 us  [swap_ylo(): return lax.ppermute(block, 'ylo', [(0, 1), (1, 0)])]
    all_to_all x2 -> x0, waiting for transfers between devices: 40.3 us -> none  [the longest x1 40.1 us: shards(): lax.all_to_all(picked, CHIPS, split_axis=0, concat_axis=0, tiled=True)]
    dot_general x3 -> x2, matrix products: 47.1 us -> 21.5 us  [the longest x1 17.7 us: shards(): jnp.einsum('kech,dh->kecd', grad_pre, weights, preferred_element_type=jnp...]
    ppermute x1 -> x15, starting transfers between devices: 0.01 us -> 21.8 us  [the longest x7 12.9 us: shards(): lax.ppermute(pair_sum[k], CHIPS, chip_route(chips, k))]
    unnamed x11 -> x23, local copies, waits for them, and re-layouts: 1.63 us -> 15.3 us
    all_to_all x2 -> x0, starting transfers between devices: 12.8 us -> none  [the longest x1 6.9 us: shards(): lax.all_to_all(picked, CHIPS, split_axis=0, concat_axis=0, tiled=True)]
    squeeze x0 -> x3, local copies, waits for them, and re-layouts: none -> 9.03 us  [the longest x1 5.32 us: shards(): other_part = lax.ppermute(partial_rows[1], 'core', [(0, 1), (1, 0)])]
  transfers between devices with their start and end apart: 8 -> 19, of which waited for: 5 -> 13; matrix products, arithmetic and copies ran while one was open for 21% -> 9% of each run, Pallas kernels for 0% -> 0%
where the time goes in v2:
time: 363 us; the launch traced here: 362 us
  waiting for transfers between devices  233 us (64%)
  matrix products  39.7 us (11%)
  local copies, waits for them, and re-layouts  33.8 us (9%)
  starting transfers between devices  25.8 us (7%)
  other arithmetic  15.2 us (4%)
  between operations  14.3 us (4%)
    ppermute x7, waiting for transfers between devices, shards(): lax.ppermute(picked[k], CHIPS, chip_route(chips, k))  128 us
    ppermute x1, waiting for transfers between devices, shards(): grad_rows = lax.ppermute(grad_in, RING, ring_route(sections, -1))  43.2 us
    ppermute x7, waiting for transfers between devices, shards(): lax.ppermute(pair_sum[k], CHIPS, chip_route(chips, k))  31.5 us
    ppermute x1, waiting for transfers between devices, shards(): rows = lax.ppermute(prev_out[0], RING, ring_route(sections, 1))  28.6 us
    dot_general x1, matrix products, shards(): jnp.einsum('kech,dh->kecd', grad_pre, weights, preferred_element_type=jnp...  17.7 us
    dot_general x1, matrix products, shards(): jnp.einsum('scd,dh->sch', both.reshape(2 * experts, capacity, model_width...  16.6 us
    unnamed x23, local copies, waits for them, and re-layouts  15.3 us
    ppermute x7, starting transfers between devices, shards(): lax.ppermute(pair_sum[k], CHIPS, chip_route(chips, k))  12.9 us
  transfers between devices with their start and end apart: 19, of which 13 were waited for; matrix products, arithmetic and copies ran while one was open for 9% of the time, Pallas kernels for 0%

profile of v2, /device:TPU:30, one launch (start us, length us, event | category | flops | bytes accessed | tf_op | source)
XLA Modules:
  0.0 361.9 jit_solution(9785324596857847333)
XLA Ops:
  8.6 1.8 gather_fusion
  10.4 1.7 select_convert_fusion
  12.1 2.6 gather_fusion.2
  14.7 3.1 fusion.12
  17.7 17.7 %fusion.4 = bf16[2,8,48,7168]{3,2,1,0:T(8,128)(2,1)} fusion(bf16[1,1,7168,1024]{3,2,1,0:T(8,128)(2,1)} %param.12, bf16[2,8,48,512]{3,2,1,0:T(8,128)(2,1)} %bitcast.120, bf16[2,8,48,512]{3,2,1,0:T(8,128)(2,1)} %bitcast.119), kind=kOutput, calls=%fused_computation.9 | convolution fusion | flops 11282939904 | bytes 27262976 | tf_op jit(solution)/shard_map/kech,dh->kecd/dot_general | solution.py:84
  35.5 5.3 %slice_bitcast_fusion = bf16[8,48,7168]{2,1,0:T(8,128)(2,1)} fusion(bf16[2,8,48,7168]{3,2,1,0:T(8,128)(2,1)} %fusion.4), kind=kLoop, calls=%fused_computation.15 | loop fusion | bytes 11010048 | tf_op jit(solution)/shard_map/squeeze | solution.py:87
  42.7 1.8 collective-permute-done
  50.2 6.4 %fusion.7 = bf16[8,48,7168]{2,1,0:T(8,128)(2,1)S(1)} fusion(bf16[8,48,7168]{2,1,0:T(8,128)(2,1)} %collective-permute-done.2, bf16[2,8,48,7168]{3,2,1,0:T(8,128)(2,1)} %fusion.4), kind=kLoop, calls=%fused_computation.11 | loop fusion | flops 11010048 | bytes 16515072 | tf_op jit(solution)/shard_map/convert_element_type | solution.py:88
  56.6 28.6 %collective-permute-done.1 = bf16[128,7168]{1,0:T(8,128)(2,1)S(1)} collective-permute-done((bf16[128,7168]{1,0:T(8,128)(2,1)}, bf16[128,7168]{1,0:T(8,128)(2,1)S(1)}, u32[]{:S(2)}, u32[]{:S(2)}) %collective-permute-start.1) | collective-permute-done | bytes 1835040 | tf_op jit(solution)/shard_map/ppermute | solution.py:78
  88.1 2.5 slice_bitcast_fusion.2
  90.6 2.0 collective-permute-start.10
  92.6 1.9 collective-permute-start.11
  94.5 3.6 collective-permute-start.13
  98.1 8.4 %collective-permute-done.3 = bf16[48,7168]{1,0:T(8,128)(2,1)S(1)} collective-permute-done((bf16[48,7168]{1,0:T(8,128)(2,1)S(1)}, bf16[48,7168]{1,0:T(8,128)(2,1)S(1)}, u32[]{:S(2)}, u32[]{:S(2)}) %collective-permute-start.3) | collective-permute-done | bytes 688160 | tf_op jit(solution)/shard_map/ppermute | solution.py:103
  106.4 1.9 collective-permute-start.4
  109.3 44.1 %collective-permute-done.4 = bf16[48,7168]{1,0:T(8,128)(2,1)S(1)} collective-permute-done((bf16[48,7168]{1,0:T(8,128)(2,1)S(1)}, bf16[48,7168]{1,0:T(8,128)(2,1)S(1)}, u32[]{:S(2)}, u32[]{:S(2)}) %collective-permute-start.4) | collective-permute-done | bytes 688160 | tf_op jit(solution)/shard_map/ppermute | solution.py:103
  155.8 13.9 %collective-permute-done.5 = bf16[48,7168]{1,0:T(8,128)(2,1)S(1)} collective-permute-done((bf16[48,7168]{1,0:T(8,128)(2,1)S(1)}, bf16[48,7168]{1,0:T(8,128)(2,1)S(1)}, u32[]{:S(2)}, u32[]{:S(2)}) %collective-permute-start.5) | collective-permute-done | bytes 688160 | tf_op jit(solution)/shard_map/ppermute | solution.py:103
  169.7 3.6 collective-permute-start.6
  174.2 13.4 %collective-permute-done.6 = bf16[48,7168]{1,0:T(8,128)(2,1)S(1)} collective-permute-done((bf16[48,7168]{1,0:T(8,128)(2,1)S(1)}, bf16[48,7168]{1,0:T(8,128)(2,1)S(1)}, u32[]{:S(2)}, u32[]{:S(2)}) %collective-permute-start.6) | collective-permute-done | bytes 688160 | tf_op jit(solution)/shard_map/ppermute | solution.py:103
  187.6 1.6 collective-permute-start.7
  190.2 15.2 %collective-permute-done.7 = bf16[48,7168]{1,0:T(8,128)(2,1)S(1)} collective-permute-done((bf16[48,7168]{1,0:T(8,128)(2,1)S(1)}, bf16[48,7168]{1,0:T(8,128)(2,1)S(1)}, u32[]{:S(2)}, u32[]{:S(2)}) %collective-permute-start.7) | collective-permute-done | bytes 688160 | tf_op jit(solution)/shard_map/ppermute | solution.py:103
  206.3 14.8 %collective-permute-done.8 = bf16[48,7168]{1,0:T(8,128)(2,1)S(1)} collective-permute-done((bf16[48,7168]{1,0:T(8,128)(2,1)S(1)}, bf16[48,7168]{1,0:T(8,128)(2,1)S(1)}, u32[]{:S(2)}, u32[]{:S(2)}) %collective-permute-start.8) | collective-permute-done | bytes 688160 | tf_op jit(solution)/shard_map/ppermute | solution.py:103
  222.3 17.8 %collective-permute-done.9 = bf16[48,7168]{1,0:T(8,128)(2,1)S(1)} collective-permute-done((bf16[48,7168]{1,0:T(8,128)(2,1)S(1)}, bf16[48,7168]{1,0:T(8,128)(2,1)S(1)}, u32[]{:S(2)}, u32[]{:S(2)}) %collective-permute-start.9) | collective-permute-done | bytes 688160 | tf_op jit(solution)/shard_map/ppermute | solution.py:103
  240.0 2.8 collective-permute-start.14
  244.8 2.5 collective-permute-start.16
  250.1 11.6 %collective-permute-done.14 = bf16[48,7168]{1,0:T(8,128)(2,1)S(1)} collective-permute-done((bf16[48,7168]{1,0:T(8,128)(2,1)}, bf16[48,7168]{1,0:T(8,128)(2,1)S(1)}, u32[]{:S(2)}, u32[]{:S(2)}) %collective-permute-start.14) | collective-permute-done | bytes 688160 | tf_op jit(solution)/shard_map/ppermute | solution.py:92
  262.6 19.9 %collective-permute-done.15 = bf16[48,7168]{1,0:T(8,128)(2,1)S(1)} collective-permute-done((bf16[48,7168]{1,0:T(8,128)(2,1)}, bf16[48,7168]{1,0:T(8,128)(2,1)S(1)}, u32[]{:S(2)}, u32[]{:S(2)}) %collective-permute-start.15) | collective-permute-done | bytes 688160 | tf_op jit(solution)/shard_map/ppermute | solution.py:92
  284.4 3.8 %fusion.8 = bf16[128,7168]{1,0:T(8,128)(2,1)S(1)} fusion(bf16[8,48,7168]{2,1,0:T(8,128)(2,1)} %bitcast_dynamic-update-slice_fusion, bf16[8,48,128]{2,1,0:T(8,128)(2,1)S(1)} %gather_fusion.4, pred[8]{0:T(512)(128)(4,1)S(1)} %compare_and_fusion.2), kind=kOutput, calls=%fused_computation.14 | convolution fusion | flops 705609728 | bytes 7438344 | tf_op jit(solution)/shard_map/ect,ecd->td/dot_general | solution.py:121
  288.2 2.1 collective-permute-start.17
  290.3 43.2 %collective-permute-done.17 = bf16[128,7168]{1,0:T(8,128)(2,1)} collective-permute-done((bf16[128,7168]{1,0:T(8,128)(2,1)S(1)}, bf16[128,7168]{1,0:T(8,128)(2,1)}, u32[]{:S(2)}, u32[]{:S(2)}) %collective-permute-start.17) | collective-permute-done | bytes 1835040 | tf_op jit(solution)/shard_map/ppermute | solution.py:124
  333.5 16.6 %fusion = f32[16,48,1024]{2,1,0:T(8,128)S(1)} fusion(bf16[16,48,7168]{2,1,0:T(8,128)(2,1)} %all-gather.3.cloned.1.call-done, bf16[1,1,7168,1024]{3,2,1,0:T(8,128)(2,1)} %param.12), kind=kOutput, calls=%fused_computation.5 | convolution fusion | flops 11274289152 | bytes 28835840 | tf_op jit(solution)/shard_map/scd,dh->sch/dot_general | solution.py:106
  352.2 2.8 copy.52
  (88 shorter events, 28.5 us)
Async XLA Ops:
  7.2 1.4 copy-start
  7.2 326.3 %all-gather.3.cloned.1.call-start = ((), (), s32[]{:S(2)}) async-start(), calls=%async_computation | async-start | bytes 16515072 | tf_op jit(solution)/shard_map/all_gather | solution.py:105
  35.5 5.3 %copy-start.2 = (s32[1,128,2]{1,2,0:T(2,128)S(1)}, s32[1,128,2]{1,2,0:T(2,128)}, u32[]{:S(2)}) copy-start(s32[1,128,2]{1,2,0:T(2,128)} %param.13) | copy-start | bytes 3076
  35.5 5.3 %copy-start.3 = (s32[1,128,2]{1,2,0:T(2,128)S(1)}, s32[1,128,2]{1,2,0:T(2,128)}, u32[]{:S(2)}) copy-start(s32[1,128,2]{1,2,0:T(2,128)} %param.11) | copy-start | bytes 3076
  40.8 9.4 %collective-permute-start.2 = (bf16[8,48,7168]{2,1,0:T(8,128)(2,1)}, bf16[8,48,7168]{2,1,0:T(8,128)(2,1)}, u32[]{:S(2)}, u32[]{:S(2)}) collective-permute-start(bf16[8,48,7168]{2,1,0:T(8,128)(2,1)} %slice_bitcast_fusion), channel_id=1, source_target_pairs={{0,1},{1,0},{2,3},{3,2},{4,5},{5,4},{6,7},{7,6},{8,9},{9,8},{10,11... | collective-permute-start | bytes 16515080 | tf_op jit(solution)/shard_map/ppermute | solution.py:87
  40.8 3.7 %collective-permute-start = (s32[128,4]{0,1:T(4,128)S(1)}, s32[128,4]{0,1:T(4,128)S(1)}, u32[]{:S(2)}, u32[]{:S(2)}) collective-permute-start(s32[128,4]{0,1:T(4,128)S(1)} %pad_add_fusion), channel_id=1, source_target_pairs={{0,2},{2,0},{1,3},{3,1},{4,6},{6,4},{5,7},{7,5},{8,10},{10,8},{9,1... | collective-permute-start | bytes 6152 | tf_op jit(solution)/shard_map/ppermute | solution.py:23
  41.7 43.6 %collective-permute-start.1 = (bf16[128,7168]{1,0:T(8,128)(2,1)}, bf16[128,7168]{1,0:T(8,128)(2,1)S(1)}, u32[]{:S(2)}, u32[]{:S(2)}) collective-permute-start(bf16[128,7168]{1,0:T(8,128)(2,1)} %bitcast.6), channel_id=1, source_target_pairs={{0,18},{2,16},{16,34},{18,32},{32,50},{34,48},{48,66},{50,64},{64,... | collective-permute-start | bytes 5505032 | tf_op jit(solution)/shard_map/ppermute | solution.py:78
  88.1 18.4 %collective-permute-start.3 = (bf16[48,7168]{1,0:T(8,128)(2,1)S(1)}, bf16[48,7168]{1,0:T(8,128)(2,1)S(1)}, u32[]{:S(2)}, u32[]{:S(2)}) collective-permute-start(bf16[48,7168]{1,0:T(8,128)(2,1)S(1)} %get-tuple-element.22), channel_id=1, source_target_pairs={{0,2},{2,0},{4,6},{6,4},{8,10},{10,8},{12,14},{14,12},{1,3},{3,1},... | collective-permute-start | bytes 2064392 | tf_op jit(solution)/shard_map/ppermute | solution.py:103
  90.6 153.2 %collective-permute-start.10 = (bf16[48,7168]{1,0:T(8,128)(2,1)}, bf16[48,7168]{1,0:T(8,128)(2,1)S(1)}, u32[]{:S(2)}, u32[]{:S(2)}) collective-permute-start(bf16[48,7168]{1,0:T(8,128)(2,1)} %get-tuple-element.14), channel_id=1, source_target_pairs={{0,2},{2,0},{4,6},{6,4},{8,10},{10,8},{12,14},{14,12},{1,3},{3,1},... | collective-permute-start | bytes 2064392 | tf_op jit(solution)/shard_map/ppermute | solution.py:92
  92.6 152.2 %collective-permute-start.11 = (bf16[48,7168]{1,0:T(8,128)(2,1)}, bf16[48,7168]{1,0:T(8,128)(2,1)S(1)}, u32[]{:S(2)}, u32[]{:S(2)}) collective-permute-start(bf16[48,7168]{1,0:T(8,128)(2,1)} %get-tuple-element.13), channel_id=1, source_target_pairs={{0,4},{2,6},{4,0},{6,2},{8,12},{10,14},{12,8},{14,10},{1,5},{3,7},... | collective-permute-start | bytes 2064392 | tf_op jit(solution)/shard_map/ppermute | solution.py:92
  94.5 153.7 %collective-permute-start.12 = (bf16[48,7168]{1,0:T(8,128)(2,1)}, bf16[48,7168]{1,0:T(8,128)(2,1)S(1)}, u32[]{:S(2)}, u32[]{:S(2)}) collective-permute-start(bf16[48,7168]{1,0:T(8,128)(2,1)} %get-tuple-element.12), channel_id=1, source_target_pairs={{0,6},{2,4},{4,2},{6,0},{8,14},{10,12},{12,10},{14,8},{1,7},{3,5},... | collective-permute-start | bytes 2064392 | tf_op jit(solution)/shard_map/ppermute | solution.py:92
  94.5 154.7 %collective-permute-start.13 = (bf16[48,7168]{1,0:T(8,128)(2,1)}, bf16[48,7168]{1,0:T(8,128)(2,1)S(1)}, u32[]{:S(2)}, u32[]{:S(2)}) collective-permute-start(bf16[48,7168]{1,0:T(8,128)(2,1)} %get-tuple-element.11), channel_id=1, source_target_pairs={{0,8},{2,10},{4,12},{6,14},{8,0},{10,2},{12,4},{14,6},{1,9},{3,11}... | collective-permute-start | bytes 2064392 | tf_op jit(solution)/shard_map/ppermute | solution.py:92
  106.4 46.9 %collective-permute-start.4 = (bf16[48,7168]{1,0:T(8,128)(2,1)S(1)}, bf16[48,7168]{1,0:T(8,128)(2,1)S(1)}, u32[]{:S(2)}, u32[]{:S(2)}) collective-permute-start(bf16[48,7168]{1,0:T(8,128)(2,1)S(1)} %get-tuple-element.21), channel_id=1, source_target_pairs={{0,4},{2,6},{4,0},{6,2},{8,12},{10,14},{12,8},{14,10},{1,5},{3,7},... | collective-permute-start | bytes 2064392 | tf_op jit(solution)/shard_map/ppermute | solution.py:103
  153.4 16.3 %collective-permute-start.5 = (bf16[48,7168]{1,0:T(8,128)(2,1)S(1)}, bf16[48,7168]{1,0:T(8,128)(2,1)S(1)}, u32[]{:S(2)}, u32[]{:S(2)}) collective-permute-start(bf16[48,7168]{1,0:T(8,128)(2,1)S(1)} %get-tuple-element.20), channel_id=1, source_target_pairs={{0,6},{2,4},{4,2},{6,0},{8,14},{10,12},{12,10},{14,8},{1,7},{3,5},... | collective-permute-start | bytes 2064392 | tf_op jit(solution)/shard_map/ppermute | solution.py:103
  169.7 17.9 %collective-permute-start.6 = (bf16[48,7168]{1,0:T(8,128)(2,1)S(1)}, bf16[48,7168]{1,0:T(8,128)(2,1)S(1)}, u32[]{:S(2)}, u32[]{:S(2)}) collective-permute-start(bf16[48,7168]{1,0:T(8,128)(2,1)S(1)} %get-tuple-element.19), channel_id=1, source_target_pairs={{0,8},{2,10},{4,12},{6,14},{8,0},{10,2},{12,4},{14,6},{1,9},{3,11}... | collective-permute-start | bytes 2064392 | tf_op jit(solution)/shard_map/ppermute | solution.py:103
  187.6 17.8 %collective-permute-start.7 = (bf16[48,7168]{1,0:T(8,128)(2,1)S(1)}, bf16[48,7168]{1,0:T(8,128)(2,1)S(1)}, u32[]{:S(2)}, u32[]{:S(2)}) collective-permute-start(bf16[48,7168]{1,0:T(8,128)(2,1)S(1)} %get-tuple-element.18), channel_id=1, source_target_pairs={{0,10},{2,8},{4,14},{6,12},{8,2},{10,0},{12,6},{14,4},{1,11},{3,9}... | collective-permute-start | bytes 2064392 | tf_op jit(solution)/shard_map/ppermute | solution.py:103
  205.4 15.7 %collective-permute-start.8 = (bf16[48,7168]{1,0:T(8,128)(2,1)S(1)}, bf16[48,7168]{1,0:T(8,128)(2,1)S(1)}, u32[]{:S(2)}, u32[]{:S(2)}) collective-permute-start(bf16[48,7168]{1,0:T(8,128)(2,1)S(1)} %get-tuple-element.17), channel_id=1, source_target_pairs={{0,12},{2,14},{4,8},{6,10},{8,4},{10,6},{12,0},{14,2},{1,13},{3,15... | collective-permute-start | bytes 2064392 | tf_op jit(solution)/shard_map/ppermute | solution.py:103
  221.1 18.9 %collective-permute-start.9 = (bf16[48,7168]{1,0:T(8,128)(2,1)S(1)}, bf16[48,7168]{1,0:T(8,128)(2,1)S(1)}, u32[]{:S(2)}, u32[]{:S(2)}) collective-permute-start(bf16[48,7168]{1,0:T(8,128)(2,1)S(1)} %get-tuple-element.16), channel_id=1, source_target_pairs={{0,14},{2,12},{4,10},{6,8},{8,6},{10,4},{12,2},{14,0},{1,15},{3,13... | collective-permute-start | bytes 2064392 | tf_op jit(solution)/shard_map/ppermute | solution.py:103
  240.0 21.7 %collective-permute-start.14 = (bf16[48,7168]{1,0:T(8,128)(2,1)}, bf16[48,7168]{1,0:T(8,128)(2,1)S(1)}, u32[]{:S(2)}, u32[]{:S(2)}) collective-permute-start(bf16[48,7168]{1,0:T(8,128)(2,1)} %get-tuple-element.10), channel_id=1, source_target_pairs={{0,10},{2,8},{4,14},{6,12},{8,2},{10,0},{12,6},{14,4},{1,11},{3,9}... | collective-permute-start | bytes 2064392 | tf_op jit(solution)/shard_map/ppermute | solution.py:92
  243.8 38.7 %collective-permute-start.15 = (bf16[48,7168]{1,0:T(8,128)(2,1)}, bf16[48,7168]{1,0:T(8,128)(2,1)S(1)}, u32[]{:S(2)}, u32[]{:S(2)}) collective-permute-start(bf16[48,7168]{1,0:T(8,128)(2,1)} %get-tuple-element.9), channel_id=1, source_target_pairs={{0,12},{2,14},{4,8},{6,10},{8,4},{10,6},{12,0},{14,2},{1,13},{3,15... | collective-permute-start | bytes 2064392 | tf_op jit(solution)/shard_map/ppermute | solution.py:92
  244.8 38.7 %collective-permute-start.16 = (bf16[48,7168]{1,0:T(8,128)(2,1)}, bf16[48,7168]{1,0:T(8,128)(2,1)S(1)}, u32[]{:S(2)}, u32[]{:S(2)}) collective-permute-start(bf16[48,7168]{1,0:T(8,128)(2,1)} %get-tuple-element.8), channel_id=1, source_target_pairs={{0,14},{2,12},{4,10},{6,8},{8,6},{10,4},{12,2},{14,0},{1,15},{3,13... | collective-permute-start | bytes 2064392 | tf_op jit(solution)/shard_map/ppermute | solution.py:92
  288.2 45.3 %collective-permute-start.17 = (bf16[128,7168]{1,0:T(8,128)(2,1)S(1)}, bf16[128,7168]{1,0:T(8,128)(2,1)}, u32[]{:S(2)}, u32[]{:S(2)}) collective-permute-start(bf16[128,7168]{1,0:T(8,128)(2,1)S(1)} %fusion.8), channel_id=1, source_target_pairs={{0,114},{2,112},{16,2},{18,0},{32,18},{34,16},{48,34},{50,32},{64,... | collective-permute-start | bytes 5505032 | tf_op jit(solution)/shard_map/ppermute | solution.py:124
  333.5 21.6 %copy-start.1 = (bf16[1,1,16,48,1024]{4,3,2,1,0:T(8,128)(2,1)S(1)}, bf16[1,1,16,48,1024]{4,3,2,1,0:T(8,128)(2,1)}, u32[]{:S(2)}) copy-start(bf16[1,1,16,48,1024]{4,3,2,1,0:T(8,128)(2,1)} %param.15) | copy-start | bytes 4718596
Sparse Core Ops, SparseCore 0:
  243.9 25.6 all-gather.2

commit v3 on v2

--- a/solution.py
+++ b/solution.py
@@ -53,10 +53,6 @@
     return jnp.concatenate([grad_gate, grad_up], axis=-1).astype(jnp.bfloat16)
 
 
-def chip_route(chips, k):
-    return [(j, j ^ k) for j in range(chips)]
-
-
 def make_shards(sections, zs):
     chips = 2 * zs
 
@@ -67,9 +63,8 @@
         model_width = prev_out.shape[2]
         weights = expert_weights[0, 0]
         core = lax.axis_index("core")
-        me = lax.axis_index("z") * 2 + lax.axis_index("ylo")
-        peer = me ^ jnp.arange(chips, dtype=jnp.int32)
-        worked = (peer // 2) * 4 + (1 - peer % 2) * 2
+        chip = jnp.arange(chips, dtype=jnp.int32)
+        worked = (chip // 2) * 4 + (1 - chip % 2) * 2
 
         ids = swap_ylo(jnp.concatenate([fwd_experts[0], bwd_experts[0]], axis=1))
         fwd_ids = ids[:, : fwd_experts.shape[2]]
@@ -88,20 +83,22 @@
         pair_sum = (partial_rows[0].astype(jnp.float32) + other_part.astype(jnp.float32)).astype(
             jnp.bfloat16
         )
-        returned = [pair_sum[0]] + [
-            lax.ppermute(pair_sum[k], CHIPS, chip_route(chips, k)) for k in range(1, chips)
-        ]
-        rows, _ = lax.optimization_barrier((rows, pair_sum))
+        returned = lax.all_to_all(pair_sum, CHIPS, split_axis=0, concat_axis=0, tiled=True)
+        rows, returned = lax.optimization_barrier((rows, returned))
 
         fwd_table = slot_table(fwd_ids, experts, capacity).astype(jnp.bfloat16)
-        fwd_table = jnp.take(fwd_table, peer, axis=0)
         picked = jnp.einsum(
             "ect,td->ecd", fwd_table, rows, preferred_element_type=jnp.float32
         ).astype(jnp.bfloat16)
-        arrived = jnp.stack(
-            [picked[0]]
-            + [lax.ppermute(picked[k], CHIPS, chip_route(chips, k)) for k in range(1, chips)]
-        )
+        bwd_table = slot_table(bwd_ids, experts, capacity).astype(jnp.bfloat16)
+        grad_in = jnp.einsum(
+            "ect,ecd->td", bwd_table, returned, preferred_element_type=jnp.float32
+        ).astype(jnp.bfloat16)
+        picked, grad_in = lax.optimization_barrier((picked, grad_in))
+        grad_rows = lax.ppermute(grad_in, RING, ring_route(sections, -1))
+
+        arrived = lax.all_to_all(picked, CHIPS, split_axis=0, concat_axis=0, tiled=True)
+
         both = lax.all_gather(arrived, "core", axis=0, tiled=False)
         projected = jnp.einsum(
             "scd,dh->sch",
@@ -112,16 +109,9 @@
         hidden = (jax.nn.silu(projected[..., :hid_units]) * projected[..., hid_units:]).astype(
             jnp.bfloat16
         )
-        blocks = jnp.arange(2 * experts, dtype=jnp.int32)
+        blocks = np.arange(2 * experts)
         chip_of = (blocks // 4) * 2 + (1 - (blocks // 2) % 2)
-        hidden = jnp.take(hidden, (blocks % 2) * chips + (chip_of ^ me), axis=0)
-
-        bwd_table = slot_table(bwd_ids, experts, capacity).astype(jnp.bfloat16)
-        bwd_table = jnp.take(bwd_table, peer, axis=0)
-        grad_in = jnp.einsum(
-            "ect,ecd->td", bwd_table, jnp.stack(returned), preferred_element_type=jnp.float32
-        ).astype(jnp.bfloat16)
-        grad_rows = lax.ppermute(grad_in, RING, ring_route(sections, -1))
+        hidden = hidden[(blocks % 2) * chips + chip_of]
         return (hidden[None, None], grad_rows[None])
 
     return shards

time: 363 us -> 267 us (0.74)
  waiting for transfers between devices: 233 us -> 110 us
  blocking collectives: 0 us -> 67.7 us
  local copies, waits for them, and re-layouts: 33.8 us -> 13.4 us
  starting transfers between devices: 25.8 us -> 9.81 us
  other arithmetic: 15.2 us -> 11.4 us
    ppermute x14 -> x0, waiting for transfers between devices: 159 us -> none  [the longest x7 128 us: shards(): lax.ppermute(picked[k], CHIPS, chip_route(chips, k))]
    all_to_all x0 -> x1, blocking collectives: none -> 67.7 us  [shards(): lax.all_to_all(picked, CHIPS, split_axis=0, concat_axis=0, tiled=True)]
    ppermute x1, waiting for transfers between devices: 1.85 us -> 58.5 us  [swap_ylo(): return lax.ppermute(block, 'ylo', [(0, 1), (1, 0)])]
    ppermute x1, waiting for transfers between devices: 28.6 us -> 0.01 us  [shards(): rows = lax.ppermute(prev_out[0], RING, ring_route(sections, 1))]
    ppermute x14 -> x0, starting transfers between devices: 21.8 us -> none  [the longest x7 12.9 us: shards(): lax.ppermute(pair_sum[k], CHIPS, chip_route(chips, k))]
    unnamed x23 -> x19, local copies, waits for them, and re-layouts: 15.3 us -> 4.99 us
    ppermute x1, waiting for transfers between devices: 0.25 us -> 9.15 us  [shards(): other_part = lax.ppermute(partial_rows[1], 'core', [(0, 1), (1, 0)])]
    all_to_all x0 -> x1, starting transfers between devices: none -> 6.9 us  [shards(): lax.all_to_all(pair_sum, CHIPS, split_axis=0, concat_axis=0, tiled=True)]
  transfers between devices with their start and end apart: 19 -> 6, of which waited for: 13 -> 3; matrix products, arithmetic and copies ran while one was open for 9% -> 2% of each run, Pallas kernels for 0% -> 0%
where the time goes in v3:
time: 267 us
  waiting for transfers between devices  110 us (41%)
  blocking collectives  67.7 us (25%)
  matrix products  40.8 us (15%)
  between operations  14.2 us (5%)
  local copies, waits for them, and re-layouts  13.4 us (5%)
  other arithmetic  11.4 us (4%)
  starting transfers between devices  9.81 us (4%)
    all_to_all x1, blocking collectives, shards(): lax.all_to_all(picked, CHIPS, split_axis=0, concat_axis=0, tiled=True)  67.7 us
    ppermute x1, waiting for transfers between devices, swap_ylo(): return lax.ppermute(block, 'ylo', [(0, 1), (1, 0)])  58.5 us
    ppermute x1, waiting for transfers between devices, shards(): grad_rows = lax.ppermute(grad_in, RING, ring_route(sections, -1))  41.8 us
    dot_general x1, matrix products, shards(): jnp.einsum('kech,dh->kecd', grad_pre, weights, preferred_element_type=jnp...  19.1 us
    dot_general x1, matrix products, shards(): jnp.einsum('scd,dh->sch', both.reshape(2 * experts, capacity, model_width...  16.5 us
    ppermute x1, waiting for transfers between devices, shards(): other_part = lax.ppermute(partial_rows[1], 'core', [(0, 1), (1, 0)])  9.15 us
    convert_element_type x1, other arithmetic, shards(): (partial_rows[0].astype(jnp.float32) + other_part.astype(jnp.float32)).as...  7.14 us
    all_to_all x1, starting transfers between devices, shards(): lax.all_to_all(pair_sum, CHIPS, split_axis=0, concat_axis=0, tiled=True)  6.9 us
  transfers between devices with their start and end apart: 6, of which 3 were waited for; matrix products, arithmetic and copies ran while one was open for 2% of the time, Pallas kernels for 0%

profile of v3, /device:TPU:30, one launch (start us, length us, event | category | flops | bytes accessed | tf_op | source)
XLA Modules:
  0.0 266.9 jit_solution(11440481613336915343)
XLA Ops:
  7.3 1.3 copy-done
  8.6 0.6 gather_fusion.1
  9.2 1.7 gather_fusion
  11.1 0.3 select_convert_fusion
  11.3 0.9 fusion.12
  12.3 19.1 %fusion.4 = bf16[2,8,48,7168]{3,2,1,0:T(8,128)(2,1)} fusion(bf16[1,1,7168,1024]{3,2,1,0:T(8,128)(2,1)} %param.10, bf16[2,8,48,512]{3,2,1,0:T(8,128)(2,1)S(1)} %bitcast.67, bf16[2,8,48,512]{3,2,1,0:T(8,128)(2,1)S(1)} %bitcast.66), kind=kOutput, calls=%fused_computation.7 | convolution fusion | flops 11282939904 | bytes 27262976 | tf_op jit(solution)/shard_map/kech,dh->kecd/dot_general | solution.py:79
  31.3 3.1 %slice_bitcast_fusion = bf16[8,48,7168]{2,1,0:T(8,128)(2,1)S(1)} fusion(bf16[2,8,48,7168]{3,2,1,0:T(8,128)(2,1)} %fusion.4), kind=kLoop, calls=%fused_computation.13 | loop fusion | bytes 11010048 | tf_op jit(solution)/shard_map/squeeze | solution.py:82
  34.5 9.2 %collective-permute-done.2 = bf16[8,48,7168]{2,1,0:T(8,128)(2,1)} collective-permute-done((bf16[8,48,7168]{2,1,0:T(8,128)(2,1)S(1)}, bf16[8,48,7168]{2,1,0:T(8,128)(2,1)}, u32[]{:S(2)}, u32[]{:S(2)}) %collective-permute-start.2) | collective-permute-done | bytes 5505056 | tf_op jit(solution)/shard_map/ppermute | solution.py:82
  43.7 7.1 %fusion.7 = bf16[8,48,7168]{2,1,0:T(8,128)(2,1)} fusion(bf16[8,48,7168]{2,1,0:T(8,128)(2,1)} %collective-permute-done.2, bf16[2,8,48,7168]{3,2,1,0:T(8,128)(2,1)S(1)} %copy-done.2), kind=kLoop, calls=%fused_computation.9 | loop fusion | flops 11010048 | bytes 16515072 | tf_op jit(solution)/shard_map/convert_element_type | solution.py:83
  50.8 6.9 %all-to-all-start = ((bf16[8,48,7168]{2,1,0:T(8,128)(2,1)}), bf16[8,48,7168]{2,1,0:T(8,128)(2,1)}, u32[]{:S(2)}, u32[]{:S(2)}) async-start(bf16[8,48,7168]{2,1,0:T(8,128)(2,1)} %fusion.7), calls=%async_computation | async-start | bytes 11010048 | tf_op jit(solution)/shard_map/all_to_all | solution.py:86
  57.9 1.7 collective-permute-start.1
  59.5 58.5 %collective-permute-done = s32[128,4]{0,1:T(4,128)S(1)} collective-permute-done((s32[128,4]{0,1:T(4,128)S(1)}, s32[128,4]{0,1:T(4,128)S(1)}, u32[]{:S(2)}, u32[]{:S(2)}) %collective-permute-start) | collective-permute-done | bytes 2080 | tf_op jit(solution)/shard_map/ppermute | solution.py:23
  118.6 0.1 eq.93
  118.9 0.6 reduce-window.14
  119.5 0.2 slice_reduce_fusion.1
  120.1 0.3 bitcast_reduce_fusion.1
  120.4 0.2 copy.37
  120.6 0.6 reduce-window.16
  121.2 0.2 slice_reduce_fusion
  121.8 0.3 bitcast_reduce_fusion
  122.2 0.2 copy.38
  122.4 1.6 convolution_convert_fusion
  124.0 3.7 %fusion.8 = bf16[128,7168]{1,0:T(8,128)(2,1)S(1)} fusion(bf16[8,48,7168]{2,1,0:T(8,128)(2,1)} %all-to-all-done, bf16[128,8,48]{0,2,1:T(8,128)(2,1)S(1)} %copy.38), kind=kOutput, calls=%fused_computation.12 | convolution fusion | flops 705560576 | bytes 7438336 | tf_op jit(solution)/shard_map/ect,ecd->td/dot_general | solution.py:94
  127.7 67.7 %all_to_all.10 = bf16[8,48,7168]{2,1,0:T(8,128)(2,1)} all-to-all(bf16[8,48,7168]{2,1,0:T(8,128)(2,1)S(1)} %convolution_convert_fusion), channel_id=1, replica_groups=mesh['x'=4,'yhi'=2,'z'=4,'ylo'=2,'core'=2] {'z','ylo'}, dimensions={0} | all-to-all | bytes 11010048 | tf_op jit(solution)/shard_map/all_to_all | solution.py:100
  195.4 1.0 collective-permute-start.3
  196.4 41.8 %collective-permute-done.3 = bf16[128,7168]{1,0:T(8,128)(2,1)S(1)} collective-permute-done((bf16[128,7168]{1,0:T(8,128)(2,1)S(1)}, bf16[128,7168]{1,0:T(8,128)(2,1)S(1)}, u32[]{:S(2)}, u32[]{:S(2)}) %collective-permute-start.3) | collective-permute-done | bytes 1835040 | tf_op jit(solution)/shard_map/ppermute | solution.py:98
  238.2 1.2 copy-done.3
  239.5 16.5 %fusion = f32[16,48,1024]{2,1,0:T(8,128)S(1)} fusion(bf16[16,48,7168]{2,1,0:T(8,128)(2,1)} %all-gather.3.cloned.1.call-done, bf16[1,1,7168,1024]{3,2,1,0:T(8,128)(2,1)} %param.10), kind=kOutput, calls=%fused_computation.3 | convolution fusion | flops 11274289152 | bytes 28835840 | tf_op jit(solution)/shard_map/scd,dh->sch/dot_general | solution.py:103
  255.9 0.5 fusion.15
  256.5 1.5 gather_fusion.2
  257.9 1.2 copy.40
  259.2 0.8 copy-done.1
  (47 shorter events, 1.9 us)
Async XLA Ops:
  7.2 1.4 copy-start
  31.3 12.3 %copy-start.2 = (bf16[2,8,48,7168]{3,2,1,0:T(8,128)(2,1)S(1)}, bf16[2,8,48,7168]{3,2,1,0:T(8,128)(2,1)}, u32[]{:S(2)}) copy-start(bf16[2,8,48,7168]{3,2,1,0:T(8,128)(2,1)} %fusion.4) | copy-start | bytes 33030148
  34.4 9.2 %collective-permute-start.2 = (bf16[8,48,7168]{2,1,0:T(8,128)(2,1)S(1)}, bf16[8,48,7168]{2,1,0:T(8,128)(2,1)}, u32[]{:S(2)}, u32[]{:S(2)}) collective-permute-start(bf16[8,48,7168]{2,1,0:T(8,128)(2,1)S(1)} %slice_bitcast_fusion), channel_id=1, source_target_pairs={{0,1},{1,0},{2,3},{3,2},{4,5},{5,4},{6,7},{7,6},{8,9},{9,8},{10,11... | collective-permute-start | bytes 16515080 | tf_op jit(solution)/shard_map/ppermute | solution.py:82
  50.8 6.9 %copy-start.5 = (s32[1,128,2]{1,2,0:T(2,128)S(1)}, s32[1,128,2]{1,2,0:T(2,128)}, u32[]{:S(2)}) copy-start(s32[1,128,2]{1,2,0:T(2,128)} %param.11) | copy-start | bytes 3076
  50.8 6.9 %copy-start.6 = (s32[1,128,2]{1,2,0:T(2,128)S(1)}, s32[1,128,2]{1,2,0:T(2,128)}, u32[]{:S(2)}) copy-start(s32[1,128,2]{1,2,0:T(2,128)} %param.9) | copy-start | bytes 3076
  50.8 71.6 %all-to-all-start = ((bf16[8,48,7168]{2,1,0:T(8,128)(2,1)}), bf16[8,48,7168]{2,1,0:T(8,128)(2,1)}, u32[]{:S(2)}, u32[]{:S(2)}) async-start(bf16[8,48,7168]{2,1,0:T(8,128)(2,1)} %fusion.7), calls=%async_computation | async-start | bytes 11010048 | tf_op jit(solution)/shard_map/all_to_all | solution.py:86
  57.7 181.8 %all-gather.3.cloned.1.call-start = ((), (), s32[]{:S(2)}) async-start(), calls=%async_computation.2 | async-start | bytes 16515072 | tf_op jit(solution)/shard_map/all_gather | solution.py:102
  57.7 60.3 %collective-permute-start = (s32[128,4]{0,1:T(4,128)S(1)}, s32[128,4]{0,1:T(4,128)S(1)}, u32[]{:S(2)}, u32[]{:S(2)}) collective-permute-start(s32[128,4]{0,1:T(4,128)S(1)} %pad_add_fusion), channel_id=1, source_target_pairs={{0,2},{2,0},{1,3},{3,1},{4,6},{6,4},{5,7},{7,5},{8,10},{10,8},{9,1... | collective-permute-start | bytes 6152 | tf_op jit(solution)/shard_map/ppermute | solution.py:23
  57.9 64.5 %collective-permute-start.1 = (bf16[128,7168]{1,0:T(8,128)(2,1)}, bf16[128,7168]{1,0:T(8,128)(2,1)S(1)}, u32[]{:S(2)}, u32[]{:S(2)}) collective-permute-start(bf16[128,7168]{1,0:T(8,128)(2,1)} %bitcast.70), channel_id=1, source_target_pairs={{0,18},{2,16},{16,34},{18,32},{32,50},{34,48},{48,66},{50,64},{64,... | collective-permute-start | bytes 5505032 | tf_op jit(solution)/shard_map/ppermute | solution.py:73
  195.3 1.0 copy-start.7
  195.4 42.9 %collective-permute-start.3 = (bf16[128,7168]{1,0:T(8,128)(2,1)S(1)}, bf16[128,7168]{1,0:T(8,128)(2,1)S(1)}, u32[]{:S(2)}, u32[]{:S(2)}) collective-permute-start(bf16[128,7168]{1,0:T(8,128)(2,1)S(1)} %fusion.8), channel_id=1, source_target_pairs={{0,114},{2,112},{16,2},{18,0},{32,18},{34,16},{48,34},{50,32},{64,... | collective-permute-start | bytes 5505032 | tf_op jit(solution)/shard_map/ppermute | solution.py:98
  238.2 1.2 copy-start.3
  255.9 2.0 copy-start.4
  257.9 2.1 copy-start.1
Sparse Core Ops, SparseCore 0:
  195.5 25.6 all-gather.2

commit v4 on v3

--- a/solution.py
+++ b/solution.py
@@ -76,11 +76,14 @@
         upstream = jnp.take(grad_hidden[0, 0], order, axis=0)
         saved = jnp.take(saved_pre[0, 0], order, axis=0)
         grad_pre = swiglu_backward(upstream, saved).reshape(2, chips, capacity, 2 * hid_units)
-        partial_rows = jnp.einsum(
-            "kech,dh->kecd", grad_pre, weights, preferred_element_type=jnp.float32
+        send_part = jnp.einsum(
+            "ech,dh->ecd", grad_pre[1], weights, preferred_element_type=jnp.float32
         ).astype(jnp.bfloat16)
-        other_part = lax.ppermute(partial_rows[1], "core", [(0, 1), (1, 0)])
-        pair_sum = (partial_rows[0].astype(jnp.float32) + other_part.astype(jnp.float32)).astype(
+        other_part = lax.ppermute(send_part, "core", [(0, 1), (1, 0)])
+        keep_part = jnp.einsum(
+            "ech,dh->ecd", grad_pre[0], weights, preferred_element_type=jnp.float32
+        ).astype(jnp.bfloat16)
+        pair_sum = (keep_part.astype(jnp.float32) + other_part.astype(jnp.float32)).astype(
             jnp.bfloat16
         )
         returned = lax.all_to_all(pair_sum, CHIPS, split_axis=0, concat_axis=0, tiled=True)
@@ -99,12 +102,15 @@
 
         arrived = lax.all_to_all(picked, CHIPS, split_axis=0, concat_axis=0, tiled=True)
 
-        both = lax.all_gather(arrived, "core", axis=0, tiled=False)
-        projected = jnp.einsum(
-            "scd,dh->sch",
-            both.reshape(2 * experts, capacity, model_width),
-            weights,
-            preferred_element_type=jnp.float32,
+        partner = lax.ppermute(arrived, "core", [(0, 1), (1, 0)])
+        own_proj = jnp.einsum("scd,dh->sch", arrived, weights, preferred_element_type=jnp.float32)
+        partner_proj = jnp.einsum(
+            "scd,dh->sch", partner, weights, preferred_element_type=jnp.float32
+        )
+        projected = jnp.where(
+            core == 0,
+            jnp.concatenate([own_proj, partner_proj]),
+            jnp.concatenate([partner_proj, own_proj]),
         )
         hidden = (jax.nn.silu(projected[..., :hid_units]) * projected[..., hid_units:]).astype(
             jnp.bfloat16

time: 267 us -> 269 us (level)
  matrix products: 40.8 us -> 63.6 us
  between operations: 14.2 us -> 0.88 us
  other arithmetic: 11.4 us -> 4.63 us
  local copies, waits for them, and re-layouts: 13.4 us -> 9.88 us
    dot_general x2 -> x4, matrix products: 35.5 us -> 58.3 us  [the longest x1 20.1 us: shards(): jnp.einsum('ech,dh->ecd', grad_pre[1], weights, preferred_element_type=jn...]
    convert_element_type x1 -> x0, other arithmetic: 7.14 us -> none  [shards(): (partial_rows[0].astype(jnp.float32) + other_part.astype(jnp.float32)).as...]
    squeeze x1 -> x0, local copies, waits for them, and re-layouts: 3.07 us -> none  [shards(): other_part = lax.ppermute(partial_rows[1], 'core', [(0, 1), (1, 0)])]
    ppermute x1, waiting for transfers between devices: 41.8 us -> 44.9 us  [shards(): grad_rows = lax.ppermute(grad_in, RING, ring_route(sections, -1))]
    ppermute x1 -> x2, waiting for transfers between devices: 9.15 us -> 9.02 us  [the longest x1 9.02 us: shards(): other_part = lax.ppermute(send_part, 'core', [(0, 1), (1, 0)])]
  transfers between devices with their start and end apart: 6 -> 6, of which waited for: 3 -> 3; matrix products, arithmetic and copies ran while one was open for 2% -> 6% of each run, Pallas kernels for 0% -> 0%
where the time goes in v4:
time: 269 us
  waiting for transfers between devices  112 us (42%)
  blocking collectives  67.7 us (25%)
  matrix products  63.6 us (24%)
  local copies, waits for them, and re-layouts  9.88 us (4%)
  starting transfers between devices  9.72 us (4%)
  other arithmetic  4.63 us (2%)
    all_to_all x1, blocking collectives, shards(): lax.all_to_all(picked, CHIPS, split_axis=0, concat_axis=0, tiled=True)  67.7 us
    ppermute x1, waiting for transfers between devices, swap_ylo(): return lax.ppermute(block, 'ylo', [(0, 1), (1, 0)])  58.5 us
    ppermute x1, waiting for transfers between devices, shards(): grad_rows = lax.ppermute(grad_in, RING, ring_route(sections, -1))  44.9 us
    dot_general x1, matrix products, shards(): jnp.einsum('ech,dh->ecd', grad_pre[1], weights, preferred_element_type=jn...  20.1 us
    dot_general x1, matrix products, shards(): jnp.einsum('ech,dh->ecd', grad_pre[0], weights, preferred_element_type=jn...  16.8 us
    dot_general x1, matrix products, shards(): jnp.einsum('scd,dh->sch', partner, weights, preferred_element_type=jnp.fl...  10.7 us
    dot_general x1, matrix products, shards(): jnp.einsum('scd,dh->sch', arrived, weights, preferred_element_type=jnp.fl...  10.7 us
    ppermute x1, waiting for transfers between devices, shards(): other_part = lax.ppermute(send_part, 'core', [(0, 1), (1, 0)])  9.02 us
  transfers between devices with their start and end apart: 6, of which 3 were waited for; matrix products, arithmetic and copies ran while one was open for 6% of the time, Pallas kernels for 0%

profile of v4, /device:TPU:30, one launch (start us, length us, event | category | flops | bytes accessed | tf_op | source)
XLA Modules:
  0.0 268.8 jit_solution(10422202080768646635)
XLA Ops:
  0.8 1.3 copy-done
  2.0 0.6 gather_fusion.1
  2.7 1.7 gather_fusion
  4.5 0.3 select_convert_fusion
  4.8 0.9 fusion.20
  5.7 20.1 %fusion.11 = bf16[8,48,7168]{2,1,0:T(8,128)(2,1)S(1)} fusion(bf16[1,1,7168,1024]{3,2,1,0:T(8,128)(2,1)} %param.10, bf16[16,48,512]{2,1,0:T(8,128)(2,1)S(1)} %get-tuple-element.11, bf16[16,48,512]{2,1,0:T(8,128)(2,1)S(1)} %get-tuple-element.10), kind=kOutput, calls=%fused_computation.13 | convolution fusion | flops 5643042816 | bytes 21757952 | tf_op jit(solution)/shard_map/ech,dh->ecd/dot_general | solution.py:79
  25.9 9.0 %collective-permute-done.2 = bf16[8,48,7168]{2,1,0:T(8,128)(2,1)S(1)} collective-permute-done((bf16[8,48,7168]{2,1,0:T(8,128)(2,1)S(1)}, bf16[8,48,7168]{2,1,0:T(8,128)(2,1)S(1)}, u32[]{:S(2)}, u32[]{:S(2)}) %collective-permute-start.2) | collective-permute-done | bytes 5505056 | tf_op jit(solution)/shard_map/ppermute | solution.py:82
  34.9 16.8 %add_convert_fusion = bf16[8,48,7168]{2,1,0:T(8,128)(2,1)} fusion(bf16[8,48,7168]{2,1,0:T(8,128)(2,1)S(1)} %collective-permute-done.2, bf16[1,1,7168,1024]{3,2,1,0:T(8,128)(2,1)} %param.10, bf16[16,48,512]{2,1,0:T(8,128)(2,1)S(1)} %get-tuple-element.11, bf16[16,48,512]{2,1,0:T(8,128)(2,1)S(1)} %get-tuple-element.10), kind=kOutput, calls=%fused_computation.11 | convolution fusion | flops 5654052864 | bytes 27262976 | tf_op jit(solution)/shard_map/ech,dh->ecd/dot_general | solution.py:83
  51.7 6.9 %all-to-all-start = ((bf16[8,48,7168]{2,1,0:T(8,128)(2,1)}), bf16[8,48,7168]{2,1,0:T(8,128)(2,1)}, u32[]{:S(2)}, u32[]{:S(2)}) async-start(bf16[8,48,7168]{2,1,0:T(8,128)(2,1)} %add_convert_fusion), calls=%async_computation | async-start | bytes 11010048 | tf_op jit(solution)/shard_map/all_to_all | solution.py:89
  58.8 1.7 collective-permute-start.1
  60.5 58.5 %collective-permute-done = s32[128,4]{0,1:T(4,128)S(1)} collective-permute-done((s32[128,4]{0,1:T(4,128)S(1)}, s32[128,4]{0,1:T(4,128)S(1)}, u32[]{:S(2)}, u32[]{:S(2)}) %collective-permute-start) | collective-permute-done | bytes 2080 | tf_op jit(solution)/shard_map/ppermute | solution.py:23
  119.3 0.1 eq.82
  119.5 0.1 eq.97
  119.8 0.6 reduce-window.14
  120.4 0.2 slice_reduce_fusion.1
  121.0 0.3 bitcast_reduce_fusion.1
  121.3 0.2 copy.30
  121.6 0.6 reduce-window.16
  122.1 0.2 slice_reduce_fusion
  122.7 0.3 bitcast_reduce_fusion
  123.1 0.2 copy.31
  123.3 1.6 convolution_convert_fusion
  124.9 3.7 %fusion.16 = bf16[128,7168]{1,0:T(8,128)(2,1)S(1)} fusion(bf16[8,48,7168]{2,1,0:T(8,128)(2,1)} %all-to-all-done, bf16[128,8,48]{0,2,1:T(8,128)(2,1)S(1)} %copy.31), kind=kOutput, calls=%fused_computation.16 | convolution fusion | flops 705560576 | bytes 7438336 | tf_op jit(solution)/shard_map/ect,ecd->td/dot_general | solution.py:97
  128.6 67.7 %all_to_all.10 = bf16[8,48,7168]{2,1,0:T(8,128)(2,1)} all-to-all(bf16[8,48,7168]{2,1,0:T(8,128)(2,1)S(1)} %convolution_convert_fusion), channel_id=1, replica_groups=mesh['x'=4,'yhi'=2,'z'=4,'ylo'=2,'core'=2] {'z','ylo'}, dimensions={0} | all-to-all | bytes 11010048 | tf_op jit(solution)/shard_map/all_to_all | solution.py:103
  196.3 0.9 collective-permute-start.4
  197.2 44.9 %collective-permute-done.4 = bf16[128,7168]{1,0:T(8,128)(2,1)} collective-permute-done((bf16[128,7168]{1,0:T(8,128)(2,1)S(1)}, bf16[128,7168]{1,0:T(8,128)(2,1)}, u32[]{:S(2)}, u32[]{:S(2)}) %collective-permute-start.4) | collective-permute-done | bytes 1835040 | tf_op jit(solution)/shard_map/ppermute | solution.py:101
  242.1 10.7 %fusion.2 = f32[8,48,1024]{2,1,0:T(8,128)S(1)} fusion(bf16[8,48,7168]{2,1,0:T(8,128)(2,1)} %all_to_all.10, bf16[1,1,7168,1024]{3,2,1,0:T(8,128)(2,1)} %param.10), kind=kOutput, calls=%fused_computation.5 | convolution fusion | flops 5637144576 | bytes 21757952 | tf_op jit(solution)/shard_map/scd,dh->sch/dot_general | solution.py:106
  252.8 10.7 %fusion = f32[8,48,1024]{2,1,0:T(8,128)S(1)} fusion(bf16[8,48,7168]{2,1,0:T(8,128)(2,1)} %collective-permute-done.3, bf16[1,1,7168,1024]{3,2,1,0:T(8,128)(2,1)} %param.10), kind=kOutput, calls=%fused_computation.3 | convolution fusion | flops 5637144576 | bytes 21757952 | tf_op jit(solution)/shard_map/scd,dh->sch/dot_general | solution.py:107
  263.5 0.4 maximum_select_fusion
  264.0 0.5 fusion.23
  264.5 1.5 gather_fusion.2
  266.0 2.8 %copy.33 = bf16[1,128,7168]{2,1,0:T(8,128)(2,1)} copy(bf16[1,128,7168]{2,1,0:T(8,128)(2,1)} %bitcast.22) | data formatting | bytes 3670016
  (41 shorter events, 1.7 us)
Async XLA Ops:
  0.6 1.4 copy-start
  25.8 9.1 %collective-permute-start.2 = (bf16[8,48,7168]{2,1,0:T(8,128)(2,1)S(1)}, bf16[8,48,7168]{2,1,0:T(8,128)(2,1)S(1)}, u32[]{:S(2)}, u32[]{:S(2)}) collective-permute-start(bf16[8,48,7168]{2,1,0:T(8,128)(2,1)S(1)} %fusion.11), channel_id=1, source_target_pairs={{0,1},{1,0},{2,3},{3,2},{4,5},{5,4},{6,7},{7,6},{8,9},{9,8},{10,11... | collective-permute-start | bytes 16515080 | tf_op jit(solution)/shard_map/ppermute | solution.py:82
  51.7 6.9 %copy-start.2 = (s32[1,128,2]{1,2,0:T(2,128)S(1)}, s32[1,128,2]{1,2,0:T(2,128)}, u32[]{:S(2)}) copy-start(s32[1,128,2]{1,2,0:T(2,128)} %param.11) | copy-start | bytes 3076
  51.7 6.9 %copy-start.3 = (s32[1,128,2]{1,2,0:T(2,128)S(1)}, s32[1,128,2]{1,2,0:T(2,128)}, u32[]{:S(2)}) copy-start(s32[1,128,2]{1,2,0:T(2,128)} %param.9) | copy-start | bytes 3076
  51.7 71.6 %all-to-all-start = ((bf16[8,48,7168]{2,1,0:T(8,128)(2,1)}), bf16[8,48,7168]{2,1,0:T(8,128)(2,1)}, u32[]{:S(2)}, u32[]{:S(2)}) async-start(bf16[8,48,7168]{2,1,0:T(8,128)(2,1)} %add_convert_fusion), calls=%async_computation | async-start | bytes 11010048 | tf_op jit(solution)/shard_map/all_to_all | solution.py:89
  58.7 60.3 %collective-permute-start = (s32[128,4]{0,1:T(4,128)S(1)}, s32[128,4]{0,1:T(4,128)S(1)}, u32[]{:S(2)}, u32[]{:S(2)}) collective-permute-start(s32[128,4]{0,1:T(4,128)S(1)} %pad_add_fusion), channel_id=1, source_target_pairs={{0,2},{2,0},{1,3},{3,1},{4,6},{6,4},{5,7},{7,5},{8,10},{10,8},{9,1... | collective-permute-start | bytes 6152 | tf_op jit(solution)/shard_map/ppermute | solution.py:23
  58.8 64.5 %collective-permute-start.1 = (bf16[128,7168]{1,0:T(8,128)(2,1)}, bf16[128,7168]{1,0:T(8,128)(2,1)S(1)}, u32[]{:S(2)}, u32[]{:S(2)}) collective-permute-start(bf16[128,7168]{1,0:T(8,128)(2,1)} %bitcast.63), channel_id=1, source_target_pairs={{0,18},{2,16},{16,34},{18,32},{32,50},{34,48},{48,66},{50,64},{64,... | collective-permute-start | bytes 5505032 | tf_op jit(solution)/shard_map/ppermute | solution.py:73
  128.6 68.6 %copy-start.4 = (s32[16]{0:T(128)S(1)}, s32[16]{0:T(128)}, u32[]{:S(2)}) copy-start(s32[16]{0:T(128)} %constant.91) | copy-start | bytes 196
  196.3 56.5 %collective-permute-start.3 = (bf16[8,48,7168]{2,1,0:T(8,128)(2,1)}, bf16[8,48,7168]{2,1,0:T(8,128)(2,1)}, u32[]{:S(2)}, u32[]{:S(2)}) collective-permute-start(bf16[8,48,7168]{2,1,0:T(8,128)(2,1)} %all_to_all.10), channel_id=1, source_target_pairs={{0,1},{1,0},{2,3},{3,2},{4,5},{5,4},{6,7},{7,6},{8,9},{9,8},{10,11... | collective-permute-start | bytes 16515080 | tf_op jit(solution)/shard_map/ppermute | solution.py:105
  196.3 45.9 %collective-permute-start.4 = (bf16[128,7168]{1,0:T(8,128)(2,1)S(1)}, bf16[128,7168]{1,0:T(8,128)(2,1)}, u32[]{:S(2)}, u32[]{:S(2)}) collective-permute-start(bf16[128,7168]{1,0:T(8,128)(2,1)S(1)} %fusion.16), channel_id=1, source_target_pairs={{0,114},{2,112},{16,2},{18,0},{32,18},{34,16},{48,34},{50,32},{64,... | collective-permute-start | bytes 5505032 | tf_op jit(solution)/shard_map/ppermute | solution.py:101
  264.0 4.8 %copy-start.1 = (bf16[1,1,16,48,1024]{4,3,2,1,0:T(8,128)(2,1)S(1)}, bf16[1,1,16,48,1024]{4,3,2,1,0:T(8,128)(2,1)}, u32[]{:S(2)}) copy-start(bf16[1,1,16,48,1024]{4,3,2,1,0:T(8,128)(2,1)} %param.13) | copy-start | bytes 4718596

commit v5 on v3

--- a/solution.py
+++ b/solution.py
@@ -112,6 +112,7 @@
         blocks = np.arange(2 * experts)
         chip_of = (blocks // 4) * 2 + (1 - (blocks // 2) % 2)
         hidden = hidden[(blocks % 2) * chips + chip_of]
+        hidden, grad_rows = lax.optimization_barrier((hidden, grad_rows))
         return (hidden[None, None], grad_rows[None])
 
     return shards

time: 267 us -> 251 us (0.940)
  waiting for transfers between devices: 110 us -> 92 us
    ppermute x1, waiting for transfers between devices: 41.8 us -> 0.01 us  [shards(): grad_rows = lax.ppermute(grad_in, RING, ring_route(sections, -1))]
    all_gather x1, waiting for transfers between devices: 0.01 us -> 24.3 us  [shards(): both = lax.all_gather(arrived, 'core', axis=0, tiled=False)]
  transfers between devices with their start and end apart: 6 -> 6, of which waited for: 3 -> 3; matrix products, arithmetic and copies ran while one was open for 2% -> 9% of each run, Pallas kernels for 0% -> 0%
where the time goes in v5:
time: 251 us; the launch traced here: 250 us
  waiting for transfers between devices  92 us (37%)
  blocking collectives  67.7 us (27%)
  matrix products  40.8 us (16%)
  between operations  14.2 us (6%)
  local copies, waits for them, and re-layouts  13.7 us (5%)
  other arithmetic  11.4 us (5%)
  starting transfers between devices  9.74 us (4%)
    all_to_all x1, blocking collectives, shards(): lax.all_to_all(picked, CHIPS, split_axis=0, concat_axis=0, tiled=True)  67.7 us
    ppermute x1, waiting for transfers between devices, swap_ylo(): return lax.ppermute(block, 'ylo', [(0, 1), (1, 0)])  58.5 us
    all_gather x1, waiting for transfers between devices, shards(): both = lax.all_gather(arrived, 'core', axis=0, tiled=False)  24.3 us
    dot_general x1, matrix products, shards(): jnp.einsum('kech,dh->kecd', grad_pre, weights, preferred_element_type=jnp...  19.1 us
    dot_general x1, matrix products, shards(): jnp.einsum('scd,dh->sch', both.reshape(2 * experts, capacity, model_width...  16.5 us
    ppermute x1, waiting for transfers between devices, shards(): other_part = lax.ppermute(partial_rows[1], 'core', [(0, 1), (1, 0)])  9.15 us
    convert_element_type x1, other arithmetic, shards(): (partial_rows[0].astype(jnp.float32) + other_part.astype(jnp.float32)).as...  7.14 us
    all_to_all x1, starting transfers between devices, shards(): lax.all_to_all(pair_sum, CHIPS, split_axis=0, concat_axis=0, tiled=True)  6.9 us
  transfers between devices with their start and end apart: 6, of which 3 were waited for; matrix products, arithmetic and copies ran while one was open for 9% of the time, Pallas kernels for 0%

profile of v5, /device:TPU:30, one launch (start us, length us, event | category | flops | bytes accessed | tf_op | source)
XLA Modules:
  0.0 249.5 jit_solution(12662332092905498130)
XLA Ops:
  7.3 1.3 copy-done
  8.6 0.6 gather_fusion.1
  9.2 1.7 gather_fusion
  11.1 0.3 select_convert_fusion
  11.3 0.9 fusion.12
  12.3 19.1 %fusion.4 = bf16[2,8,48,7168]{3,2,1,0:T(8,128)(2,1)} fusion(bf16[1,1,7168,1024]{3,2,1,0:T(8,128)(2,1)} %param.10, bf16[2,8,48,512]{3,2,1,0:T(8,128)(2,1)S(1)} %bitcast.66, bf16[2,8,48,512]{3,2,1,0:T(8,128)(2,1)S(1)} %bitcast.65), kind=kOutput, calls=%fused_computation.7 | convolution fusion | flops 11282939904 | bytes 27262976 | tf_op jit(solution)/shard_map/kech,dh->kecd/dot_general | solution.py:79
  31.3 3.1 %slice_bitcast_fusion = bf16[8,48,7168]{2,1,0:T(8,128)(2,1)S(1)} fusion(bf16[2,8,48,7168]{3,2,1,0:T(8,128)(2,1)} %fusion.4), kind=kLoop, calls=%fused_computation.13 | loop fusion | bytes 11010048 | tf_op jit(solution)/shard_map/squeeze | solution.py:82
  34.5 9.2 %collective-permute-done.2 = bf16[8,48,7168]{2,1,0:T(8,128)(2,1)} collective-permute-done((bf16[8,48,7168]{2,1,0:T(8,128)(2,1)S(1)}, bf16[8,48,7168]{2,1,0:T(8,128)(2,1)}, u32[]{:S(2)}, u32[]{:S(2)}) %collective-permute-start.2) | collective-permute-done | bytes 5505056 | tf_op jit(solution)/shard_map/ppermute | solution.py:82
  43.7 7.1 %fusion.7 = bf16[8,48,7168]{2,1,0:T(8,128)(2,1)} fusion(bf16[8,48,7168]{2,1,0:T(8,128)(2,1)} %collective-permute-done.2, bf16[2,8,48,7168]{3,2,1,0:T(8,128)(2,1)S(1)} %copy-done.2), kind=kLoop, calls=%fused_computation.9 | loop fusion | flops 11010048 | bytes 16515072 | tf_op jit(solution)/shard_map/convert_element_type | solution.py:83
  50.8 6.9 %all-to-all-start = ((bf16[8,48,7168]{2,1,0:T(8,128)(2,1)}), bf16[8,48,7168]{2,1,0:T(8,128)(2,1)}, u32[]{:S(2)}, u32[]{:S(2)}) async-start(bf16[8,48,7168]{2,1,0:T(8,128)(2,1)} %fusion.7), calls=%async_computation | async-start | bytes 11010048 | tf_op jit(solution)/shard_map/all_to_all | solution.py:86
  57.9 1.7 collective-permute-start.1
  59.5 58.5 %collective-permute-done = s32[128,4]{0,1:T(4,128)S(1)} collective-permute-done((s32[128,4]{0,1:T(4,128)S(1)}, s32[128,4]{0,1:T(4,128)S(1)}, u32[]{:S(2)}, u32[]{:S(2)}) %collective-permute-start) | collective-permute-done | bytes 2080 | tf_op jit(solution)/shard_map/ppermute | solution.py:23
  118.3 0.1 eq.78
  118.6 0.1 eq.93
  118.9 0.6 reduce-window.14
  119.5 0.2 slice_reduce_fusion.1
  120.1 0.3 bitcast_reduce_fusion.1
  120.4 0.2 copy.37
  120.6 0.6 reduce-window.16
  121.2 0.2 slice_reduce_fusion
  121.8 0.3 bitcast_reduce_fusion
  122.2 0.2 copy.38
  122.4 1.6 convolution_convert_fusion
  124.0 3.7 %fusion.8 = bf16[128,7168]{1,0:T(8,128)(2,1)S(1)} fusion(bf16[8,48,7168]{2,1,0:T(8,128)(2,1)} %all-to-all-done, bf16[128,8,48]{0,2,1:T(8,128)(2,1)S(1)} %copy.38), kind=kOutput, calls=%fused_computation.12 | convolution fusion | flops 705560576 | bytes 7438336 | tf_op jit(solution)/shard_map/ect,ecd->td/dot_general | solution.py:94
  127.7 67.7 %all_to_all.10 = bf16[8,48,7168]{2,1,0:T(8,128)(2,1)} all-to-all(bf16[8,48,7168]{2,1,0:T(8,128)(2,1)S(1)} %convolution_convert_fusion), channel_id=1, replica_groups=mesh['x'=4,'yhi'=2,'z'=4,'ylo'=2,'core'=2] {'z','ylo'}, dimensions={0} | all-to-all | bytes 11010048 | tf_op jit(solution)/shard_map/all_to_all | solution.py:100
  195.4 0.6 copy-done.5
  196.0 0.9 collective-permute-start.3
  196.9 24.3 %all-gather.3.cloned.1.call-done = bf16[16,48,7168]{2,1,0:T(8,128)(2,1)} async-done(((bf16[8,48,7168]{2,1,0:T(8,128)(2,1)}), bf16[16,48,7168]{2,1,0:T(8,128)(2,1)}) %all-gather.3.cloned.1.call-update) | async-done | bytes 11010064 | tf_op jit(solution)/shard_map/all_gather | solution.py:102
  221.2 16.5 %fusion = f32[16,48,1024]{2,1,0:T(8,128)S(1)} fusion(bf16[16,48,7168]{2,1,0:T(8,128)(2,1)} %all-gather.3.cloned.1.call-done, bf16[1,1,7168,1024]{3,2,1,0:T(8,128)(2,1)} %param.10), kind=kOutput, calls=%fused_computation.3 | convolution fusion | flops 11274289152 | bytes 28835840 | tf_op jit(solution)/shard_map/scd,dh->sch/dot_general | solution.py:103
  237.7 0.5 fusion.15
  238.2 1.5 gather_fusion.2
  239.7 3.0 %copy.40 = bf16[1,128,7168]{2,1,0:T(8,128)(2,1)} copy(bf16[1,128,7168]{2,1,0:T(8,128)(2,1)} %bitcast.27) | data formatting | bytes 3670016
  (43 shorter events, 1.7 us)
Async XLA Ops:
  7.2 1.4 copy-start
  31.3 12.3 %copy-start.2 = (bf16[2,8,48,7168]{3,2,1,0:T(8,128)(2,1)S(1)}, bf16[2,8,48,7168]{3,2,1,0:T(8,128)(2,1)}, u32[]{:S(2)}) copy-start(bf16[2,8,48,7168]{3,2,1,0:T(8,128)(2,1)} %fusion.4) | copy-start | bytes 33030148
  34.4 9.2 %collective-permute-start.2 = (bf16[8,48,7168]{2,1,0:T(8,128)(2,1)S(1)}, bf16[8,48,7168]{2,1,0:T(8,128)(2,1)}, u32[]{:S(2)}, u32[]{:S(2)}) collective-permute-start(bf16[8,48,7168]{2,1,0:T(8,128)(2,1)S(1)} %slice_bitcast_fusion), channel_id=1, source_target_pairs={{0,1},{1,0},{2,3},{3,2},{4,5},{5,4},{6,7},{7,6},{8,9},{9,8},{10,11... | collective-permute-start | bytes 16515080 | tf_op jit(solution)/shard_map/ppermute | solution.py:82
  50.8 6.9 %copy-start.3 = (s32[1,128,2]{1,2,0:T(2,128)S(1)}, s32[1,128,2]{1,2,0:T(2,128)}, u32[]{:S(2)}) copy-start(s32[1,128,2]{1,2,0:T(2,128)} %param.11) | copy-start | bytes 3076
  50.8 6.9 %copy-start.4 = (s32[1,128,2]{1,2,0:T(2,128)S(1)}, s32[1,128,2]{1,2,0:T(2,128)}, u32[]{:S(2)}) copy-start(s32[1,128,2]{1,2,0:T(2,128)} %param.9) | copy-start | bytes 3076
  50.8 71.6 %all-to-all-start = ((bf16[8,48,7168]{2,1,0:T(8,128)(2,1)}), bf16[8,48,7168]{2,1,0:T(8,128)(2,1)}, u32[]{:S(2)}, u32[]{:S(2)}) async-start(bf16[8,48,7168]{2,1,0:T(8,128)(2,1)} %fusion.7), calls=%async_computation | async-start | bytes 11010048 | tf_op jit(solution)/shard_map/all_to_all | solution.py:86
  57.7 163.5 %all-gather.3.cloned.1.call-start = ((), (), s32[]{:S(2)}) async-start(), calls=%async_computation.2 | async-start | bytes 16515072 | tf_op jit(solution)/shard_map/all_gather | solution.py:102
  57.7 60.3 %collective-permute-start = (s32[128,4]{0,1:T(4,128)S(1)}, s32[128,4]{0,1:T(4,128)S(1)}, u32[]{:S(2)}, u32[]{:S(2)}) collective-permute-start(s32[128,4]{0,1:T(4,128)S(1)} %pad_add_fusion), channel_id=1, source_target_pairs={{0,2},{2,0},{1,3},{3,1},{4,6},{6,4},{5,7},{7,5},{8,10},{10,8},{9,1... | collective-permute-start | bytes 6152 | tf_op jit(solution)/shard_map/ppermute | solution.py:23
  57.9 64.5 %collective-permute-start.1 = (bf16[128,7168]{1,0:T(8,128)(2,1)}, bf16[128,7168]{1,0:T(8,128)(2,1)S(1)}, u32[]{:S(2)}, u32[]{:S(2)}) collective-permute-start(bf16[128,7168]{1,0:T(8,128)(2,1)} %bitcast.69), channel_id=1, source_target_pairs={{0,18},{2,16},{16,34},{18,32},{32,50},{34,48},{48,66},{50,64},{64,... | collective-permute-start | bytes 5505032 | tf_op jit(solution)/shard_map/ppermute | solution.py:73
  195.3 0.7 copy-start.5
  196.0 43.7 %collective-permute-start.3 = (bf16[128,7168]{1,0:T(8,128)(2,1)S(1)}, bf16[128,7168]{1,0:T(8,128)(2,1)}, u32[]{:S(2)}, u32[]{:S(2)}) collective-permute-start(bf16[128,7168]{1,0:T(8,128)(2,1)S(1)} %fusion.8), channel_id=1, source_target_pairs={{0,114},{2,112},{16,2},{18,0},{32,18},{34,16},{48,34},{50,32},{64,... | collective-permute-start | bytes 5505032 | tf_op jit(solution)/shard_map/ppermute | solution.py:98
  239.7 3.0 %copy-start.1 = (bf16[1,1,16,48,1024]{4,3,2,1,0:T(8,128)(2,1)S(1)}, bf16[1,1,16,48,1024]{4,3,2,1,0:T(8,128)(2,1)}, u32[]{:S(2)}) copy-start(bf16[1,1,16,48,1024]{4,3,2,1,0:T(8,128)(2,1)} %param.13) | copy-start | bytes 4718596
Sparse Core Ops, SparseCore 0:
  195.5 25.6 all-gather.2

commit v6 on v5

--- a/solution.py
+++ b/solution.py
@@ -72,17 +72,14 @@
 
         rows = lax.ppermute(prev_out[0], RING, ring_route(sections, 1))
 
-        order = jnp.concatenate([worked + core, worked + 1 - core])
+        order = jnp.concatenate([worked, worked + 1])
         upstream = jnp.take(grad_hidden[0, 0], order, axis=0)
         saved = jnp.take(saved_pre[0, 0], order, axis=0)
         grad_pre = swiglu_backward(upstream, saved).reshape(2, chips, capacity, 2 * hid_units)
         partial_rows = jnp.einsum(
             "kech,dh->kecd", grad_pre, weights, preferred_element_type=jnp.float32
         ).astype(jnp.bfloat16)
-        other_part = lax.ppermute(partial_rows[1], "core", [(0, 1), (1, 0)])
-        pair_sum = (partial_rows[0].astype(jnp.float32) + other_part.astype(jnp.float32)).astype(
-            jnp.bfloat16
-        )
+        pair_sum = lax.psum_scatter(partial_rows, "core", scatter_dimension=0, tiled=False)
         returned = lax.all_to_all(pair_sum, CHIPS, split_axis=0, concat_axis=0, tiled=True)
         rows, returned = lax.optimization_barrier((rows, returned))
 

time: 251 us -> 256 us (1.020)
  waiting for transfers between devices: 92 us -> 107 us
  other arithmetic: 11.4 us -> 4.23 us
  local copies, waits for them, and re-layouts: 13.7 us -> 10.6 us
    reduce_scatter x0 -> x1, waiting for transfers between devices: none -> 24.7 us  [shards(): lax.psum_scatter(partial_rows, 'core', scatter_dimension=0, tiled=False)]
    ppermute x1 -> x0, waiting for transfers between devices: 9.15 us -> none  [shards(): other_part = lax.ppermute(partial_rows[1], 'core', [(0, 1), (1, 0)])]
    convert_element_type x1 -> x0, other arithmetic: 7.14 us -> none  [shards(): (partial_rows[0].astype(jnp.float32) + other_part.astype(jnp.float32)).as...]
    squeeze x1 -> x0, local copies, waits for them, and re-layouts: 3.07 us -> none  [shards(): other_part = lax.ppermute(partial_rows[1], 'core', [(0, 1), (1, 0)])]
    unnamed x15 -> x13, local copies, waits for them, and re-layouts: 5.29 us -> 5.24 us
where the time goes in v6:
time: 256 us; the launch traced here: 254 us
  waiting for transfers between devices  107 us (42%)
  blocking collectives  67.8 us (26%)
  matrix products  40.8 us (16%)
  between operations  14.2 us (6%)
  local copies, waits for them, and re-layouts  10.6 us (4%)
  starting transfers between devices  9.21 us (4%)
  other arithmetic  4.23 us (2%)
    all_to_all x1, blocking collectives, shards(): lax.all_to_all(picked, CHIPS, split_axis=0, concat_axis=0, tiled=True)  67.8 us
    ppermute x1, waiting for transfers between devices, swap_ylo(): return lax.ppermute(block, 'ylo', [(0, 1), (1, 0)])  58.4 us
    reduce_scatter x1, waiting for transfers between devices, shards(): lax.psum_scatter(partial_rows, 'core', scatter_dimension=0, tiled=False)  24.7 us
    all_gather x1, waiting for transfers between devices, shards(): both = lax.all_gather(arrived, 'core', axis=0, tiled=False)  24.1 us
    dot_general x1, matrix products, shards(): jnp.einsum('kech,dh->kecd', grad_pre, weights, preferred_element_type=jnp...  19.1 us
    dot_general x1, matrix products, shards(): jnp.einsum('scd,dh->sch', both.reshape(2 * experts, capacity, model_width...  16.5 us
    all_to_all x1, starting transfers between devices, shards(): lax.all_to_all(pair_sum, CHIPS, split_axis=0, concat_axis=0, tiled=True)  6.03 us
    unnamed x13, local copies, waits for them, and re-layouts  5.24 us
  transfers between devices with their start and end apart: 6, of which 3 were waited for; matrix products, arithmetic and copies ran while one was open for 9% of the time, Pallas kernels for 0%

profile of v6, /device:TPU:30, one launch (start us, length us, event | category | flops | bytes accessed | tf_op | source)
XLA Modules:
  0.0 254.0 jit_solution(6870012571505838248)
XLA Ops:
  7.3 1.2 copy-done
  8.6 0.6 gather_fusion.1
  9.2 1.7 gather_fusion
  11.1 0.3 select_convert_fusion
  11.3 0.9 fusion.11
  12.3 19.1 %fusion.4 = bf16[2,8,48,7168]{3,2,1,0:T(8,128)(2,1)} fusion(bf16[1,1,7168,1024]{3,2,1,0:T(8,128)(2,1)} %param.10, bf16[2,8,48,512]{3,2,1,0:T(8,128)(2,1)S(1)} %bitcast.61, bf16[2,8,48,512]{3,2,1,0:T(8,128)(2,1)S(1)} %bitcast.60), kind=kOutput, calls=%fused_computation.7 | convolution fusion | flops 11282939904 | bytes 27262976 | tf_op jit(solution)/shard_map/kech,dh->kecd/dot_general | solution.py:79
  31.3 24.7 %reduce-scatter.2.cloned.1.call-done = bf16[1,8,48,7168]{3,2,1,0:T(8,128)(2,1)} async-done(((bf16[2,8,48,7168]{3,2,1,0:T(8,128)(2,1)}), bf16[1,8,48,7168]{3,2,1,0:T(8,128)(2,1)}) %reduce-scatter.2.cloned.1.call-update) | async-done | bytes 5505040 | tf_op jit(solution)/shard_map/reduce_scatter | solution.py:82
  56.0 6.0 %all-to-all-start = ((bf16[8,48,7168]{2,1,0:T(8,128)(2,1)}), bf16[8,48,7168]{2,1,0:T(8,128)(2,1)}, u32[]{:S(2)}, u32[]{:S(2)}) async-start(bf16[8,48,7168]{2,1,0:T(8,128)(2,1)} %bitcast.57), calls=%async_computation.1 | async-start | bytes 11010048 | tf_op jit(solution)/shard_map/all_to_all | solution.py:83
  62.2 1.9 collective-permute-start.1
  64.1 58.4 %collective-permute-done = s32[128,4]{0,1:T(4,128)S(1)} collective-permute-done((s32[128,4]{0,1:T(4,128)S(1)}, s32[128,4]{0,1:T(4,128)S(1)}, u32[]{:S(2)}, u32[]{:S(2)}) %collective-permute-start) | collective-permute-done | bytes 2080 | tf_op jit(solution)/shard_map/ppermute | solution.py:23
  122.6 0.1 eq.82
  122.8 0.1 eq.78
  123.0 0.1 eq.93
  123.1 0.1 eq.89
  123.3 0.6 reduce-window.14
  123.9 0.2 slice_reduce_fusion.1
  124.5 0.3 bitcast_reduce_fusion.1
  124.8 0.2 copy.37
  125.0 0.6 reduce-window.16
  125.6 0.2 slice_reduce_fusion
  126.2 0.3 bitcast_reduce_fusion
  126.6 0.2 copy.38
  126.8 1.6 convolution_convert_fusion
  128.4 3.7 %fusion.7 = bf16[128,7168]{1,0:T(8,128)(2,1)S(1)} fusion(bf16[8,48,7168]{2,1,0:T(8,128)(2,1)} %all-to-all-done, bf16[128,8,48]{0,2,1:T(8,128)(2,1)S(1)} %copy.38), kind=kOutput, calls=%fused_computation.10 | convolution fusion | flops 705560576 | bytes 7438336 | tf_op jit(solution)/shard_map/ect,ecd->td/dot_general | solution.py:91
  132.1 67.8 %all_to_all.10 = bf16[8,48,7168]{2,1,0:T(8,128)(2,1)} all-to-all(bf16[8,48,7168]{2,1,0:T(8,128)(2,1)S(1)} %convolution_convert_fusion), channel_id=1, replica_groups=mesh['x'=4,'yhi'=2,'z'=4,'ylo'=2,'core'=2] {'z','ylo'}, dimensions={0} | all-to-all | bytes 11010048 | tf_op jit(solution)/shard_map/all_to_all | solution.py:97
  199.9 0.6 copy-done.4
  200.5 1.1 collective-permute-start.2
  201.6 24.1 %all-gather.3.cloned.1.call-done = bf16[16,48,7168]{2,1,0:T(8,128)(2,1)} async-done(((bf16[8,48,7168]{2,1,0:T(8,128)(2,1)}), bf16[16,48,7168]{2,1,0:T(8,128)(2,1)}) %all-gather.3.cloned.1.call-update) | async-done | bytes 11010064 | tf_op jit(solution)/shard_map/all_gather | solution.py:99
  225.8 16.5 %fusion = f32[16,48,1024]{2,1,0:T(8,128)S(1)} fusion(bf16[16,48,7168]{2,1,0:T(8,128)(2,1)} %all-gather.3.cloned.1.call-done, bf16[1,1,7168,1024]{3,2,1,0:T(8,128)(2,1)} %param.10), kind=kOutput, calls=%fused_computation.3 | convolution fusion | flops 11274289152 | bytes 28835840 | tf_op jit(solution)/shard_map/scd,dh->sch/dot_general | solution.py:100
  242.2 0.5 fusion.14
  242.7 1.5 gather_fusion.2
  244.2 3.0 %copy.40 = bf16[1,128,7168]{2,1,0:T(8,128)(2,1)} copy(bf16[1,128,7168]{2,1,0:T(8,128)(2,1)} %bitcast.26) | data formatting | bytes 3670016
  (40 shorter events, 1.4 us)
Async XLA Ops:
  7.2 1.4 copy-start
  7.2 48.8 %reduce-scatter.2.cloned.1.call-start = ((), (), s32[]{:S(2)}) async-start(), calls=%async_computation.3 | async-start | bytes 16515072 | tf_op jit(solution)/shard_map/reduce_scatter | solution.py:82
  56.0 6.0 %copy-start.2 = (s32[1,128,2]{1,2,0:T(2,128)S(1)}, s32[1,128,2]{1,2,0:T(2,128)}, u32[]{:S(2)}) copy-start(s32[1,128,2]{1,2,0:T(2,128)} %param.11) | copy-start | bytes 3076
  56.0 6.0 %copy-start.3 = (s32[1,128,2]{1,2,0:T(2,128)S(1)}, s32[1,128,2]{1,2,0:T(2,128)}, u32[]{:S(2)}) copy-start(s32[1,128,2]{1,2,0:T(2,128)} %param.9) | copy-start | bytes 3076
  56.0 70.8 %all-to-all-start = ((bf16[8,48,7168]{2,1,0:T(8,128)(2,1)}), bf16[8,48,7168]{2,1,0:T(8,128)(2,1)}, u32[]{:S(2)}, u32[]{:S(2)}) async-start(bf16[8,48,7168]{2,1,0:T(8,128)(2,1)} %bitcast.57), calls=%async_computation.1 | async-start | bytes 11010048 | tf_op jit(solution)/shard_map/all_to_all | solution.py:83
  62.0 163.7 %all-gather.3.cloned.1.call-start = ((), (), s32[]{:S(2)}) async-start(), calls=%async_computation.4 | async-start | bytes 16515072 | tf_op jit(solution)/shard_map/all_gather | solution.py:99
  62.1 60.4 %collective-permute-start = (s32[128,4]{0,1:T(4,128)S(1)}, s32[128,4]{0,1:T(4,128)S(1)}, u32[]{:S(2)}, u32[]{:S(2)}) collective-permute-start(s32[128,4]{0,1:T(4,128)S(1)} %pad_add_fusion), channel_id=1, source_target_pairs={{0,2},{2,0},{1,3},{3,1},{4,6},{6,4},{5,7},{7,5},{8,10},{10,8},{9,1... | collective-permute-start | bytes 6152 | tf_op jit(solution)/shard_map/ppermute | solution.py:23
  62.2 64.6 %collective-permute-start.1 = (bf16[128,7168]{1,0:T(8,128)(2,1)}, bf16[128,7168]{1,0:T(8,128)(2,1)S(1)}, u32[]{:S(2)}, u32[]{:S(2)}) collective-permute-start(bf16[128,7168]{1,0:T(8,128)(2,1)} %bitcast.64), channel_id=1, source_target_pairs={{0,18},{2,16},{16,34},{18,32},{32,50},{34,48},{48,66},{50,64},{64,... | collective-permute-start | bytes 5505032 | tf_op jit(solution)/shard_map/ppermute | solution.py:73
  199.9 0.7 copy-start.4
  200.5 43.7 %collective-permute-start.2 = (bf16[128,7168]{1,0:T(8,128)(2,1)S(1)}, bf16[128,7168]{1,0:T(8,128)(2,1)}, u32[]{:S(2)}, u32[]{:S(2)}) collective-permute-start(bf16[128,7168]{1,0:T(8,128)(2,1)S(1)} %fusion.7), channel_id=1, source_target_pairs={{0,114},{2,112},{16,2},{18,0},{32,18},{34,16},{48,34},{50,32},{64,... | collective-permute-start | bytes 5505032 | tf_op jit(solution)/shard_map/ppermute | solution.py:95
  244.2 3.0 %copy-start.1 = (bf16[1,1,16,48,1024]{4,3,2,1,0:T(8,128)(2,1)S(1)}, bf16[1,1,16,48,1024]{4,3,2,1,0:T(8,128)(2,1)}, u32[]{:S(2)}) copy-start(bf16[1,1,16,48,1024]{4,3,2,1,0:T(8,128)(2,1)} %param.13) | copy-start | bytes 4718596
Sparse Core Ops, SparseCore 0:
  31.5 24.4 reduce-scatter.1
  200.0 25.6 all-gather.2

commit v7 on v5

--- a/solution.py
+++ b/solution.py
@@ -72,7 +72,13 @@
 
         rows = lax.ppermute(prev_out[0], RING, ring_route(sections, 1))
 
-        order = jnp.concatenate([worked + core, worked + 1 - core])
+        fwd_table = slot_table(fwd_ids, experts, capacity).astype(jnp.bfloat16)
+        picked = jnp.einsum(
+            "ect,td->ecd", fwd_table, rows, preferred_element_type=jnp.float32
+        ).astype(jnp.bfloat16)
+        arrived = lax.all_to_all(picked, CHIPS, split_axis=0, concat_axis=0, tiled=True)
+        picked, order_in = lax.optimization_barrier((picked, jnp.arange(2 * chips, dtype=jnp.int32)))
+        order = jnp.concatenate([worked + core, worked + 1 - core]) + 0 * order_in
         upstream = jnp.take(grad_hidden[0, 0], order, axis=0)
         saved = jnp.take(saved_pre[0, 0], order, axis=0)
         grad_pre = swiglu_backward(upstream, saved).reshape(2, chips, capacity, 2 * hid_units)
@@ -84,20 +90,13 @@
             jnp.bfloat16
         )
         returned = lax.all_to_all(pair_sum, CHIPS, split_axis=0, concat_axis=0, tiled=True)
-        rows, returned = lax.optimization_barrier((rows, returned))
 
-        fwd_table = slot_table(fwd_ids, experts, capacity).astype(jnp.bfloat16)
-        picked = jnp.einsum(
-            "ect,td->ecd", fwd_table, rows, preferred_element_type=jnp.float32
-        ).astype(jnp.bfloat16)
         bwd_table = slot_table(bwd_ids, experts, capacity).astype(jnp.bfloat16)
         grad_in = jnp.einsum(
             "ect,ecd->td", bwd_table, returned, preferred_element_type=jnp.float32
         ).astype(jnp.bfloat16)
-        picked, grad_in = lax.optimization_barrier((picked, grad_in))
         grad_rows = lax.ppermute(grad_in, RING, ring_route(sections, -1))
 
-        arrived = lax.all_to_all(picked, CHIPS, split_axis=0, concat_axis=0, tiled=True)
 
         both = lax.all_gather(arrived, "core", axis=0, tiled=False)
         projected = jnp.einsum(

time: 251 us -> 259 us (1.032)
  blocking collectives: 67.7 us -> 0 us
  waiting for transfers between devices: 92 us -> 153 us
  starting transfers between devices: 9.74 us -> 16.4 us
  matrix products: 40.8 us -> 44.8 us
    all_to_all x1 -> x0, blocking collectives: 67.7 us -> none  [shards(): lax.all_to_all(picked, CHIPS, split_axis=0, concat_axis=0, tiled=True)]
    ppermute x1, waiting for transfers between devices: 58.5 us -> 0.01 us  [swap_ylo(): return lax.ppermute(block, 'ylo', [(0, 1), (1, 0)])]
    all_to_all x1, waiting for transfers between devices: 0.01 us -> 58.4 us  [shards(): lax.all_to_all(pair_sum, CHIPS, split_axis=0, concat_axis=0, tiled=True)]
    all_to_all x0 -> x1, waiting for transfers between devices: none -> 36.7 us  [shards(): lax.all_to_all(picked, CHIPS, split_axis=0, concat_axis=0, tiled=True)]
    ppermute x1, waiting for transfers between devices: 0.01 us -> 36.1 us  [shards(): rows = lax.ppermute(prev_out[0], RING, ring_route(sections, 1))]
    all_gather x1, waiting for transfers between devices: 24.3 us -> 0.01 us  [shards(): both = lax.all_gather(arrived, 'core', axis=0, tiled=False)]
    ppermute x1, waiting for transfers between devices: 0.01 us -> 21.9 us  [shards(): grad_rows = lax.ppermute(grad_in, RING, ring_route(sections, -1))]
    ppermute x1, waiting for transfers between devices: 9.15 us -> 0.01 us  [shards(): other_part = lax.ppermute(partial_rows[1], 'core', [(0, 1), (1, 0)])]
  transfers between devices with their start and end apart: 6 -> 7, of which waited for: 3 -> 4; matrix products, arithmetic and copies ran while one was open for 9% -> 25% of each run, Pallas kernels for 0% -> 0%
where the time goes in v7:
time: 259 us; the launch traced here: 256 us
  waiting for transfers between devices  153 us (59%)
  matrix products  44.8 us (17%)
  starting transfers between devices  16.4 us (6%)
  between operations  14.2 us (5%)
  local copies, waits for them, and re-layouts  14.1 us (5%)
  other arithmetic  13.9 us (5%)
    all_to_all x1, waiting for transfers between devices, shards(): lax.all_to_all(pair_sum, CHIPS, split_axis=0, concat_axis=0, tiled=True)  58.4 us
    all_to_all x1, waiting for transfers between devices, shards(): lax.all_to_all(picked, CHIPS, split_axis=0, concat_axis=0, tiled=True)  36.7 us
    ppermute x1, waiting for transfers between devices, shards(): rows = lax.ppermute(prev_out[0], RING, ring_route(sections, 1))  36.1 us
    ppermute x1, waiting for transfers between devices, shards(): grad_rows = lax.ppermute(grad_in, RING, ring_route(sections, -1))  21.9 us
    dot_general x1, matrix products, shards(): jnp.einsum('kech,dh->kecd', grad_pre, weights, preferred_element_type=jnp...  19.1 us
    dot_general x1, matrix products, shards(): jnp.einsum('scd,dh->sch', both.reshape(2 * experts, capacity, model_width...  16.5 us
    convert_element_type x1, other arithmetic, shards(): (partial_rows[0].astype(jnp.float32) + other_part.astype(jnp.float32)).as...  8.85 us
    all_to_all x1, starting transfers between devices, shards(): lax.all_to_all(picked, CHIPS, split_axis=0, concat_axis=0, tiled=True)  6.77 us
  transfers between devices with their start and end apart: 7, of which 4 were waited for; matrix products, arithmetic and copies ran while one was open for 25% of the time, Pallas kernels for 0%

profile of v7, /device:TPU:30, one launch (start us, length us, event | category | flops | bytes accessed | tf_op | source)
XLA Modules:
  0.0 256.4 jit_solution(4141985982064885043)
XLA Ops:
  7.2 0.8 pad_add_fusion
  8.0 0.7 collective-permute-start
  8.7 1.0 collective-permute-start.1
  9.8 0.6 gather_fusion.2
  10.5 1.7 gather_fusion.1
  12.3 0.3 select_convert_fusion
  12.6 0.9 fusion.12
  13.8 0.1 eq.78
  13.9 0.6 reduce-window.14
  14.5 0.2 slice_reduce_fusion.1
  15.1 0.3 bitcast_reduce_fusion.1
  15.4 0.2 copy.37
  15.6 36.1 %collective-permute-done.1 = bf16[128,7168]{1,0:T(8,128)(2,1)} collective-permute-done((bf16[128,7168]{1,0:T(8,128)(2,1)}, bf16[128,7168]{1,0:T(8,128)(2,1)}, u32[]{:S(2)}, u32[]{:S(2)}) %collective-permute-start.1) | collective-permute-done | bytes 1835040 | tf_op jit(solution)/shard_map/ppermute | solution.py:73
  51.7 5.5 %convolution_convert_fusion = bf16[8,48,7168]{2,1,0:T(8,128)(2,1)} fusion(bf16[128,7168]{1,0:T(8,128)(2,1)} %collective-permute-done.1, bf16[128,8,48]{0,2,1:T(8,128)(2,1)S(1)} %copy.37), kind=kOutput, calls=%fused_computation.10 | convolution fusion | flops 707395584 | bytes 7438336 | tf_op jit(solution)/shard_map/ect,td->ecd/dot_general | solution.py:76
  57.2 6.8 %all-to-all-start = ((bf16[8,48,7168]{2,1,0:T(8,128)(2,1)}), bf16[8,48,7168]{2,1,0:T(8,128)(2,1)}, u32[]{:S(2)}, u32[]{:S(2)}) async-start(bf16[8,48,7168]{2,1,0:T(8,128)(2,1)} %convolution_convert_fusion), calls=%async_computation | async-start | bytes 11010048 | tf_op jit(solution)/shard_map/all_to_all | solution.py:79
  64.0 19.1 %fusion.4 = bf16[2,8,48,7168]{3,2,1,0:T(8,128)(2,1)} fusion(bf16[1,1,7168,1024]{3,2,1,0:T(8,128)(2,1)} %param.10, bf16[2,8,48,512]{3,2,1,0:T(8,128)(2,1)S(1)} %bitcast.66, bf16[2,8,48,512]{3,2,1,0:T(8,128)(2,1)S(1)} %bitcast.65), kind=kOutput, calls=%fused_computation.7 | convolution fusion | flops 11282939904 | bytes 27262976 | tf_op jit(solution)/shard_map/kech,dh->kecd/dot_general | solution.py:85
  83.1 5.4 %slice_bitcast_fusion = bf16[8,48,7168]{2,1,0:T(8,128)(2,1)} fusion(bf16[2,8,48,7168]{3,2,1,0:T(8,128)(2,1)} %fusion.4), kind=kLoop, calls=%fused_computation.13 | loop fusion | bytes 11010048 | tf_op jit(solution)/shard_map/squeeze | solution.py:88
  88.5 36.7 %all-to-all-done = bf16[8,48,7168]{2,1,0:T(8,128)(2,1)} async-done(((bf16[8,48,7168]{2,1,0:T(8,128)(2,1)}), bf16[8,48,7168]{2,1,0:T(8,128)(2,1)}, u32[]{:S(2)}, u32[]{:S(2)}) %all-to-all-start) | async-done | bytes 5505056 | tf_op jit(solution)/shard_map/all_to_all | solution.py:79
  125.2 8.8 %fusion.7 = bf16[8,48,7168]{2,1,0:T(8,128)(2,1)} fusion(bf16[8,48,7168]{2,1,0:T(8,128)(2,1)} %collective-permute-done.2, bf16[2,8,48,7168]{3,2,1,0:T(8,128)(2,1)} %fusion.4), kind=kLoop, calls=%fused_computation.9 | loop fusion | flops 11010048 | bytes 16515072 | tf_op jit(solution)/shard_map/convert_element_type | solution.py:89
  134.1 6.1 %all-to-all-start.1 = ((bf16[8,48,7168]{2,1,0:T(8,128)(2,1)}), bf16[8,48,7168]{2,1,0:T(8,128)(2,1)}, u32[]{:S(2)}, u32[]{:S(2)}) async-start(bf16[8,48,7168]{2,1,0:T(8,128)(2,1)} %fusion.7), calls=%async_computation.1 | async-start | bytes 11010048 | tf_op jit(solution)/shard_map/all_to_all | solution.py:92
  140.6 0.6 reduce-window.16
  141.2 0.2 slice_reduce_fusion
  141.8 0.3 bitcast_reduce_fusion
  142.1 0.2 copy.38
  142.3 58.4 %all-to-all-done.1 = bf16[8,48,7168]{2,1,0:T(8,128)(2,1)} async-done(((bf16[8,48,7168]{2,1,0:T(8,128)(2,1)}), bf16[8,48,7168]{2,1,0:T(8,128)(2,1)}, u32[]{:S(2)}, u32[]{:S(2)}) %all-to-all-start.1) | async-done | bytes 5505056 | tf_op jit(solution)/shard_map/all_to_all | solution.py:92
  200.7 3.7 %fusion.8 = bf16[128,7168]{1,0:T(8,128)(2,1)S(1)} fusion(bf16[8,48,7168]{2,1,0:T(8,128)(2,1)} %all-to-all-done.1, bf16[128,8,48]{0,2,1:T(8,128)(2,1)S(1)} %copy.38), kind=kOutput, calls=%fused_computation.12 | convolution fusion | flops 705560576 | bytes 7438336 | tf_op jit(solution)/shard_map/ect,ecd->td/dot_general | solution.py:95
  204.4 1.8 collective-permute-start.3
  206.2 16.5 %fusion.2 = f32[16,48,1024]{2,1,0:T(8,128)S(1)} fusion(bf16[16,48,7168]{2,1,0:T(8,128)(2,1)} %all-gather.3.cloned.1.call-done, bf16[1,1,7168,1024]{3,2,1,0:T(8,128)(2,1)} %param.10), kind=kOutput, calls=%fused_computation.5 | convolution fusion | flops 11274289152 | bytes 28835840 | tf_op jit(solution)/shard_map/scd,dh->sch/dot_general | solution.py:102
  222.7 0.5 fusion.15
  223.2 1.5 gather_fusion
  224.7 21.9 %collective-permute-done.3 = bf16[128,7168]{1,0:T(8,128)(2,1)} collective-permute-done((bf16[128,7168]{1,0:T(8,128)(2,1)S(1)}, bf16[128,7168]{1,0:T(8,128)(2,1)}, u32[]{:S(2)}, u32[]{:S(2)}) %collective-permute-start.3) | collective-permute-done | bytes 1835040 | tf_op jit(solution)/shard_map/ppermute | solution.py:98
  246.6 3.0 %copy.40 = bf16[1,128,7168]{2,1,0:T(8,128)(2,1)} copy(bf16[1,128,7168]{2,1,0:T(8,128)(2,1)} %bitcast.27) | data formatting | bytes 3670016
  (38 shorter events, 1.6 us)
Async XLA Ops:
  7.2 2.7 %copy-start = (bf16[1,1,16,48,1024]{4,3,2,1,0:T(8,128)(2,1)S(1)}, bf16[1,1,16,48,1024]{4,3,2,1,0:T(8,128)(2,1)}, u32[]{:S(2)}) copy-start(bf16[1,1,16,48,1024]{4,3,2,1,0:T(8,128)(2,1)} %param.13) | copy-start | bytes 4718596
  8.0 5.5 %collective-permute-start = (s32[128,4]{0,1:T(4,128)S(1)}, s32[128,4]{0,1:T(4,128)S(1)}, u32[]{:S(2)}, u32[]{:S(2)}) collective-permute-start(s32[128,4]{0,1:T(4,128)S(1)} %pad_add_fusion), channel_id=1, source_target_pairs={{0,2},{2,0},{1,3},{3,1},{4,6},{6,4},{5,7},{7,5},{8,10},{10,8},{9,1... | collective-permute-start | bytes 6152 | tf_op jit(solution)/shard_map/ppermute | solution.py:23
  8.7 43.0 %collective-permute-start.1 = (bf16[128,7168]{1,0:T(8,128)(2,1)}, bf16[128,7168]{1,0:T(8,128)(2,1)}, u32[]{:S(2)}, u32[]{:S(2)}) collective-permute-start(bf16[128,7168]{1,0:T(8,128)(2,1)} %bitcast.69), channel_id=1, source_target_pairs={{0,18},{2,16},{16,34},{18,32},{32,50},{34,48},{48,66},{50,64},{64,... | collective-permute-start | bytes 5505032 | tf_op jit(solution)/shard_map/ppermute | solution.py:73
  57.2 68.0 %all-to-all-start = ((bf16[8,48,7168]{2,1,0:T(8,128)(2,1)}), bf16[8,48,7168]{2,1,0:T(8,128)(2,1)}, u32[]{:S(2)}, u32[]{:S(2)}) async-start(bf16[8,48,7168]{2,1,0:T(8,128)(2,1)} %convolution_convert_fusion), calls=%async_computation | async-start | bytes 11010048 | tf_op jit(solution)/shard_map/all_to_all | solution.py:79
  64.0 142.2 %all-gather.3.cloned.1.call-start = ((), (), s32[]{:S(2)}) async-start(), calls=%async_computation.2 | async-start | bytes 16515072 | tf_op jit(solution)/shard_map/all_gather | solution.py:101
  88.5 36.7 %collective-permute-start.2 = (bf16[8,48,7168]{2,1,0:T(8,128)(2,1)}, bf16[8,48,7168]{2,1,0:T(8,128)(2,1)}, u32[]{:S(2)}, u32[]{:S(2)}) collective-permute-start(bf16[8,48,7168]{2,1,0:T(8,128)(2,1)} %slice_bitcast_fusion), channel_id=1, source_target_pairs={{0,1},{1,0},{2,3},{3,2},{4,5},{5,4},{6,7},{7,6},{8,9},{9,8},{10,11... | collective-permute-start | bytes 16515080 | tf_op jit(solution)/shard_map/ppermute | solution.py:88
  134.1 6.1 %copy-start.2 = (s32[16]{0:T(128)S(1)}, s32[16]{0:T(128)}, u32[]{:S(2)}) copy-start(s32[16]{0:T(128)} %constant.91) | copy-start | bytes 196
  134.1 66.6 %all-to-all-start.1 = ((bf16[8,48,7168]{2,1,0:T(8,128)(2,1)}), bf16[8,48,7168]{2,1,0:T(8,128)(2,1)}, u32[]{:S(2)}, u32[]{:S(2)}) async-start(bf16[8,48,7168]{2,1,0:T(8,128)(2,1)} %fusion.7), calls=%async_computation.1 | async-start | bytes 11010048 | tf_op jit(solution)/shard_map/all_to_all | solution.py:92
  204.4 42.2 %collective-permute-start.3 = (bf16[128,7168]{1,0:T(8,128)(2,1)S(1)}, bf16[128,7168]{1,0:T(8,128)(2,1)}, u32[]{:S(2)}, u32[]{:S(2)}) collective-permute-start(bf16[128,7168]{1,0:T(8,128)(2,1)S(1)} %fusion.8), channel_id=1, source_target_pairs={{0,114},{2,112},{16,2},{18,0},{32,18},{34,16},{48,34},{50,32},{64,... | collective-permute-start | bytes 5505032 | tf_op jit(solution)/shard_map/ppermute | solution.py:98
  246.5 3.0 %copy-start.1 = (bf16[1,1,16,48,1024]{4,3,2,1,0:T(8,128)(2,1)S(1)}, bf16[1,1,16,48,1024]{4,3,2,1,0:T(8,128)(2,1)}, u32[]{:S(2)}) copy-start(bf16[1,1,16,48,1024]{4,3,2,1,0:T(8,128)(2,1)} %param.13) | copy-start | bytes 4718596
Sparse Core Ops, SparseCore 0:
  125.3 26.1 all-gather.2

commit v8 on v5

--- a/solution.py
+++ b/solution.py
@@ -90,28 +90,28 @@
         picked = jnp.einsum(
             "ect,td->ecd", fwd_table, rows, preferred_element_type=jnp.float32
         ).astype(jnp.bfloat16)
+        arrived = lax.all_to_all(picked, CHIPS, split_axis=0, concat_axis=0, tiled=True)
+
+        partner = lax.ppermute(arrived, "core", [(0, 1), (1, 0)])
         bwd_table = slot_table(bwd_ids, experts, capacity).astype(jnp.bfloat16)
         grad_in = jnp.einsum(
             "ect,ecd->td", bwd_table, returned, preferred_element_type=jnp.float32
         ).astype(jnp.bfloat16)
-        picked, grad_in = lax.optimization_barrier((picked, grad_in))
+        grad_in, partner = lax.optimization_barrier((grad_in, partner))
         grad_rows = lax.ppermute(grad_in, RING, ring_route(sections, -1))
 
-        arrived = lax.all_to_all(picked, CHIPS, split_axis=0, concat_axis=0, tiled=True)
-
-        both = lax.all_gather(arrived, "core", axis=0, tiled=False)
         projected = jnp.einsum(
             "scd,dh->sch",
-            both.reshape(2 * experts, capacity, model_width),
+            jnp.concatenate([arrived, partner]),
             weights,
             preferred_element_type=jnp.float32,
         )
         hidden = (jax.nn.silu(projected[..., :hid_units]) * projected[..., hid_units:]).astype(
             jnp.bfloat16
         )
-        blocks = np.arange(2 * experts)
+        blocks = jnp.arange(2 * experts, dtype=jnp.int32)
         chip_of = (blocks // 4) * 2 + (1 - (blocks // 2) % 2)
-        hidden = hidden[(blocks % 2) * chips + chip_of]
+        hidden = jnp.take(hidden, jnp.where(blocks % 2 == core, chip_of, chips + chip_of), axis=0)
         hidden, grad_rows = lax.optimization_barrier((hidden, grad_rows))
         return (hidden[None, None], grad_rows[None])
 

time: 251 us -> 244 us (0.972)
  between operations: 14.2 us -> 0.86 us
  other arithmetic: 11.4 us -> 16 us
  waiting for transfers between devices: 92 us -> 95.1 us
  matrix products: 40.8 us -> 43.8 us
  local copies, waits for them, and re-layouts: 13.7 us -> 10.9 us
    ppermute x1, waiting for transfers between devices: 0.01 us -> 24.4 us  [shards(): grad_rows = lax.ppermute(grad_in, RING, ring_route(sections, -1))]
    all_gather x1 -> x0, waiting for transfers between devices: 24.3 us -> none  [shards(): both = lax.all_gather(arrived, 'core', axis=0, tiled=False)]
  transfers between devices with their start and end apart: 6 -> 6, of which waited for: 3 -> 5; matrix products, arithmetic and copies ran while one was open for 9% -> 12% of each run, Pallas kernels for 0% -> 0%
where the time goes in v8:
time: 244 us; the launch traced here: 243 us
  waiting for transfers between devices  95.1 us (39%)
  blocking collectives  67.5 us (28%)
  matrix products  43.8 us (18%)
  other arithmetic  16 us (7%)
  local copies, waits for them, and re-layouts  10.9 us (4%)
  starting transfers between devices  9.12 us (4%)
    all_to_all x1, blocking collectives, shards(): lax.all_to_all(picked, CHIPS, split_axis=0, concat_axis=0, tiled=True)  67.5 us
    ppermute x1, waiting for transfers between devices, swap_ylo(): return lax.ppermute(block, 'ylo', [(0, 1), (1, 0)])  59.2 us
    ppermute x1, waiting for transfers between devices, shards(): grad_rows = lax.ppermute(grad_in, RING, ring_route(sections, -1))  24.4 us
    dot_general x1, matrix products, shards(): jnp.einsum('kech,dh->kecd', grad_pre, weights, preferred_element_type=jnp...  19.1 us
    dot_general x1, matrix products, shards(): jnp.einsum('scd,dh->sch', jnp.concatenate([arrived, partner]), weights, p...  18.2 us
    ppermute x1, waiting for transfers between devices, shards(): other_part = lax.ppermute(partial_rows[1], 'core', [(0, 1), (1, 0)])  9.15 us
    convert_element_type x1, other arithmetic, shards(): (partial_rows[0].astype(jnp.float32) + other_part.astype(jnp.float32)).as...  7.22 us
    all_to_all x1, starting transfers between devices, shards(): lax.all_to_all(pair_sum, CHIPS, split_axis=0, concat_axis=0, tiled=True)  6.91 us
  transfers between devices with their start and end apart: 6, of which 5 were waited for; matrix products, arithmetic and copies ran while one was open for 12% of the time, Pallas kernels for 0%

profile of v8, /device:TPU:30, one launch (start us, length us, event | category | flops | bytes accessed | tf_op | source)
XLA Modules:
  0.0 243.2 jit_solution(3049774597145347748)
XLA Ops:
  0.9 1.2 copy-done
  2.0 0.6 gather_fusion
  2.7 1.9 select_convert_fusion
  4.7 0.6 gather_fusion.1
  5.3 2.7 %fusion.15 = (bf16[16,48,512]{2,1,0:T(8,128)(2,1)S(1)}, bf16[16,48,512]{2,1,0:T(8,128)(2,1)S(1)}) fusion(f32[16,48,1024]{2,1,0:T(8,128)} %select_convert_fusion, bf16[16,48,512]{2,1,0:T(8,128)(2,1)S(1)} %gather_fusion.1, pred[16]{0:T(512)(128)(4,1)S(1)} %get-tuple-element.15), kind=kLoop, calls=%fused_computation.23 | loop fusion | flops 5898240 | bytes 5505040 | tf_op jit(solution)/shard_map/convert.6
  8.0 19.1 %fusion.4 = bf16[2,8,48,7168]{3,2,1,0:T(8,128)(2,1)} fusion(bf16[1,1,7168,1024]{3,2,1,0:T(8,128)(2,1)} %param.10, bf16[2,8,48,512]{3,2,1,0:T(8,128)(2,1)S(1)} %bitcast.65, bf16[2,8,48,512]{3,2,1,0:T(8,128)(2,1)S(1)} %bitcast.64), kind=kOutput, calls=%fused_computation.7 | convolution fusion | flops 11282939904 | bytes 27262976 | tf_op jit(solution)/shard_map/kech,dh->kecd/dot_general | solution.py:79
  27.1 3.1 %slice_bitcast_fusion = bf16[8,48,7168]{2,1,0:T(8,128)(2,1)S(1)} fusion(bf16[2,8,48,7168]{3,2,1,0:T(8,128)(2,1)} %fusion.4), kind=kLoop, calls=%fused_computation.16 | loop fusion | bytes 11010048 | tf_op jit(solution)/shard_map/squeeze | solution.py:82
  30.2 9.2 %collective-permute-done.2 = bf16[8,48,7168]{2,1,0:T(8,128)(2,1)} collective-permute-done((bf16[8,48,7168]{2,1,0:T(8,128)(2,1)S(1)}, bf16[8,48,7168]{2,1,0:T(8,128)(2,1)}, u32[]{:S(2)}, u32[]{:S(2)}) %collective-permute-start.2) | collective-permute-done | bytes 5505056 | tf_op jit(solution)/shard_map/ppermute | solution.py:82
  39.4 7.2 %fusion.10 = bf16[8,48,7168]{2,1,0:T(8,128)(2,1)} fusion(bf16[8,48,7168]{2,1,0:T(8,128)(2,1)} %collective-permute-done.2, bf16[2,8,48,7168]{3,2,1,0:T(8,128)(2,1)S(1)} %copy-done.2), kind=kLoop, calls=%fused_computation.12 | loop fusion | flops 11010048 | bytes 16515072 | tf_op jit(solution)/shard_map/convert_element_type | solution.py:83
  46.6 6.9 %all-to-all-start = ((bf16[8,48,7168]{2,1,0:T(8,128)(2,1)}), bf16[8,48,7168]{2,1,0:T(8,128)(2,1)}, u32[]{:S(2)}, u32[]{:S(2)}) async-start(bf16[8,48,7168]{2,1,0:T(8,128)(2,1)} %fusion.10), calls=%async_computation | async-start | bytes 11010048 | tf_op jit(solution)/shard_map/all_to_all | solution.py:86
  53.5 1.2 collective-permute-start
  54.7 59.2 %collective-permute-done = s32[128,4]{0,1:T(4,128)S(1)} collective-permute-done((s32[128,4]{0,1:T(4,128)S(1)}, s32[128,4]{0,1:T(4,128)S(1)}, u32[]{:S(2)}, u32[]{:S(2)}) %collective-permute-start) | collective-permute-done | bytes 2080 | tf_op jit(solution)/shard_map/ppermute | solution.py:23
  114.3 0.6 reduce-window.14
  114.9 0.2 slice_reduce_fusion.1
  115.5 0.3 bitcast_reduce_fusion.1
  115.8 0.2 copy.29
  116.0 0.2 all-to-all-done
  116.2 1.6 convolution_convert_fusion
  117.8 67.5 %all_to_all.10 = bf16[8,48,7168]{2,1,0:T(8,128)(2,1)} all-to-all(bf16[8,48,7168]{2,1,0:T(8,128)(2,1)S(1)} %convolution_convert_fusion), channel_id=1, replica_groups=mesh['x'=4,'yhi'=2,'z'=4,'ylo'=2,'core'=2] {'z','ylo'}, dimensions={0} | all-to-all | bytes 11010048 | tf_op jit(solution)/shard_map/all_to_all | solution.py:93
  185.7 0.6 reduce-window.16
  186.3 0.2 slice_reduce_fusion
  186.9 0.3 bitcast_reduce_fusion
  187.3 0.2 copy.30
  187.5 5.0 %fusion.11 = bf16[128,7168]{1,0:T(8,128)(2,1)} fusion(bf16[8,48,7168]{2,1,0:T(8,128)(2,1)} %all-to-all-done, bf16[128,8,48]{0,2,1:T(8,128)(2,1)S(1)} %copy.30), kind=kOutput, calls=%fused_computation.15 | convolution fusion | flops 705560576 | bytes 7438336 | tf_op jit(solution)/shard_map/ect,ecd->td/dot_general | solution.py:97
  192.4 2.2 collective-permute-done.3
  194.7 0.9 collective-permute-start.4
  195.6 18.2 %fusion = f32[16,48,1024]{2,1,0:T(8,128)S(1)} fusion(bf16[1,1,7168,1024]{3,2,1,0:T(8,128)(2,1)} %param.10, bf16[8,48,7168]{2,1,0:T(8,128)(2,1)} %collective-permute-done.3, bf16[8,48,7168]{2,1,0:T(8,128)(2,1)} %all_to_all.10), kind=kOutput, calls=%fused_computation.3 | convolution fusion | flops 11279794176 | bytes 28835840 | tf_op jit(solution)/shard_map/scd,dh->sch/dot_general | solution.py:103
  213.8 0.5 fusion.18
  214.3 0.6 gather_fusion.2
  214.9 1.0 broadcast_select_fusion
  215.9 24.4 %collective-permute-done.4 = bf16[128,7168]{1,0:T(8,128)(2,1)} collective-permute-done((bf16[128,7168]{1,0:T(8,128)(2,1)}, bf16[128,7168]{1,0:T(8,128)(2,1)}, u32[]{:S(2)}, u32[]{:S(2)}) %collective-permute-start.4) | collective-permute-done | bytes 1835040 | tf_op jit(solution)/shard_map/ppermute | solution.py:101
  240.4 2.8 %copy.32 = bf16[1,128,7168]{2,1,0:T(8,128)(2,1)} copy(bf16[1,128,7168]{2,1,0:T(8,128)(2,1)} %bitcast.27) | data formatting | bytes 3670016
  (46 shorter events, 1.9 us)
Async XLA Ops:
  0.6 1.4 copy-start
  2.7 2.0 copy-start.3
  27.1 12.3 %copy-start.2 = (bf16[2,8,48,7168]{3,2,1,0:T(8,128)(2,1)S(1)}, bf16[2,8,48,7168]{3,2,1,0:T(8,128)(2,1)}, u32[]{:S(2)}) copy-start(bf16[2,8,48,7168]{3,2,1,0:T(8,128)(2,1)} %fusion.4) | copy-start | bytes 33030148
  30.1 9.2 %collective-permute-start.2 = (bf16[8,48,7168]{2,1,0:T(8,128)(2,1)S(1)}, bf16[8,48,7168]{2,1,0:T(8,128)(2,1)}, u32[]{:S(2)}, u32[]{:S(2)}) collective-permute-start(bf16[8,48,7168]{2,1,0:T(8,128)(2,1)S(1)} %slice_bitcast_fusion), channel_id=1, source_target_pairs={{0,1},{1,0},{2,3},{3,2},{4,5},{5,4},{6,7},{7,6},{8,9},{9,8},{10,11... | collective-permute-start | bytes 16515080 | tf_op jit(solution)/shard_map/ppermute | solution.py:82
  46.6 6.9 %copy-start.4 = (s32[1,128,2]{1,2,0:T(2,128)S(1)}, s32[1,128,2]{1,2,0:T(2,128)}, u32[]{:S(2)}) copy-start(s32[1,128,2]{1,2,0:T(2,128)} %param.11) | copy-start | bytes 3076
  46.6 6.9 %copy-start.5 = (s32[1,128,2]{1,2,0:T(2,128)S(1)}, s32[1,128,2]{1,2,0:T(2,128)}, u32[]{:S(2)}) copy-start(s32[1,128,2]{1,2,0:T(2,128)} %param.9) | copy-start | bytes 3076
  46.6 69.6 %all-to-all-start = ((bf16[8,48,7168]{2,1,0:T(8,128)(2,1)}), bf16[8,48,7168]{2,1,0:T(8,128)(2,1)}, u32[]{:S(2)}, u32[]{:S(2)}) async-start(bf16[8,48,7168]{2,1,0:T(8,128)(2,1)} %fusion.10), calls=%async_computation | async-start | bytes 11010048 | tf_op jit(solution)/shard_map/all_to_all | solution.py:86
  53.5 62.5 %collective-permute-start.1 = (bf16[128,7168]{1,0:T(8,128)(2,1)}, bf16[128,7168]{1,0:T(8,128)(2,1)S(1)}, u32[]{:S(2)}, u32[]{:S(2)}) collective-permute-start(bf16[128,7168]{1,0:T(8,128)(2,1)} %bitcast.68), channel_id=1, source_target_pairs={{0,18},{2,16},{16,34},{18,32},{32,50},{34,48},{48,66},{50,64},{64,... | collective-permute-start | bytes 5505032 | tf_op jit(solution)/shard_map/ppermute | solution.py:73
  53.5 60.3 %collective-permute-start = (s32[128,4]{0,1:T(4,128)S(1)}, s32[128,4]{0,1:T(4,128)S(1)}, u32[]{:S(2)}, u32[]{:S(2)}) collective-permute-start(s32[128,4]{0,1:T(4,128)S(1)} %pad_add_fusion), channel_id=1, source_target_pairs={{0,2},{2,0},{1,3},{3,1},{4,6},{6,4},{5,7},{7,5},{8,10},{10,8},{9,1... | collective-permute-start | bytes 6152 | tf_op jit(solution)/shard_map/ppermute | solution.py:23
  185.3 9.4 %collective-permute-start.3 = (bf16[8,48,7168]{2,1,0:T(8,128)(2,1)}, bf16[8,48,7168]{2,1,0:T(8,128)(2,1)}, u32[]{:S(2)}, u32[]{:S(2)}) collective-permute-start(bf16[8,48,7168]{2,1,0:T(8,128)(2,1)} %all_to_all.10), channel_id=1, source_target_pairs={{0,1},{1,0},{2,3},{3,2},{4,5},{5,4},{6,7},{7,6},{8,9},{9,8},{10,11... | collective-permute-start | bytes 16515080 | tf_op jit(solution)/shard_map/ppermute | solution.py:95
  194.7 45.7 %collective-permute-start.4 = (bf16[128,7168]{1,0:T(8,128)(2,1)}, bf16[128,7168]{1,0:T(8,128)(2,1)}, u32[]{:S(2)}, u32[]{:S(2)}) collective-permute-start(bf16[128,7168]{1,0:T(8,128)(2,1)} %fusion.11), channel_id=1, source_target_pairs={{0,114},{2,112},{16,2},{18,0},{32,18},{34,16},{48,34},{50,32},{64,... | collective-permute-start | bytes 5505032 | tf_op jit(solution)/shard_map/ppermute | solution.py:101
  213.8 29.4 %copy-start.1 = (bf16[1,1,16,48,1024]{4,3,2,1,0:T(8,128)(2,1)S(1)}, bf16[1,1,16,48,1024]{4,3,2,1,0:T(8,128)(2,1)}, u32[]{:S(2)}) copy-start(bf16[1,1,16,48,1024]{4,3,2,1,0:T(8,128)(2,1)} %param.13) | copy-start | bytes 4718596

commit v9 on v8

--- a/solution.py
+++ b/solution.py
@@ -72,15 +72,21 @@
 
         rows = lax.ppermute(prev_out[0], RING, ring_route(sections, 1))
 
-        order = jnp.concatenate([worked + core, worked + 1 - core])
-        upstream = jnp.take(grad_hidden[0, 0], order, axis=0)
-        saved = jnp.take(saved_pre[0, 0], order, axis=0)
-        grad_pre = swiglu_backward(upstream, saved).reshape(2, chips, capacity, 2 * hid_units)
+        def by_chip(blocks):
+            split = blocks.reshape((zs, 2, 2) + blocks.shape[1:])[:, ::-1]
+            return jnp.swapaxes(jnp.swapaxes(split, 1, 2), 0, 1).reshape(blocks.shape)
+
+        grad_pre = swiglu_backward(by_chip(grad_hidden[0, 0]), by_chip(saved_pre[0, 0]))
         partial_rows = jnp.einsum(
-            "kech,dh->kecd", grad_pre, weights, preferred_element_type=jnp.float32
-        ).astype(jnp.bfloat16)
-        other_part = lax.ppermute(partial_rows[1], "core", [(0, 1), (1, 0)])
-        pair_sum = (partial_rows[0].astype(jnp.float32) + other_part.astype(jnp.float32)).astype(
+            "kch,dh->kcd",
+            grad_pre.reshape(2, chips * capacity, 2 * hid_units),
+            weights,
+            preferred_element_type=jnp.float32,
+        ).astype(jnp.bfloat16).reshape(2, chips, capacity, model_width)
+        send_part = lax.dynamic_index_in_dim(partial_rows, 1 - core, axis=0, keepdims=False)
+        keep_part = lax.dynamic_index_in_dim(partial_rows, core, axis=0, keepdims=False)
+        other_part = lax.ppermute(send_part, "core", [(0, 1), (1, 0)])
+        pair_sum = (keep_part.astype(jnp.float32) + other_part.astype(jnp.float32)).astype(
             jnp.bfloat16
         )
         returned = lax.all_to_all(pair_sum, CHIPS, split_axis=0, concat_axis=0, tiled=True)

time: 244 us -> 245 us (level)
  local copies, waits for them, and re-layouts: 10.9 us -> 13.8 us
  matrix products: 43.8 us -> 41.2 us
    another operation x3 -> x5, local copies, waits for them, and re-layouts: 0.22 us -> 2.71 us  [the longest x2 2.49 us: by_chip(): split = blocks.reshape((zs, 2, 2) + blocks.shape[1:])[:, ::-1]]
where the time goes in v9:
time: 245 us
  waiting for transfers between devices  96.2 us (39%)
  blocking collectives  67.5 us (28%)
  matrix products  41.2 us (17%)
  other arithmetic  16.1 us (7%)
  local copies, waits for them, and re-layouts  13.8 us (6%)
  starting transfers between devices  9.21 us (4%)
    all_to_all x1, blocking collectives, shards(): lax.all_to_all(picked, CHIPS, split_axis=0, concat_axis=0, tiled=True)  67.5 us
    ppermute x1, waiting for transfers between devices, swap_ylo(): return lax.ppermute(block, 'ylo', [(0, 1), (1, 0)])  59 us
    ppermute x1, waiting for transfers between devices, shards(): grad_rows = lax.ppermute(grad_in, RING, ring_route(sections, -1))  24.2 us
    dot_general x1, matrix products, shards(): jnp.einsum('scd,dh->sch', jnp.concatenate([arrived, partner]), weights, p...  18.2 us
    dot_general x1, matrix products, shards(): jnp.einsum('kch,dh->kcd', grad_pre.reshape(2, chips * capacity, 2 * hid_u...  17.7 us
    ppermute x1, waiting for transfers between devices, shards(): other_part = lax.ppermute(send_part, 'core', [(0, 1), (1, 0)])  9.37 us
    convert_element_type x1, other arithmetic, shards(): (keep_part.astype(jnp.float32) + other_part.astype(jnp.float32)).astype(j...  8.78 us
    all_to_all x1, starting transfers between devices, shards(): lax.all_to_all(pair_sum, CHIPS, split_axis=0, concat_axis=0, tiled=True)  6.91 us
  transfers between devices with their start and end apart: 6, of which 5 were waited for; matrix products, arithmetic and copies ran while one was open for 12% of the time, Pallas kernels for 0%

profile of v9, /device:TPU:30, one launch (start us, length us, event | category | flops | bytes accessed | tf_op | source)
XLA Modules:
  0.0 244.8 jit_solution(14658929568368648531)
XLA Ops:
  0.6 1.6 copy.31
  2.2 0.4 reverse_convert_fusion
  2.6 0.7 copy-done
  3.3 0.9 copy.30
  4.3 3.0 %fusion.16 = (bf16[16,48,512]{2,1,0:T(8,128)(2,1)}, bf16[16,48,512]{2,1,0:T(8,128)(2,1)}) fusion(f32[16,48,1024]{2,1,0:T(8,128)S(1)} %bitcast.64, bf16[4,2,2,48,512]{4,3,1,0,2:T(8,128)(2,1)} %copy.30), kind=kLoop, calls=%fused_computation.21 | loop fusion | flops 5505024 | bytes 5505024 | tf_op jit(solution)/shard_map/convert.10
  7.3 17.7 %fusion.4 = bf16[2,384,7168]{2,1,0:T(8,128)(2,1)} fusion(bf16[1,1,7168,1024]{3,2,1,0:T(8,128)(2,1)} %param.8, bf16[2,384,512]{2,1,0:T(8,128)(2,1)} %bitcast.71, bf16[2,384,512]{2,1,0:T(8,128)(2,1)} %bitcast.70), kind=kOutput, calls=%fused_computation.5 | convolution fusion | flops 11282939904 | bytes 27262976 | tf_op jit(solution)/shard_map/kch,dh->kcd/dot_general | solution.py:80
  25.0 5.3 %dynamic-slice_bitcast_fusion = bf16[8,48,7168]{2,1,0:T(8,128)(2,1)} fusion(bf16[2,8,48,7168]{3,2,1,0:T(8,128)(2,1)} %bitcast.65, s32[]{:T(128)S(6)} %select_n.122), kind=kLoop, calls=%fused_computation.14 | loop fusion | bytes 11010052 | tf_op jit(solution)/shard_map/jit(dynamic_index_in_dim)/squeeze | solution.py:86
  30.3 9.4 %collective-permute-done.2 = bf16[8,48,7168]{2,1,0:T(8,128)(2,1)} collective-permute-done((bf16[8,48,7168]{2,1,0:T(8,128)(2,1)}, bf16[8,48,7168]{2,1,0:T(8,128)(2,1)}, u32[]{:S(2)}, u32[]{:S(2)}) %collective-permute-start.2) | collective-permute-done | bytes 5505056 | tf_op jit(solution)/shard_map/ppermute | solution.py:88
  39.7 8.8 %fusion.10 = bf16[8,48,7168]{2,1,0:T(8,128)(2,1)} fusion(bf16[8,48,7168]{2,1,0:T(8,128)(2,1)} %collective-permute-done.2, bf16[2,8,48,7168]{3,2,1,0:T(8,128)(2,1)} %bitcast.66, s32[]{:T(128)S(6)} %select_n.121), kind=kLoop, calls=%fused_computation.10 | loop fusion | flops 11010048 | bytes 16515076 | tf_op jit(solution)/shard_map/convert_element_type | solution.py:89
  48.4 6.9 %all-to-all-start = ((bf16[8,48,7168]{2,1,0:T(8,128)(2,1)}), bf16[8,48,7168]{2,1,0:T(8,128)(2,1)}, u32[]{:S(2)}, u32[]{:S(2)}) async-start(bf16[8,48,7168]{2,1,0:T(8,128)(2,1)} %fusion.10), calls=%async_computation | async-start | bytes 11010048 | tf_op jit(solution)/shard_map/all_to_all | solution.py:92
  55.4 1.3 collective-permute-start
  56.7 59.0 %collective-permute-done = s32[128,4]{0,1:T(4,128)S(1)} collective-permute-done((s32[128,4]{0,1:T(4,128)S(1)}, s32[128,4]{0,1:T(4,128)S(1)}, u32[]{:S(2)}, u32[]{:S(2)}) %collective-permute-start) | collective-permute-done | bytes 2080 | tf_op jit(solution)/shard_map/ppermute | solution.py:23
  116.1 0.6 reduce-window.14
  116.7 0.2 slice_reduce_fusion.1
  117.3 0.3 bitcast_reduce_fusion.1
  117.7 0.2 copy.36
  117.9 0.2 all-to-all-done
  118.0 1.6 convolution_convert_fusion
  119.6 67.5 %all_to_all.10 = bf16[8,48,7168]{2,1,0:T(8,128)(2,1)} all-to-all(bf16[8,48,7168]{2,1,0:T(8,128)(2,1)S(1)} %convolution_convert_fusion), channel_id=1, replica_groups=mesh['x'=4,'yhi'=2,'z'=4,'ylo'=2,'core'=2] {'z','ylo'}, dimensions={0} | all-to-all | bytes 11010048 | tf_op jit(solution)/shard_map/all_to_all | solution.py:99
  187.6 0.6 reduce-window.16
  188.2 0.2 slice_reduce_fusion
  188.8 0.3 bitcast_reduce_fusion
  189.1 0.2 copy.37
  189.3 3.7 %fusion.11 = bf16[128,7168]{1,0:T(8,128)(2,1)S(1)} fusion(bf16[8,48,7168]{2,1,0:T(8,128)(2,1)} %all-to-all-done, bf16[128,8,48]{0,2,1:T(8,128)(2,1)S(1)} %copy.37), kind=kOutput, calls=%fused_computation.13 | convolution fusion | flops 705560576 | bytes 7438336 | tf_op jit(solution)/shard_map/ect,ecd->td/dot_general | solution.py:103
  193.0 3.5 %collective-permute-done.3 = bf16[8,48,7168]{2,1,0:T(8,128)(2,1)} collective-permute-done((bf16[8,48,7168]{2,1,0:T(8,128)(2,1)}, bf16[8,48,7168]{2,1,0:T(8,128)(2,1)}, u32[]{:S(2)}, u32[]{:S(2)}) %collective-permute-start.3) | collective-permute-done | bytes 5505056 | tf_op jit(solution)/shard_map/ppermute | solution.py:101
  196.5 0.9 collective-permute-start.4
  197.4 18.2 %fusion = f32[16,48,1024]{2,1,0:T(8,128)S(1)} fusion(bf16[1,1,7168,1024]{3,2,1,0:T(8,128)(2,1)} %param.8, bf16[8,48,7168]{2,1,0:T(8,128)(2,1)} %collective-permute-done.3, bf16[8,48,7168]{2,1,0:T(8,128)(2,1)} %all_to_all.10), kind=kOutput, calls=%fused_computation.1 | convolution fusion | flops 11279794176 | bytes 28835840 | tf_op jit(solution)/shard_map/scd,dh->sch/dot_general | solution.py:109
  215.6 0.5 fusion.13
  216.1 0.6 gather_fusion
  216.7 1.0 broadcast_select_fusion
  217.8 24.2 %collective-permute-done.4 = bf16[128,7168]{1,0:T(8,128)(2,1)} collective-permute-done((bf16[128,7168]{1,0:T(8,128)(2,1)S(1)}, bf16[128,7168]{1,0:T(8,128)(2,1)}, u32[]{:S(2)}, u32[]{:S(2)}) %collective-permute-start.4) | collective-permute-done | bytes 1835040 | tf_op jit(solution)/shard_map/ppermute | solution.py:107
  242.0 2.8 %copy.39 = bf16[1,128,7168]{2,1,0:T(8,128)(2,1)} copy(bf16[1,128,7168]{2,1,0:T(8,128)(2,1)} %bitcast.30) | data formatting | bytes 3670016
  (34 shorter events, 1.6 us)
Async XLA Ops:
  2.2 1.1 copy-start
  30.3 9.4 %collective-permute-start.2 = (bf16[8,48,7168]{2,1,0:T(8,128)(2,1)}, bf16[8,48,7168]{2,1,0:T(8,128)(2,1)}, u32[]{:S(2)}, u32[]{:S(2)}) collective-permute-start(bf16[8,48,7168]{2,1,0:T(8,128)(2,1)} %dynamic-slice_bitcast_fusion), channel_id=1, source_target_pairs={{0,1},{1,0},{2,3},{3,2},{4,5},{5,4},{6,7},{7,6},{8,9},{9,8},{10,11... | collective-permute-start | bytes 16515080 | tf_op jit(solution)/shard_map/ppermute | solution.py:88
  48.4 6.9 %copy-start.1 = (s32[1,128,2]{1,2,0:T(2,128)S(1)}, s32[1,128,2]{1,2,0:T(2,128)}, u32[]{:S(2)}) copy-start(s32[1,128,2]{1,2,0:T(2,128)} %param.9) | copy-start | bytes 3076
  48.4 6.9 %copy-start.2 = (s32[1,128,2]{1,2,0:T(2,128)S(1)}, s32[1,128,2]{1,2,0:T(2,128)}, u32[]{:S(2)}) copy-start(s32[1,128,2]{1,2,0:T(2,128)} %param.7) | copy-start | bytes 3076
  48.4 69.6 %all-to-all-start = ((bf16[8,48,7168]{2,1,0:T(8,128)(2,1)}), bf16[8,48,7168]{2,1,0:T(8,128)(2,1)}, u32[]{:S(2)}, u32[]{:S(2)}) async-start(bf16[8,48,7168]{2,1,0:T(8,128)(2,1)} %fusion.10), calls=%async_computation | async-start | bytes 11010048 | tf_op jit(solution)/shard_map/all_to_all | solution.py:92
  55.4 62.5 %collective-permute-start.1 = (bf16[128,7168]{1,0:T(8,128)(2,1)}, bf16[128,7168]{1,0:T(8,128)(2,1)S(1)}, u32[]{:S(2)}, u32[]{:S(2)}) collective-permute-start(bf16[128,7168]{1,0:T(8,128)(2,1)} %bitcast.74), channel_id=1, source_target_pairs={{0,18},{2,16},{16,34},{18,32},{32,50},{34,48},{48,66},{50,64},{64,... | collective-permute-start | bytes 5505032 | tf_op jit(solution)/shard_map/ppermute | solution.py:73
  55.4 60.3 %collective-permute-start = (s32[128,4]{0,1:T(4,128)S(1)}, s32[128,4]{0,1:T(4,128)S(1)}, u32[]{:S(2)}, u32[]{:S(2)}) collective-permute-start(s32[128,4]{0,1:T(4,128)S(1)} %pad_add_fusion), channel_id=1, source_target_pairs={{0,2},{2,0},{1,3},{3,1},{4,6},{6,4},{5,7},{7,5},{8,10},{10,8},{9,1... | collective-permute-start | bytes 6152 | tf_op jit(solution)/shard_map/ppermute | solution.py:23
  187.1 9.4 %collective-permute-start.3 = (bf16[8,48,7168]{2,1,0:T(8,128)(2,1)}, bf16[8,48,7168]{2,1,0:T(8,128)(2,1)}, u32[]{:S(2)}, u32[]{:S(2)}) collective-permute-start(bf16[8,48,7168]{2,1,0:T(8,128)(2,1)} %all_to_all.10), channel_id=1, source_target_pairs={{0,1},{1,0},{2,3},{3,2},{4,5},{5,4},{6,7},{7,6},{8,9},{9,8},{10,11... | collective-permute-start | bytes 16515080 | tf_op jit(solution)/shard_map/ppermute | solution.py:101
  196.5 45.5 %collective-permute-start.4 = (bf16[128,7168]{1,0:T(8,128)(2,1)S(1)}, bf16[128,7168]{1,0:T(8,128)(2,1)}, u32[]{:S(2)}, u32[]{:S(2)}) collective-permute-start(bf16[128,7168]{1,0:T(8,128)(2,1)S(1)} %fusion.11), channel_id=1, source_target_pairs={{0,114},{2,112},{16,2},{18,0},{32,18},{34,16},{48,34},{50,32},{64,... | collective-permute-start | bytes 5505032 | tf_op jit(solution)/shard_map/ppermute | solution.py:107

commit v10 on v8

--- a/solution.py
+++ b/solution.py
@@ -76,13 +76,15 @@
         upstream = jnp.take(grad_hidden[0, 0], order, axis=0)
         saved = jnp.take(saved_pre[0, 0], order, axis=0)
         grad_pre = swiglu_backward(upstream, saved).reshape(2, chips, capacity, 2 * hid_units)
-        partial_rows = jnp.einsum(
-            "kech,dh->kecd", grad_pre, weights, preferred_element_type=jnp.float32
-        ).astype(jnp.bfloat16)
-        other_part = lax.ppermute(partial_rows[1], "core", [(0, 1), (1, 0)])
-        pair_sum = (partial_rows[0].astype(jnp.float32) + other_part.astype(jnp.float32)).astype(
-            jnp.bfloat16
-        )
+        width = model_width // 2
+        sums = []
+        for cols in (weights[:width], weights[width:]):
+            part = jnp.einsum(
+                "kech,dh->kecd", grad_pre, cols, preferred_element_type=jnp.float32
+            ).astype(jnp.bfloat16)
+            other = lax.ppermute(part[1], "core", [(0, 1), (1, 0)])
+            sums.append(part[0].astype(jnp.float32) + other.astype(jnp.float32))
+        pair_sum = jnp.concatenate(sums, axis=-1).astype(jnp.bfloat16)
         returned = lax.all_to_all(pair_sum, CHIPS, split_axis=0, concat_axis=0, tiled=True)
         rows, returned = lax.optimization_barrier((rows, returned))
 

time: 244 us -> 234 us (0.959)
  waiting for transfers between devices: 95.1 us -> 90.1 us
  local copies, waits for them, and re-layouts: 10.9 us -> 8.17 us
  other arithmetic: 16 us -> 13.4 us
    convert_element_type x1 -> x0, other arithmetic: 7.22 us -> none  [shards(): (partial_rows[0].astype(jnp.float32) + other_part.astype(jnp.float32)).as...]
    ppermute x1 -> x2, waiting for transfers between devices: 9.15 us -> 4.04 us  [shards(): other = lax.ppermute(part[1], 'core', [(0, 1), (1, 0)])]
    concatenate x0 -> x1, other arithmetic: none -> 3.23 us  [shards(): pair_sum = jnp.concatenate(sums, axis=-1).astype(jnp.bfloat16)]
    squeeze x1 -> x2, local copies, waits for them, and re-layouts: 3.07 us -> 0.39 us  [shards(): other = lax.ppermute(part[1], 'core', [(0, 1), (1, 0)])]
    another operation x7 -> x9, other arithmetic: 4.18 us -> 5.6 us
    dot_general x1 -> x2, matrix products: 19.1 us -> 18.4 us  [shards(): jnp.einsum('kech,dh->kecd', grad_pre, cols, preferred_element_type=jnp.fl...]
  transfers between devices with their start and end apart: 6 -> 7, of which waited for: 5 -> 5; matrix products, arithmetic and copies ran while one was open for 12% -> 17% of each run, Pallas kernels for 0% -> 0%
where the time goes in v10:
time: 234 us; the launch traced here: 233 us
  waiting for transfers between devices  90.1 us (39%)
  blocking collectives  67.7 us (29%)
  matrix products  43.1 us (18%)
  other arithmetic  13.4 us (6%)
  starting transfers between devices  9.86 us (4%)
  local copies, waits for them, and re-layouts  8.17 us (3%)
    all_to_all x1, blocking collectives, shards(): lax.all_to_all(picked, CHIPS, split_axis=0, concat_axis=0, tiled=True)  67.7 us
    ppermute x1, waiting for transfers between devices, swap_ylo(): return lax.ppermute(block, 'ylo', [(0, 1), (1, 0)])  59.2 us
    ppermute x1, waiting for transfers between devices, shards(): grad_rows = lax.ppermute(grad_in, RING, ring_route(sections, -1))  24.4 us
    dot_general x2, matrix products, shards(): jnp.einsum('kech,dh->kecd', grad_pre, cols, preferred_element_type=jnp.fl...  18.4 us
    dot_general x1, matrix products, shards(): jnp.einsum('scd,dh->sch', jnp.concatenate([arrived, partner]), weights, p...  18.2 us
    all_to_all x1, starting transfers between devices, shards(): lax.all_to_all(pair_sum, CHIPS, split_axis=0, concat_axis=0, tiled=True)  6.92 us
    another operation x9, other arithmetic  5.6 us
    dot_general x1, matrix products, shards(): jnp.einsum('ect,ecd->td', bwd_table, returned, preferred_element_type=jnp...  4.95 us
  transfers between devices with their start and end apart: 7, of which 5 were waited for; matrix products, arithmetic and copies ran while one was open for 17% of the time, Pallas kernels for 0%

profile of v10, /device:TPU:30, one launch (start us, length us, event | category | flops | bytes accessed | tf_op | source)
XLA Modules:
  0.0 233.3 jit_solution(13983078993192492278)
XLA Ops:
  0.9 1.2 copy-done
  2.0 0.6 gather_fusion
  2.7 1.9 select_convert_fusion
  4.7 0.6 gather_fusion.1
  5.3 2.7 %fusion.23 = (bf16[16,48,512]{2,1,0:T(8,128)(2,1)S(1)}, bf16[16,48,512]{2,1,0:T(8,128)(2,1)S(1)}) fusion(f32[16,48,1024]{2,1,0:T(8,128)} %select_convert_fusion, bf16[16,48,512]{2,1,0:T(8,128)(2,1)S(1)} %gather_fusion.1, pred[16]{0:T(512)(128)(4,1)S(1)} %get-tuple-element.15), kind=kLoop, calls=%fused_computation.33 | loop fusion | flops 5898240 | bytes 5505040 | tf_op jit(solution)/shard_map/convert.9
  8.0 9.2 %fusion.15 = bf16[2,8,48,3584]{3,2,1,0:T(8,128)(2,1)S(1)} fusion(bf16[1,1,7168,1024]{3,2,1,0:T(8,128)(2,1)} %param.10, bf16[2,8,48,512]{3,2,1,0:T(8,128)(2,1)S(1)} %bitcast.83, bf16[2,8,48,512]{3,2,1,0:T(8,128)(2,1)S(1)} %bitcast.81), kind=kOutput, calls=%fused_computation.18 | convolution fusion | flops 5643042816 | bytes 14417920 | tf_op jit(solution)/shard_map/kech,dh->kecd/dot_general | solution.py:82
  17.5 9.2 %fusion.12 = bf16[2,8,48,3584]{3,2,1,0:T(8,128)(2,1)S(1)} fusion(bf16[1,1,7168,1024]{3,2,1,0:T(8,128)(2,1)} %param.10, bf16[2,8,48,512]{3,2,1,0:T(8,128)(2,1)S(1)} %bitcast.84, bf16[2,8,48,512]{3,2,1,0:T(8,128)(2,1)S(1)} %bitcast.82), kind=kOutput, calls=%fused_computation.17 | convolution fusion | flops 5643042816 | bytes 14417920 | tf_op jit(solution)/shard_map/kech,dh->kecd/dot_general | solution.py:82
  26.9 0.6 collective-permute-start.2
  27.5 0.7 fusion.18
  28.1 4.0 %collective-permute-done.2 = bf16[8,48,3584]{2,1,0:T(8,128)(2,1)S(1)} collective-permute-done((bf16[8,48,3584]{2,1,0:T(8,128)(2,1)S(1)}, bf16[8,48,3584]{2,1,0:T(8,128)(2,1)S(1)}, u32[]{:S(2)}, u32[]{:S(2)}) %collective-permute-start.2) | collective-permute-done | bytes 2752544 | tf_op jit(solution)/shard_map/ppermute | solution.py:85
  32.2 0.7 fusion.19
  32.9 3.2 %pad_maximum_fusion = bf16[8,48,7168]{2,1,0:T(8,128)(2,1)} fusion(bf16[8,48,3584]{2,1,0:T(8,128)(2,1)S(1)} %fusion.18, bf16[8,48,3584]{2,1,0:T(8,128)(2,1)S(1)} %fusion.19), kind=kLoop, calls=%fused_computation.19 | loop fusion | flops 11010048 | bytes 11010048 | tf_op jit(solution)/shard_map/concatenate | solution.py:87
  36.2 6.9 %all-to-all-start = ((bf16[8,48,7168]{2,1,0:T(8,128)(2,1)}), bf16[8,48,7168]{2,1,0:T(8,128)(2,1)}, u32[]{:S(2)}, u32[]{:S(2)}) async-start(bf16[8,48,7168]{2,1,0:T(8,128)(2,1)} %pad_maximum_fusion), calls=%async_computation | async-start | bytes 11010048 | tf_op jit(solution)/shard_map/all_to_all | solution.py:88
  43.1 1.4 collective-permute-start
  44.5 59.2 %collective-permute-done = s32[128,4]{0,1:T(4,128)S(1)} collective-permute-done((s32[128,4]{0,1:T(4,128)S(1)}, s32[128,4]{0,1:T(4,128)S(1)}, u32[]{:S(2)}, u32[]{:S(2)}) %collective-permute-start) | collective-permute-done | bytes 2080 | tf_op jit(solution)/shard_map/ppermute | solution.py:23
  104.1 0.6 reduce-window.14
  104.7 0.2 slice_reduce_fusion.1
  105.3 0.3 bitcast_reduce_fusion.1
  106.0 1.6 convolution_convert_fusion
  107.6 67.7 %all_to_all.10 = bf16[8,48,7168]{2,1,0:T(8,128)(2,1)} all-to-all(bf16[8,48,7168]{2,1,0:T(8,128)(2,1)S(1)} %convolution_convert_fusion), channel_id=1, replica_groups=mesh['x'=4,'yhi'=2,'z'=4,'ylo'=2,'core'=2] {'z','ylo'}, dimensions={0} | all-to-all | bytes 11010048 | tf_op jit(solution)/shard_map/all_to_all | solution.py:95
  175.8 0.6 reduce-window.16
  176.4 0.2 slice_reduce_fusion
  177.0 0.3 bitcast_reduce_fusion
  177.5 4.9 %fusion.5 = bf16[128,7168]{1,0:T(8,128)(2,1)} fusion(bf16[8,48,7168]{2,1,0:T(8,128)(2,1)} %all-to-all-done, bf16[128,8,48]{0,2,1:T(8,128)(2,1)S(1)} %copy.31), kind=kOutput, calls=%fused_computation.10 | convolution fusion | flops 705560576 | bytes 7438336 | tf_op jit(solution)/shard_map/ect,ecd->td/dot_general | solution.py:99
  182.5 2.2 collective-permute-done.4
  184.7 0.9 collective-permute-start.5
  185.7 18.2 %fusion = f32[16,48,1024]{2,1,0:T(8,128)S(1)} fusion(bf16[1,1,7168,1024]{3,2,1,0:T(8,128)(2,1)} %param.10, bf16[8,48,7168]{2,1,0:T(8,128)(2,1)} %collective-permute-done.4, bf16[8,48,7168]{2,1,0:T(8,128)(2,1)} %all_to_all.10), kind=kOutput, calls=%fused_computation.3 | convolution fusion | flops 11279794176 | bytes 28835840 | tf_op jit(solution)/shard_map/scd,dh->sch/dot_general | solution.py:105
  203.8 0.5 fusion.26
  204.4 0.6 gather_fusion.2
  205.0 1.0 broadcast_select_fusion
  206.0 24.4 %collective-permute-done.5 = bf16[128,7168]{1,0:T(8,128)(2,1)} collective-permute-done((bf16[128,7168]{1,0:T(8,128)(2,1)}, bf16[128,7168]{1,0:T(8,128)(2,1)}, u32[]{:S(2)}, u32[]{:S(2)}) %collective-permute-start.5) | collective-permute-done | bytes 1835040 | tf_op jit(solution)/shard_map/ppermute | solution.py:103
  230.4 2.8 %copy.33 = bf16[1,128,7168]{2,1,0:T(8,128)(2,1)} copy(bf16[1,128,7168]{2,1,0:T(8,128)(2,1)} %bitcast.33) | data formatting | bytes 3670016
  (50 shorter events, 2.9 us)
Async XLA Ops:
  0.6 1.4 copy-start
  2.7 2.0 copy-start.2
  17.4 10.1 %collective-permute-start.3 = (bf16[8,48,3584]{2,1,0:T(8,128)(2,1)S(1)}, bf16[8,48,3584]{2,1,0:T(8,128)(2,1)S(1)}, u32[]{:S(2)}, u32[]{:S(2)}) collective-permute-start(bf16[8,48,3584]{2,1,0:T(8,128)(2,1)S(1)} %slice_bitcast_fusion), channel_id=1, source_target_pairs={{0,1},{1,0},{2,3},{3,2},{4,5},{5,4},{6,7},{7,6},{8,9},{9,8},{10,11... | collective-permute-start | bytes 8257544 | tf_op jit(solution)/shard_map/ppermute | solution.py:85
  26.9 5.3 %collective-permute-start.2 = (bf16[8,48,3584]{2,1,0:T(8,128)(2,1)S(1)}, bf16[8,48,3584]{2,1,0:T(8,128)(2,1)S(1)}, u32[]{:S(2)}, u32[]{:S(2)}) collective-permute-start(bf16[8,48,3584]{2,1,0:T(8,128)(2,1)S(1)} %slice_bitcast_fusion.2), channel_id=1, source_target_pairs={{0,1},{1,0},{2,3},{3,2},{4,5},{5,4},{6,7},{7,6},{8,9},{9,8},{10,11... | collective-permute-start | bytes 8257544 | tf_op jit(solution)/shard_map/ppermute | solution.py:85
  36.2 6.9 %copy-start.3 = (s32[1,128,2]{1,2,0:T(2,128)S(1)}, s32[1,128,2]{1,2,0:T(2,128)}, u32[]{:S(2)}) copy-start(s32[1,128,2]{1,2,0:T(2,128)} %param.11) | copy-start | bytes 3076
  36.2 6.9 %copy-start.4 = (s32[1,128,2]{1,2,0:T(2,128)S(1)}, s32[1,128,2]{1,2,0:T(2,128)}, u32[]{:S(2)}) copy-start(s32[1,128,2]{1,2,0:T(2,128)} %param.9) | copy-start | bytes 3076
  36.2 69.8 %all-to-all-start = ((bf16[8,48,7168]{2,1,0:T(8,128)(2,1)}), bf16[8,48,7168]{2,1,0:T(8,128)(2,1)}, u32[]{:S(2)}, u32[]{:S(2)}) async-start(bf16[8,48,7168]{2,1,0:T(8,128)(2,1)} %pad_maximum_fusion), calls=%async_computation | async-start | bytes 11010048 | tf_op jit(solution)/shard_map/all_to_all | solution.py:88
  43.1 62.7 %collective-permute-start.1 = (bf16[128,7168]{1,0:T(8,128)(2,1)}, bf16[128,7168]{1,0:T(8,128)(2,1)S(1)}, u32[]{:S(2)}, u32[]{:S(2)}) collective-permute-start(bf16[128,7168]{1,0:T(8,128)(2,1)} %bitcast.87), channel_id=1, source_target_pairs={{0,18},{2,16},{16,34},{18,32},{32,50},{34,48},{48,66},{50,64},{64,... | collective-permute-start | bytes 5505032 | tf_op jit(solution)/shard_map/ppermute | solution.py:73
  43.1 60.5 %collective-permute-start = (s32[128,4]{0,1:T(4,128)S(1)}, s32[128,4]{0,1:T(4,128)S(1)}, u32[]{:S(2)}, u32[]{:S(2)}) collective-permute-start(s32[128,4]{0,1:T(4,128)S(1)} %pad_add_fusion), channel_id=1, source_target_pairs={{0,2},{2,0},{1,3},{3,1},{4,6},{6,4},{5,7},{7,5},{8,10},{10,8},{9,1... | collective-permute-start | bytes 6152 | tf_op jit(solution)/shard_map/ppermute | solution.py:23
  175.3 9.4 %collective-permute-start.4 = (bf16[8,48,7168]{2,1,0:T(8,128)(2,1)}, bf16[8,48,7168]{2,1,0:T(8,128)(2,1)}, u32[]{:S(2)}, u32[]{:S(2)}) collective-permute-start(bf16[8,48,7168]{2,1,0:T(8,128)(2,1)} %all_to_all.10), channel_id=1, source_target_pairs={{0,1},{1,0},{2,3},{3,2},{4,5},{5,4},{6,7},{7,6},{8,9},{9,8},{10,11... | collective-permute-start | bytes 16515080 | tf_op jit(solution)/shard_map/ppermute | solution.py:97
  184.7 45.7 %collective-permute-start.5 = (bf16[128,7168]{1,0:T(8,128)(2,1)}, bf16[128,7168]{1,0:T(8,128)(2,1)}, u32[]{:S(2)}, u32[]{:S(2)}) collective-permute-start(bf16[128,7168]{1,0:T(8,128)(2,1)} %fusion.5), channel_id=1, source_target_pairs={{0,114},{2,112},{16,2},{18,0},{32,18},{34,16},{48,34},{50,32},{64,... | collective-permute-start | bytes 5505032 | tf_op jit(solution)/shard_map/ppermute | solution.py:103
  204.3 28.9 %copy-start.1 = (bf16[1,1,16,48,1024]{4,3,2,1,0:T(8,128)(2,1)S(1)}, bf16[1,1,16,48,1024]{4,3,2,1,0:T(8,128)(2,1)}, u32[]{:S(2)}) copy-start(bf16[1,1,16,48,1024]{4,3,2,1,0:T(8,128)(2,1)} %param.13) | copy-start | bytes 4718596

commit v11 on v10

--- a/solution.py
+++ b/solution.py
@@ -76,9 +76,9 @@
         upstream = jnp.take(grad_hidden[0, 0], order, axis=0)
         saved = jnp.take(saved_pre[0, 0], order, axis=0)
         grad_pre = swiglu_backward(upstream, saved).reshape(2, chips, capacity, 2 * hid_units)
-        width = model_width // 2
+        width = model_width // 4
         sums = []
-        for cols in (weights[:width], weights[width:]):
+        for cols in [weights[i * width : (i + 1) * width] for i in range(4)]:
             part = jnp.einsum(
                 "kech,dh->kecd", grad_pre, cols, preferred_element_type=jnp.float32
             ).astype(jnp.bfloat16)

time: 234 us -> 235 us (level)
  matrix products: 43.1 us -> 46 us
    dot_general x2 -> x4, matrix products: 18.4 us -> 21.3 us  [shards(): jnp.einsum('kech,dh->kecd', grad_pre, cols, preferred_element_type=jnp.fl...]
    another operation x9 -> x11, other arithmetic: 5.6 us -> 5.47 us
  transfers between devices with their start and end apart: 7 -> 9, of which waited for: 5 -> 5; matrix products, arithmetic and copies ran while one was open for 17% -> 20% of each run, Pallas kernels for 0% -> 0%
where the time goes in v11:
time: 235 us; the launch traced here: 234 us
  waiting for transfers between devices  87.8 us (37%)
  blocking collectives  67.7 us (29%)
  matrix products  46 us (20%)
  other arithmetic  13 us (6%)
  starting transfers between devices  10.5 us (4%)
  local copies, waits for them, and re-layouts  8.14 us (3%)
    all_to_all x1, blocking collectives, shards(): lax.all_to_all(picked, CHIPS, split_axis=0, concat_axis=0, tiled=True)  67.7 us
    ppermute x1, waiting for transfers between devices, swap_ylo(): return lax.ppermute(block, 'ylo', [(0, 1), (1, 0)])  59.2 us
    ppermute x1, waiting for transfers between devices, shards(): grad_rows = lax.ppermute(grad_in, RING, ring_route(sections, -1))  24.4 us
    dot_general x4, matrix products, shards(): jnp.einsum('kech,dh->kecd', grad_pre, cols, preferred_element_type=jnp.fl...  21.3 us
    dot_general x1, matrix products, shards(): jnp.einsum('scd,dh->sch', jnp.concatenate([arrived, partner]), weights, p...  18.2 us
    all_to_all x1, starting transfers between devices, shards(): lax.all_to_all(pair_sum, CHIPS, split_axis=0, concat_axis=0, tiled=True)  6.92 us
    another operation x11, other arithmetic  5.47 us
    dot_general x1, matrix products, shards(): jnp.einsum('ect,ecd->td', bwd_table, returned, preferred_element_type=jnp...  4.95 us
  transfers between devices with their start and end apart: 9, of which 5 were waited for; matrix products, arithmetic and copies ran while one was open for 20% of the time, Pallas kernels for 0%

profile of v11, /device:TPU:30, one launch (start us, length us, event | category | flops | bytes accessed | tf_op | source)
XLA Modules:
  0.0 234.1 jit_solution(1486431889359602502)
XLA Ops:
  0.9 1.2 copy-done
  2.0 0.6 gather_fusion
  2.7 1.9 select_convert_fusion
  4.7 0.6 gather_fusion.1
  5.3 2.7 %fusion.37 = (bf16[16,48,512]{2,1,0:T(8,128)(2,1)S(1)}, bf16[16,48,512]{2,1,0:T(8,128)(2,1)S(1)}) fusion(f32[16,48,1024]{2,1,0:T(8,128)} %select_convert_fusion, bf16[16,48,512]{2,1,0:T(8,128)(2,1)S(1)} %gather_fusion.1, pred[16]{0:T(512)(128)(4,1)S(1)} %get-tuple-element.15), kind=kLoop, calls=%fused_computation.41 | loop fusion | flops 5898240 | bytes 5505040 | tf_op jit(solution)/shard_map/convert.13
  8.0 5.3 %fusion.27 = bf16[2,8,48,1792]{3,2,1,0:T(8,128)(2,1)S(1)} fusion(bf16[1,1,7168,1024]{3,2,1,0:T(8,128)(2,1)} %param.10, bf16[2,8,48,512]{3,2,1,0:T(8,128)(2,1)S(1)} %bitcast.117, bf16[2,8,48,512]{3,2,1,0:T(8,128)(2,1)S(1)} %bitcast.113), kind=kOutput, calls=%fused_computation.27 | convolution fusion | flops 2823094272 | bytes 7995392 | tf_op jit(solution)/shard_map/kech,dh->kecd/dot_general | solution.py:82
  13.5 5.3 %fusion.24 = bf16[2,8,48,1792]{3,2,1,0:T(8,128)(2,1)S(1)} fusion(bf16[1,1,7168,1024]{3,2,1,0:T(8,128)(2,1)} %param.10, bf16[2,8,48,512]{3,2,1,0:T(8,128)(2,1)S(1)} %bitcast.118, bf16[2,8,48,512]{3,2,1,0:T(8,128)(2,1)S(1)} %bitcast.114), kind=kOutput, calls=%fused_computation.26 | convolution fusion | flops 2823094272 | bytes 7995392 | tf_op jit(solution)/shard_map/kech,dh->kecd/dot_general | solution.py:82
  18.9 0.6 collective-permute-start.4
  19.5 5.3 %fusion.21 = bf16[2,8,48,1792]{3,2,1,0:T(8,128)(2,1)S(1)} fusion(bf16[1,1,7168,1024]{3,2,1,0:T(8,128)(2,1)} %param.10, bf16[2,8,48,512]{3,2,1,0:T(8,128)(2,1)S(1)} %bitcast.119, bf16[2,8,48,512]{3,2,1,0:T(8,128)(2,1)S(1)} %bitcast.115), kind=kOutput, calls=%fused_computation.25 | convolution fusion | flops 2823094272 | bytes 7995392 | tf_op jit(solution)/shard_map/kech,dh->kecd/dot_general | solution.py:82
  25.0 5.3 %fusion.18 = bf16[2,8,48,1792]{3,2,1,0:T(8,128)(2,1)S(1)} fusion(bf16[1,1,7168,1024]{3,2,1,0:T(8,128)(2,1)} %param.10, bf16[2,8,48,512]{3,2,1,0:T(8,128)(2,1)S(1)} %bitcast.120, bf16[2,8,48,512]{3,2,1,0:T(8,128)(2,1)S(1)} %bitcast.116), kind=kOutput, calls=%fused_computation.24 | convolution fusion | flops 2823094272 | bytes 7995392 | tf_op jit(solution)/shard_map/kech,dh->kecd/dot_general | solution.py:82
  30.4 0.6 collective-permute-start.2
  32.0 1.8 collective-permute-done.2
  33.7 0.3 fusion.33
  34.1 3.0 %pad_maximum_fusion = bf16[8,48,7168]{2,1,0:T(8,128)(2,1)} fusion(bf16[8,48,1792]{2,1,0:T(8,128)(2,1)S(1)} %fusion.30, bf16[8,48,1792]{2,1,0:T(8,128)(2,1)S(1)} %fusion.31, bf16[8,48,1792]{2,1,0:T(8,128)(2,1)S(1)} %fusion.32, bf16[8,48,1792]{2,1,0:T(8,128)(2,1)S(1)} %fusion.33), kind=kLoop, calls=%fused_computation.11 | loop fusion | flops 22020096 | bytes 11010048 | tf_op jit(solution)/shard_map/concatenate | solution.py:87
  37.0 6.9 %all-to-all-start = ((bf16[8,48,7168]{2,1,0:T(8,128)(2,1)}), bf16[8,48,7168]{2,1,0:T(8,128)(2,1)}, u32[]{:S(2)}, u32[]{:S(2)}) async-start(bf16[8,48,7168]{2,1,0:T(8,128)(2,1)} %pad_maximum_fusion), calls=%async_computation | async-start | bytes 11010048 | tf_op jit(solution)/shard_map/all_to_all | solution.py:88
  44.0 1.4 collective-permute-start
  45.3 59.2 %collective-permute-done = s32[128,4]{0,1:T(4,128)S(1)} collective-permute-done((s32[128,4]{0,1:T(4,128)S(1)}, s32[128,4]{0,1:T(4,128)S(1)}, u32[]{:S(2)}, u32[]{:S(2)}) %collective-permute-start) | collective-permute-done | bytes 2080 | tf_op jit(solution)/shard_map/ppermute | solution.py:23
  105.0 0.6 reduce-window.14
  106.1 0.3 bitcast_reduce_fusion.1
  106.9 1.6 convolution_convert_fusion
  108.5 67.7 %all_to_all.10 = bf16[8,48,7168]{2,1,0:T(8,128)(2,1)} all-to-all(bf16[8,48,7168]{2,1,0:T(8,128)(2,1)S(1)} %convolution_convert_fusion), channel_id=1, replica_groups=mesh['x'=4,'yhi'=2,'z'=4,'ylo'=2,'core'=2] {'z','ylo'}, dimensions={0} | all-to-all | bytes 11010048 | tf_op jit(solution)/shard_map/all_to_all | solution.py:95
  176.7 0.6 reduce-window.16
  177.9 0.3 bitcast_reduce_fusion
  178.4 4.9 %fusion.5 = bf16[128,7168]{1,0:T(8,128)(2,1)} fusion(bf16[8,48,7168]{2,1,0:T(8,128)(2,1)} %all-to-all-done, bf16[128,8,48]{0,2,1:T(8,128)(2,1)S(1)} %copy.33), kind=kOutput, calls=%fused_computation.10 | convolution fusion | flops 705560576 | bytes 7438336 | tf_op jit(solution)/shard_map/ect,ecd->td/dot_general | solution.py:99
  183.3 2.2 collective-permute-done.6
  185.6 0.9 collective-permute-start.7
  186.5 18.2 %fusion = f32[16,48,1024]{2,1,0:T(8,128)S(1)} fusion(bf16[1,1,7168,1024]{3,2,1,0:T(8,128)(2,1)} %param.10, bf16[8,48,7168]{2,1,0:T(8,128)(2,1)} %collective-permute-done.6, bf16[8,48,7168]{2,1,0:T(8,128)(2,1)} %all_to_all.10), kind=kOutput, calls=%fused_computation.3 | convolution fusion | flops 11279794176 | bytes 28835840 | tf_op jit(solution)/shard_map/scd,dh->sch/dot_general | solution.py:105
  204.7 0.5 fusion.40
  205.2 0.6 gather_fusion.2
  205.8 1.0 broadcast_select_fusion
  206.9 24.4 %collective-permute-done.7 = bf16[128,7168]{1,0:T(8,128)(2,1)} collective-permute-done((bf16[128,7168]{1,0:T(8,128)(2,1)}, bf16[128,7168]{1,0:T(8,128)(2,1)}, u32[]{:S(2)}, u32[]{:S(2)}) %collective-permute-start.7) | collective-permute-done | bytes 1835040 | tf_op jit(solution)/shard_map/ppermute | solution.py:103
  231.3 2.8 %copy.35 = bf16[1,128,7168]{2,1,0:T(8,128)(2,1)} copy(bf16[1,128,7168]{2,1,0:T(8,128)(2,1)} %bitcast.43) | data formatting | bytes 3670016
  (60 shorter events, 4.3 us)
Async XLA Ops:
  0.6 1.4 copy-start
  2.7 2.0 copy-start.2
  13.4 17.6 %collective-permute-start.5 = (bf16[8,48,1792]{2,1,0:T(8,128)(2,1)S(1)}, bf16[8,48,1792]{2,1,0:T(8,128)(2,1)S(1)}, u32[]{:S(2)}, u32[]{:S(2)}) collective-permute-start(bf16[8,48,1792]{2,1,0:T(8,128)(2,1)S(1)} %slice_bitcast_fusion), channel_id=1, source_target_pairs={{0,1},{1,0},{2,3},{3,2},{4,5},{5,4},{6,7},{7,6},{8,9},{9,8},{10,11... | collective-permute-start | bytes 4128776 | tf_op jit(solution)/shard_map/ppermute | solution.py:85
  18.9 12.4 %collective-permute-start.4 = (bf16[8,48,1792]{2,1,0:T(8,128)(2,1)S(1)}, bf16[8,48,1792]{2,1,0:T(8,128)(2,1)S(1)}, u32[]{:S(2)}, u32[]{:S(2)}) collective-permute-start(bf16[8,48,1792]{2,1,0:T(8,128)(2,1)S(1)} %slice_bitcast_fusion.2), channel_id=1, source_target_pairs={{0,1},{1,0},{2,3},{3,2},{4,5},{5,4},{6,7},{7,6},{8,9},{9,8},{10,11... | collective-permute-start | bytes 4128776 | tf_op jit(solution)/shard_map/ppermute | solution.py:85
  24.9 6.7 %collective-permute-start.3 = (bf16[8,48,1792]{2,1,0:T(8,128)(2,1)S(1)}, bf16[8,48,1792]{2,1,0:T(8,128)(2,1)S(1)}, u32[]{:S(2)}, u32[]{:S(2)}) collective-permute-start(bf16[8,48,1792]{2,1,0:T(8,128)(2,1)S(1)} %slice_bitcast_fusion.4), channel_id=1, source_target_pairs={{0,1},{1,0},{2,3},{3,2},{4,5},{5,4},{6,7},{7,6},{8,9},{9,8},{10,11... | collective-permute-start | bytes 4128776 | tf_op jit(solution)/shard_map/ppermute | solution.py:85
  30.4 3.3 %collective-permute-start.2 = (bf16[8,48,1792]{2,1,0:T(8,128)(2,1)S(1)}, bf16[8,48,1792]{2,1,0:T(8,128)(2,1)S(1)}, u32[]{:S(2)}, u32[]{:S(2)}) collective-permute-start(bf16[8,48,1792]{2,1,0:T(8,128)(2,1)S(1)} %slice_bitcast_fusion.6), channel_id=1, source_target_pairs={{0,1},{1,0},{2,3},{3,2},{4,5},{5,4},{6,7},{7,6},{8,9},{9,8},{10,11... | collective-permute-start | bytes 4128776 | tf_op jit(solution)/shard_map/ppermute | solution.py:85
  37.0 6.9 %copy-start.3 = (s32[1,128,2]{1,2,0:T(2,128)S(1)}, s32[1,128,2]{1,2,0:T(2,128)}, u32[]{:S(2)}) copy-start(s32[1,128,2]{1,2,0:T(2,128)} %param.11) | copy-start | bytes 3076
  37.0 6.9 %copy-start.4 = (s32[1,128,2]{1,2,0:T(2,128)S(1)}, s32[1,128,2]{1,2,0:T(2,128)}, u32[]{:S(2)}) copy-start(s32[1,128,2]{1,2,0:T(2,128)} %param.9) | copy-start | bytes 3076
  37.0 69.8 %all-to-all-start = ((bf16[8,48,7168]{2,1,0:T(8,128)(2,1)}), bf16[8,48,7168]{2,1,0:T(8,128)(2,1)}, u32[]{:S(2)}, u32[]{:S(2)}) async-start(bf16[8,48,7168]{2,1,0:T(8,128)(2,1)} %pad_maximum_fusion), calls=%async_computation | async-start | bytes 11010048 | tf_op jit(solution)/shard_map/all_to_all | solution.py:88
  44.0 62.7 %collective-permute-start.1 = (bf16[128,7168]{1,0:T(8,128)(2,1)}, bf16[128,7168]{1,0:T(8,128)(2,1)S(1)}, u32[]{:S(2)}, u32[]{:S(2)}) collective-permute-start(bf16[128,7168]{1,0:T(8,128)(2,1)} %bitcast.123), channel_id=1, source_target_pairs={{0,18},{2,16},{16,34},{18,32},{32,50},{34,48},{48,66},{50,64},{64,... | collective-permute-start | bytes 5505032 | tf_op jit(solution)/shard_map/ppermute | solution.py:73
  44.0 60.5 %collective-permute-start = (s32[128,4]{0,1:T(4,128)S(1)}, s32[128,4]{0,1:T(4,128)S(1)}, u32[]{:S(2)}, u32[]{:S(2)}) collective-permute-start(s32[128,4]{0,1:T(4,128)S(1)} %pad_add_fusion), channel_id=1, source_target_pairs={{0,2},{2,0},{1,3},{3,1},{4,6},{6,4},{5,7},{7,5},{8,10},{10,8},{9,1... | collective-permute-start | bytes 6152 | tf_op jit(solution)/shard_map/ppermute | solution.py:23
  176.2 9.4 %collective-permute-start.6 = (bf16[8,48,7168]{2,1,0:T(8,128)(2,1)}, bf16[8,48,7168]{2,1,0:T(8,128)(2,1)}, u32[]{:S(2)}, u32[]{:S(2)}) collective-permute-start(bf16[8,48,7168]{2,1,0:T(8,128)(2,1)} %all_to_all.10), channel_id=1, source_target_pairs={{0,1},{1,0},{2,3},{3,2},{4,5},{5,4},{6,7},{7,6},{8,9},{9,8},{10,11... | collective-permute-start | bytes 16515080 | tf_op jit(solution)/shard_map/ppermute | solution.py:97
  185.6 45.7 %collective-permute-start.7 = (bf16[128,7168]{1,0:T(8,128)(2,1)}, bf16[128,7168]{1,0:T(8,128)(2,1)}, u32[]{:S(2)}, u32[]{:S(2)}) collective-permute-start(bf16[128,7168]{1,0:T(8,128)(2,1)} %fusion.5), channel_id=1, source_target_pairs={{0,114},{2,112},{16,2},{18,0},{32,18},{34,16},{48,34},{50,32},{64,... | collective-permute-start | bytes 5505032 | tf_op jit(solution)/shard_map/ppermute | solution.py:103
  205.2 28.9 %copy-start.1 = (bf16[1,1,16,48,1024]{4,3,2,1,0:T(8,128)(2,1)S(1)}, bf16[1,1,16,48,1024]{4,3,2,1,0:T(8,128)(2,1)}, u32[]{:S(2)}) copy-start(bf16[1,1,16,48,1024]{4,3,2,1,0:T(8,128)(2,1)} %param.13) | copy-start | bytes 4718596

commit v12 on v10

--- a/solution.py
+++ b/solution.py
@@ -94,19 +94,32 @@
         ).astype(jnp.bfloat16)
         arrived = lax.all_to_all(picked, CHIPS, split_axis=0, concat_axis=0, tiled=True)
 
-        partner = lax.ppermute(arrived, "core", [(0, 1), (1, 0)])
+        half = capacity // 2
+        partner_a = lax.ppermute(arrived[:, :half], "core", [(0, 1), (1, 0)])
+        partner_b = lax.ppermute(arrived[:, half:], "core", [(0, 1), (1, 0)])
         bwd_table = slot_table(bwd_ids, experts, capacity).astype(jnp.bfloat16)
         grad_in = jnp.einsum(
             "ect,ecd->td", bwd_table, returned, preferred_element_type=jnp.float32
         ).astype(jnp.bfloat16)
-        grad_in, partner = lax.optimization_barrier((grad_in, partner))
+        grad_in, partner_a = lax.optimization_barrier((grad_in, partner_a))
         grad_rows = lax.ppermute(grad_in, RING, ring_route(sections, -1))
 
-        projected = jnp.einsum(
-            "scd,dh->sch",
-            jnp.concatenate([arrived, partner]),
-            weights,
-            preferred_element_type=jnp.float32,
+        projected = jnp.concatenate(
+            [
+                jnp.einsum(
+                    "scd,dh->sch",
+                    jnp.concatenate([arrived[:, :half], partner_a]),
+                    weights,
+                    preferred_element_type=jnp.float32,
+                ),
+                jnp.einsum(
+                    "scd,dh->sch",
+                    jnp.concatenate([arrived[:, half:], partner_b]),
+                    weights,
+                    preferred_element_type=jnp.float32,
+                ),
+            ],
+            axis=1,
         )
         hidden = (jax.nn.silu(projected[..., :hid_units]) * projected[..., hid_units:]).astype(
             jnp.bfloat16

time: 234 us -> 233 us (level)
  local copies, waits for them, and re-layouts: 8.17 us -> 12.8 us
  other arithmetic: 13.4 us -> 9.88 us
  waiting for transfers between devices: 90.1 us -> 86.7 us
    slice x1 -> x2, local copies, waits for them, and re-layouts: 0.21 us -> 3.06 us  [the longest x1 2.85 us: shards(): arrived[:, :half]]
    dot_general x1 -> x2, matrix products: 18.2 us -> 19.2 us  [the longest x1 11.3 us: shards(): jnp.einsum('scd,dh->sch', jnp.concatenate([arrived[:, :half], partner_a])...]
  transfers between devices with their start and end apart: 7 -> 8, of which waited for: 5 -> 4; matrix products, arithmetic and copies ran while one was open for 17% -> 17% of each run, Pallas kernels for 0% -> 0%
where the time goes in v12:
time: 233 us
  waiting for transfers between devices  86.7 us (37%)
  blocking collectives  67.6 us (29%)
  matrix products  44.3 us (19%)
  local copies, waits for them, and re-layouts  12.8 us (5%)
  starting transfers between devices  10.7 us (5%)
  other arithmetic  9.88 us (4%)
    all_to_all x1, blocking collectives, shards(): lax.all_to_all(picked, CHIPS, split_axis=0, concat_axis=0, tiled=True)  67.6 us
    ppermute x1, waiting for transfers between devices, swap_ylo(): return lax.ppermute(block, 'ylo', [(0, 1), (1, 0)])  59.2 us
    ppermute x1, waiting for transfers between devices, shards(): grad_rows = lax.ppermute(grad_in, RING, ring_route(sections, -1))  23.3 us
    dot_general x2, matrix products, shards(): jnp.einsum('kech,dh->kecd', grad_pre, cols, preferred_element_type=jnp.fl...  18.4 us
    dot_general x1, matrix products, shards(): jnp.einsum('scd,dh->sch', jnp.concatenate([arrived[:, :half], partner_a])...  11.3 us
    dot_general x1, matrix products, shards(): jnp.einsum('scd,dh->sch', jnp.concatenate([arrived[:, half:], partner_b])...  7.88 us
    all_to_all x1, starting transfers between devices, shards(): lax.all_to_all(pair_sum, CHIPS, split_axis=0, concat_axis=0, tiled=True)  6.91 us
    dot_general x1, matrix products, shards(): jnp.einsum('ect,ecd->td', bwd_table, returned, preferred_element_type=jnp...  5.1 us
  transfers between devices with their start and end apart: 8, of which 4 were waited for; matrix products, arithmetic and copies ran while one was open for 17% of the time, Pallas kernels for 0%

profile of v12, /device:TPU:30, one launch (start us, length us, event | category | flops | bytes accessed | tf_op | source)
XLA Modules:
  0.0 232.9 jit_solution(12587298475026735734)
XLA Ops:
  0.9 2.7 %gather_fusion.1 = bf16[16,48,512]{2,1,0:T(8,128)(2,1)} fusion(bf16[16,48,512]{2,1,0:T(8,128)(2,1)} %bitcast.81, s32[1024]{0:T(1024)S(1)} %pad_clamp_fusion.2), kind=kCustom, calls=%fused_computation.clone | custom fusion | bytes 1572928 | tf_op jit(solution)/shard_map/jit(_take)/gather | solution.py:76
  3.6 0.6 gather_fusion
  4.2 0.3 select_convert_fusion
  4.5 0.8 copy-done.2
  5.4 0.9 fusion.28
  6.3 9.2 %fusion.14 = bf16[2,8,48,3584]{3,2,1,0:T(8,128)(2,1)S(1)} fusion(bf16[1,1,7168,1024]{3,2,1,0:T(8,128)(2,1)} %param.10, bf16[2,8,48,512]{3,2,1,0:T(8,128)(2,1)S(1)} %bitcast.85, bf16[2,8,48,512]{3,2,1,0:T(8,128)(2,1)S(1)} %bitcast.83), kind=kOutput, calls=%fused_computation.17 | convolution fusion | flops 5643042816 | bytes 14417920 | tf_op jit(solution)/shard_map/kech,dh->kecd/dot_general | solution.py:82
  15.8 9.2 %fusion.11 = bf16[2,8,48,3584]{3,2,1,0:T(8,128)(2,1)S(1)} fusion(bf16[1,1,7168,1024]{3,2,1,0:T(8,128)(2,1)} %param.10, bf16[2,8,48,512]{3,2,1,0:T(8,128)(2,1)S(1)} %bitcast.86, bf16[2,8,48,512]{3,2,1,0:T(8,128)(2,1)S(1)} %bitcast.84), kind=kOutput, calls=%fused_computation.16 | convolution fusion | flops 5643042816 | bytes 14417920 | tf_op jit(solution)/shard_map/kech,dh->kecd/dot_general | solution.py:82
  25.2 0.6 collective-permute-start.2
  25.7 0.7 fusion.23
  26.4 4.0 %collective-permute-done.2 = bf16[8,48,3584]{2,1,0:T(8,128)(2,1)S(1)} collective-permute-done((bf16[8,48,3584]{2,1,0:T(8,128)(2,1)S(1)}, bf16[8,48,3584]{2,1,0:T(8,128)(2,1)S(1)}, u32[]{:S(2)}, u32[]{:S(2)}) %collective-permute-start.2) | collective-permute-done | bytes 2752544 | tf_op jit(solution)/shard_map/ppermute | solution.py:85
  30.5 0.7 fusion.24
  31.2 3.2 %pad_maximum_fusion = bf16[8,48,7168]{2,1,0:T(8,128)(2,1)} fusion(bf16[8,48,3584]{2,1,0:T(8,128)(2,1)S(1)} %fusion.23, bf16[8,48,3584]{2,1,0:T(8,128)(2,1)S(1)} %fusion.24), kind=kLoop, calls=%fused_computation.18 | loop fusion | flops 11010048 | bytes 11010048 | tf_op jit(solution)/shard_map/concatenate | solution.py:87
  34.4 6.9 %all-to-all-start = ((bf16[8,48,7168]{2,1,0:T(8,128)(2,1)}), bf16[8,48,7168]{2,1,0:T(8,128)(2,1)}, u32[]{:S(2)}, u32[]{:S(2)}) async-start(bf16[8,48,7168]{2,1,0:T(8,128)(2,1)} %pad_maximum_fusion), calls=%async_computation | async-start | bytes 11010048 | tf_op jit(solution)/shard_map/all_to_all | solution.py:88
  41.4 1.3 collective-permute-start
  42.7 59.2 %collective-permute-done = s32[128,4]{0,1:T(4,128)S(1)} collective-permute-done((s32[128,4]{0,1:T(4,128)S(1)}, s32[128,4]{0,1:T(4,128)S(1)}, u32[]{:S(2)}, u32[]{:S(2)}) %collective-permute-start) | collective-permute-done | bytes 2080 | tf_op jit(solution)/shard_map/ppermute | solution.py:23
  102.3 0.6 reduce-window.14
  103.5 0.3 bitcast_reduce_fusion.1
  104.3 1.6 convolution_convert_fusion
  105.9 67.6 %all_to_all.10 = bf16[8,48,7168]{2,1,0:T(8,128)(2,1)S(1)} all-to-all(bf16[8,48,7168]{2,1,0:T(8,128)(2,1)S(1)} %convolution_convert_fusion), channel_id=1, replica_groups=mesh['x'=4,'yhi'=2,'z'=4,'ylo'=2,'core'=2] {'z','ylo'}, dimensions={0} | all-to-all | bytes 11010048 | tf_op jit(solution)/shard_map/all_to_all | solution.py:95
  173.5 2.9 %fusion.61 = (bf16[8,24,7168]{2,1,0:T(8,128)(2,1)}, bf16[8,24,7168]{2,1,0:T(8,128)(2,1)}) fusion(bf16[8,48,7168]{2,1,0:T(8,128)(2,1)S(1)} %all_to_all.10), kind=kLoop, calls=%fused_computation.122 | loop fusion | bytes 11010048 | tf_op jit(solution)/shard_map/slice | solution.py:111
  176.8 0.6 collective-permute-start.5
  177.4 0.6 reduce-window.16
  178.6 0.3 bitcast_reduce_fusion
  179.1 5.1 %fusion.4 = bf16[128,7168]{1,0:T(8,128)(2,1)} fusion(bf16[8,48,7168]{2,1,0:T(8,128)(2,1)} %all-to-all-done, bf16[128,8,48]{0,2,1:T(8,128)(2,1)S(1)} %copy.31), kind=kOutput, calls=%fused_computation.9 | convolution fusion | flops 705560576 | bytes 7438336 | tf_op jit(solution)/shard_map/ect,ecd->td/dot_general | solution.py:101
  184.2 1.2 collective-permute-start.6
  185.5 11.3 %fusion.2 = f32[16,24,1024]{2,1,0:T(8,128)S(1)} fusion(bf16[1,1,7168,1024]{3,2,1,0:T(8,128)(2,1)} %param.10, bf16[8,24,7168]{2,1,0:T(8,128)(2,1)} %collective-permute-done.4, bf16[8,24,7168]{2,1,0:T(8,128)(2,1)} %get-tuple-element.17), kind=kOutput, calls=%fused_computation.5 | convolution fusion | flops 5639897088 | bytes 21757952 | tf_op jit(solution)/shard_map/scd,dh->sch/dot_general | solution.py:109
  196.8 7.9 %fusion = f32[16,24,1024]{2,1,0:T(8,128)S(1)} fusion(bf16[1,1,7168,1024]{3,2,1,0:T(8,128)(2,1)S(1)} %bitcast.90, bf16[8,24,7168]{2,1,0:T(8,128)(2,1)} %collective-permute-done.5, bf16[8,24,7168]{2,1,0:T(8,128)(2,1)S(1)} %copy-done.3), kind=kOutput, calls=%fused_computation.3 | convolution fusion | flops 5639897088 | bytes 21757952 | tf_op jit(solution)/shard_map/scd,dh->sch/dot_general | solution.py:115
  204.7 0.5 fusion.33
  205.2 0.6 gather_fusion.2
  205.8 1.0 broadcast_select_fusion
  206.8 23.3 %collective-permute-done.6 = bf16[128,7168]{1,0:T(8,128)(2,1)} collective-permute-done((bf16[128,7168]{1,0:T(8,128)(2,1)}, bf16[128,7168]{1,0:T(8,128)(2,1)}, u32[]{:S(2)}, u32[]{:S(2)}) %collective-permute-start.6) | collective-permute-done | bytes 1835040 | tf_op jit(solution)/shard_map/ppermute | solution.py:105
  230.1 2.8 %copy.33 = bf16[1,128,7168]{2,1,0:T(8,128)(2,1)} copy(bf16[1,128,7168]{2,1,0:T(8,128)(2,1)} %bitcast.34) | data formatting | bytes 3670016
  (65 shorter events, 3.3 us)
Async XLA Ops:
  0.6 2.9 %copy-start = (bf16[1,1,16,48,1024]{4,3,2,1,0:T(8,128)(2,1)S(1)}, bf16[1,1,16,48,1024]{4,3,2,1,0:T(8,128)(2,1)}, u32[]{:S(2)}) copy-start(bf16[1,1,16,48,1024]{4,3,2,1,0:T(8,128)(2,1)} %param.13) | copy-start | bytes 4718596
  4.2 1.1 copy-start.2
  15.7 10.1 %collective-permute-start.3 = (bf16[8,48,3584]{2,1,0:T(8,128)(2,1)S(1)}, bf16[8,48,3584]{2,1,0:T(8,128)(2,1)S(1)}, u32[]{:S(2)}, u32[]{:S(2)}) collective-permute-start(bf16[8,48,3584]{2,1,0:T(8,128)(2,1)S(1)} %slice_bitcast_fusion), channel_id=1, source_target_pairs={{0,1},{1,0},{2,3},{3,2},{4,5},{5,4},{6,7},{7,6},{8,9},{9,8},{10,11... | collective-permute-start | bytes 8257544 | tf_op jit(solution)/shard_map/ppermute | solution.py:85
  25.2 5.3 %collective-permute-start.2 = (bf16[8,48,3584]{2,1,0:T(8,128)(2,1)S(1)}, bf16[8,48,3584]{2,1,0:T(8,128)(2,1)S(1)}, u32[]{:S(2)}, u32[]{:S(2)}) collective-permute-start(bf16[8,48,3584]{2,1,0:T(8,128)(2,1)S(1)} %slice_bitcast_fusion.2), channel_id=1, source_target_pairs={{0,1},{1,0},{2,3},{3,2},{4,5},{5,4},{6,7},{7,6},{8,9},{9,8},{10,11... | collective-permute-start | bytes 8257544 | tf_op jit(solution)/shard_map/ppermute | solution.py:85
  34.4 6.9 %copy-start.4 = (s32[1,128,2]{1,2,0:T(2,128)S(1)}, s32[1,128,2]{1,2,0:T(2,128)}, u32[]{:S(2)}) copy-start(s32[1,128,2]{1,2,0:T(2,128)} %param.11) | copy-start | bytes 3076
  34.4 6.9 %copy-start.5 = (s32[1,128,2]{1,2,0:T(2,128)S(1)}, s32[1,128,2]{1,2,0:T(2,128)}, u32[]{:S(2)}) copy-start(s32[1,128,2]{1,2,0:T(2,128)} %param.9) | copy-start | bytes 3076
  34.4 69.8 %all-to-all-start = ((bf16[8,48,7168]{2,1,0:T(8,128)(2,1)}), bf16[8,48,7168]{2,1,0:T(8,128)(2,1)}, u32[]{:S(2)}, u32[]{:S(2)}) async-start(bf16[8,48,7168]{2,1,0:T(8,128)(2,1)} %pad_maximum_fusion), calls=%async_computation | async-start | bytes 11010048 | tf_op jit(solution)/shard_map/all_to_all | solution.py:88
  41.4 62.7 %collective-permute-start.1 = (bf16[128,7168]{1,0:T(8,128)(2,1)}, bf16[128,7168]{1,0:T(8,128)(2,1)S(1)}, u32[]{:S(2)}, u32[]{:S(2)}) collective-permute-start(bf16[128,7168]{1,0:T(8,128)(2,1)} %bitcast.91), channel_id=1, source_target_pairs={{0,18},{2,16},{16,34},{18,32},{32,50},{34,48},{48,66},{50,64},{64,... | collective-permute-start | bytes 5505032 | tf_op jit(solution)/shard_map/ppermute | solution.py:73
  41.4 60.5 %collective-permute-start = (s32[128,4]{0,1:T(4,128)S(1)}, s32[128,4]{0,1:T(4,128)S(1)}, u32[]{:S(2)}, u32[]{:S(2)}) collective-permute-start(s32[128,4]{0,1:T(4,128)S(1)} %pad_add_fusion), channel_id=1, source_target_pairs={{0,2},{2,0},{1,3},{3,1},{4,6},{6,4},{5,7},{7,5},{8,10},{10,8},{9,1... | collective-permute-start | bytes 6152 | tf_op jit(solution)/shard_map/ppermute | solution.py:23
  176.3 7.9 %collective-permute-start.4 = (bf16[8,24,7168]{2,1,0:T(8,128)(2,1)}, bf16[8,24,7168]{2,1,0:T(8,128)(2,1)}, u32[]{:S(2)}, u32[]{:S(2)}) collective-permute-start(bf16[8,24,7168]{2,1,0:T(8,128)(2,1)} %get-tuple-element.17), channel_id=1, source_target_pairs={{0,1},{1,0},{2,3},{3,2},{4,5},{5,4},{6,7},{7,6},{8,9},{9,8},{10,11... | collective-permute-start | bytes 8257544 | tf_op jit(solution)/shard_map/ppermute | solution.py:98
  176.8 20.0 %collective-permute-start.5 = (bf16[8,24,7168]{2,1,0:T(8,128)(2,1)}, bf16[8,24,7168]{2,1,0:T(8,128)(2,1)}, u32[]{:S(2)}, u32[]{:S(2)}) collective-permute-start(bf16[8,24,7168]{2,1,0:T(8,128)(2,1)} %get-tuple-element.18), channel_id=1, source_target_pairs={{0,1},{1,0},{2,3},{3,2},{4,5},{5,4},{6,7},{7,6},{8,9},{9,8},{10,11... | collective-permute-start | bytes 8257544 | tf_op jit(solution)/shard_map/ppermute | solution.py:99
  179.1 17.7 %slice-start = ((s8[14680064]{0:T(1024)(128)(4,1)}), s8[4194304]{0:T(1024)(128)(4,1)S(1)}, s32[]{:S(2)}) async-start(s8[14680064]{0:T(1024)(128)(4,1)} %bitcast.89), calls=%async_computation.2 | async-start | bytes 8388608
  184.2 12.6 %copy-start.3 = (bf16[8,24,7168]{2,1,0:T(8,128)(2,1)S(1)}, bf16[8,24,7168]{2,1,0:T(8,128)(2,1)}, u32[]{:S(2)}) copy-start(bf16[8,24,7168]{2,1,0:T(8,128)(2,1)} %get-tuple-element.18) | copy-start | bytes 8257540
  184.2 12.6 %slice-start.1 = ((s8[14680064]{0:T(1024)(128)(4,1)}), s8[4194304]{0:T(1024)(128)(4,1)S(1)}, s32[]{:S(2)}) async-start(s8[14680064]{0:T(1024)(128)(4,1)} %bitcast.89), calls=%async_computation.3 | async-start | bytes 8388608
  184.2 12.6 %slice-start.2 = ((s8[14680064]{0:T(1024)(128)(4,1)}), s8[4194304]{0:T(1024)(128)(4,1)S(1)}, s32[]{:S(2)}) async-start(s8[14680064]{0:T(1024)(128)(4,1)} %bitcast.89), calls=%async_computation.4 | async-start | bytes 8388608
  184.2 12.6 %slice-start.3 = ((s8[14680064]{0:T(1024)(128)(4,1)}), s8[2097152]{0:T(1024)(128)(4,1)S(1)}, s32[]{:S(2)}) async-start(s8[14680064]{0:T(1024)(128)(4,1)} %bitcast.89), calls=%async_computation.5 | async-start | bytes 4194304
  184.2 45.9 %collective-permute-start.6 = (bf16[128,7168]{1,0:T(8,128)(2,1)}, bf16[128,7168]{1,0:T(8,128)(2,1)}, u32[]{:S(2)}, u32[]{:S(2)}) collective-permute-start(bf16[128,7168]{1,0:T(8,128)(2,1)} %fusion.4), channel_id=1, source_target_pairs={{0,114},{2,112},{16,2},{18,0},{32,18},{34,16},{48,34},{50,32},{64,... | collective-permute-start | bytes 5505032 | tf_op jit(solution)/shard_map/ppermute | solution.py:105
  205.2 27.7 %copy-start.1 = (bf16[1,1,16,48,1024]{4,3,2,1,0:T(8,128)(2,1)S(1)}, bf16[1,1,16,48,1024]{4,3,2,1,0:T(8,128)(2,1)}, u32[]{:S(2)}) copy-start(bf16[1,1,16,48,1024]{4,3,2,1,0:T(8,128)(2,1)} %param.13) | copy-start | bytes 4718596

commit v13 on v12

--- a/solution.py
+++ b/solution.py
@@ -83,8 +83,10 @@
                 "kech,dh->kecd", grad_pre, cols, preferred_element_type=jnp.float32
             ).astype(jnp.bfloat16)
             other = lax.ppermute(part[1], "core", [(0, 1), (1, 0)])
-            sums.append(part[0].astype(jnp.float32) + other.astype(jnp.float32))
-        pair_sum = jnp.concatenate(sums, axis=-1).astype(jnp.bfloat16)
+            sums.append(
+                (part[0].astype(jnp.float32) + other.astype(jnp.float32)).astype(jnp.bfloat16)
+            )
+        pair_sum = jnp.concatenate(sums, axis=-1)
         returned = lax.all_to_all(pair_sum, CHIPS, split_axis=0, concat_axis=0, tiled=True)
         rows, returned = lax.optimization_barrier((rows, returned))
 

time: 233 us -> 233 us (level)
  no operation moved by 1% of the time
where the time goes in v13:
time: 233 us
  waiting for transfers between devices  86.7 us (37%)
  blocking collectives  67.6 us (29%)
  matrix products  44.3 us (19%)
  local copies, waits for them, and re-layouts  12.8 us (5%)
  starting transfers between devices  10.7 us (5%)
  other arithmetic  9.88 us (4%)
    all_to_all x1, blocking collectives, shards(): lax.all_to_all(picked, CHIPS, split_axis=0, concat_axis=0, tiled=True)  67.6 us
    ppermute x1, waiting for transfers between devices, swap_ylo(): return lax.ppermute(block, 'ylo', [(0, 1), (1, 0)])  59.2 us
    ppermute x1, waiting for transfers between devices, shards(): grad_rows = lax.ppermute(grad_in, RING, ring_route(sections, -1))  23.3 us
    dot_general x2, matrix products, shards(): jnp.einsum('kech,dh->kecd', grad_pre, cols, preferred_element_type=jnp.fl...  18.4 us
    dot_general x1, matrix products, shards(): jnp.einsum('scd,dh->sch', jnp.concatenate([arrived[:, :half], partner_a])...  11.3 us
    dot_general x1, matrix products, shards(): jnp.einsum('scd,dh->sch', jnp.concatenate([arrived[:, half:], partner_b])...  7.88 us
    all_to_all x1, starting transfers between devices, shards(): lax.all_to_all(pair_sum, CHIPS, split_axis=0, concat_axis=0, tiled=True)  6.91 us
    dot_general x1, matrix products, shards(): jnp.einsum('ect,ecd->td', bwd_table, returned, preferred_element_type=jnp...  5.1 us
  transfers between devices with their start and end apart: 8, of which 4 were waited for; matrix products, arithmetic and copies ran while one was open for 17% of the time, Pallas kernels for 0%

profile of v13, /device:TPU:30, one launch (start us, length us, event | category | flops | bytes accessed | tf_op | source)
XLA Modules:
  0.0 232.9 jit_solution(12587298475026735734)
XLA Ops:
  0.9 2.7 %gather_fusion.1 = bf16[16,48,512]{2,1,0:T(8,128)(2,1)} fusion(bf16[16,48,512]{2,1,0:T(8,128)(2,1)} %bitcast.81, s32[1024]{0:T(1024)S(1)} %pad_clamp_fusion.2), kind=kCustom, calls=%fused_computation.clone | custom fusion | bytes 1572928 | tf_op jit(solution)/shard_map/jit(_take)/gather | solution.py:76
  3.6 0.6 gather_fusion
  4.2 0.3 select_convert_fusion
  4.5 0.8 copy-done.2
  5.4 0.9 fusion.28
  6.3 9.2 %fusion.14 = bf16[2,8,48,3584]{3,2,1,0:T(8,128)(2,1)S(1)} fusion(bf16[1,1,7168,1024]{3,2,1,0:T(8,128)(2,1)} %param.10, bf16[2,8,48,512]{3,2,1,0:T(8,128)(2,1)S(1)} %bitcast.85, bf16[2,8,48,512]{3,2,1,0:T(8,128)(2,1)S(1)} %bitcast.83), kind=kOutput, calls=%fused_computation.17 | convolution fusion | flops 5643042816 | bytes 14417920 | tf_op jit(solution)/shard_map/kech,dh->kecd/dot_general | solution.py:82
  15.8 9.2 %fusion.11 = bf16[2,8,48,3584]{3,2,1,0:T(8,128)(2,1)S(1)} fusion(bf16[1,1,7168,1024]{3,2,1,0:T(8,128)(2,1)} %param.10, bf16[2,8,48,512]{3,2,1,0:T(8,128)(2,1)S(1)} %bitcast.86, bf16[2,8,48,512]{3,2,1,0:T(8,128)(2,1)S(1)} %bitcast.84), kind=kOutput, calls=%fused_computation.16 | convolution fusion | flops 5643042816 | bytes 14417920 | tf_op jit(solution)/shard_map/kech,dh->kecd/dot_general | solution.py:82
  25.2 0.6 collective-permute-start.2
  25.7 0.7 fusion.23
  26.4 4.0 %collective-permute-done.2 = bf16[8,48,3584]{2,1,0:T(8,128)(2,1)S(1)} collective-permute-done((bf16[8,48,3584]{2,1,0:T(8,128)(2,1)S(1)}, bf16[8,48,3584]{2,1,0:T(8,128)(2,1)S(1)}, u32[]{:S(2)}, u32[]{:S(2)}) %collective-permute-start.2) | collective-permute-done | bytes 2752544 | tf_op jit(solution)/shard_map/ppermute | solution.py:85
  30.5 0.7 fusion.24
  31.2 3.2 %pad_maximum_fusion = bf16[8,48,7168]{2,1,0:T(8,128)(2,1)} fusion(bf16[8,48,3584]{2,1,0:T(8,128)(2,1)S(1)} %fusion.23, bf16[8,48,3584]{2,1,0:T(8,128)(2,1)S(1)} %fusion.24), kind=kLoop, calls=%fused_computation.18 | loop fusion | flops 11010048 | bytes 11010048 | tf_op jit(solution)/shard_map/concatenate | solution.py:89
  34.4 6.9 %all-to-all-start = ((bf16[8,48,7168]{2,1,0:T(8,128)(2,1)}), bf16[8,48,7168]{2,1,0:T(8,128)(2,1)}, u32[]{:S(2)}, u32[]{:S(2)}) async-start(bf16[8,48,7168]{2,1,0:T(8,128)(2,1)} %pad_maximum_fusion), calls=%async_computation | async-start | bytes 11010048 | tf_op jit(solution)/shard_map/all_to_all | solution.py:90
  41.4 1.3 collective-permute-start
  42.7 59.2 %collective-permute-done = s32[128,4]{0,1:T(4,128)S(1)} collective-permute-done((s32[128,4]{0,1:T(4,128)S(1)}, s32[128,4]{0,1:T(4,128)S(1)}, u32[]{:S(2)}, u32[]{:S(2)}) %collective-permute-start) | collective-permute-done | bytes 2080 | tf_op jit(solution)/shard_map/ppermute | solution.py:23
  102.3 0.6 reduce-window.14
  103.5 0.3 bitcast_reduce_fusion.1
  104.3 1.6 convolution_convert_fusion
  105.9 67.6 %all_to_all.10 = bf16[8,48,7168]{2,1,0:T(8,128)(2,1)S(1)} all-to-all(bf16[8,48,7168]{2,1,0:T(8,128)(2,1)S(1)} %convolution_convert_fusion), channel_id=1, replica_groups=mesh['x'=4,'yhi'=2,'z'=4,'ylo'=2,'core'=2] {'z','ylo'}, dimensions={0} | all-to-all | bytes 11010048 | tf_op jit(solution)/shard_map/all_to_all | solution.py:97
  173.5 2.9 %fusion.61 = (bf16[8,24,7168]{2,1,0:T(8,128)(2,1)}, bf16[8,24,7168]{2,1,0:T(8,128)(2,1)}) fusion(bf16[8,48,7168]{2,1,0:T(8,128)(2,1)S(1)} %all_to_all.10), kind=kLoop, calls=%fused_computation.122 | loop fusion | bytes 11010048 | tf_op jit(solution)/shard_map/slice | solution.py:113
  176.8 0.6 collective-permute-start.5
  177.4 0.6 reduce-window.16
  178.6 0.3 bitcast_reduce_fusion
  179.1 5.1 %fusion.4 = bf16[128,7168]{1,0:T(8,128)(2,1)} fusion(bf16[8,48,7168]{2,1,0:T(8,128)(2,1)} %all-to-all-done, bf16[128,8,48]{0,2,1:T(8,128)(2,1)S(1)} %copy.31), kind=kOutput, calls=%fused_computation.9 | convolution fusion | flops 705560576 | bytes 7438336 | tf_op jit(solution)/shard_map/ect,ecd->td/dot_general | solution.py:103
  184.2 1.2 collective-permute-start.6
  185.5 11.3 %fusion.2 = f32[16,24,1024]{2,1,0:T(8,128)S(1)} fusion(bf16[1,1,7168,1024]{3,2,1,0:T(8,128)(2,1)} %param.10, bf16[8,24,7168]{2,1,0:T(8,128)(2,1)} %collective-permute-done.4, bf16[8,24,7168]{2,1,0:T(8,128)(2,1)} %get-tuple-element.17), kind=kOutput, calls=%fused_computation.5 | convolution fusion | flops 5639897088 | bytes 21757952 | tf_op jit(solution)/shard_map/scd,dh->sch/dot_general | solution.py:111
  196.8 7.9 %fusion = f32[16,24,1024]{2,1,0:T(8,128)S(1)} fusion(bf16[1,1,7168,1024]{3,2,1,0:T(8,128)(2,1)S(1)} %bitcast.90, bf16[8,24,7168]{2,1,0:T(8,128)(2,1)} %collective-permute-done.5, bf16[8,24,7168]{2,1,0:T(8,128)(2,1)S(1)} %copy-done.3), kind=kOutput, calls=%fused_computation.3 | convolution fusion | flops 5639897088 | bytes 21757952 | tf_op jit(solution)/shard_map/scd,dh->sch/dot_general | solution.py:117
  204.7 0.5 fusion.33
  205.2 0.6 gather_fusion.2
  205.8 1.0 broadcast_select_fusion
  206.8 23.3 %collective-permute-done.6 = bf16[128,7168]{1,0:T(8,128)(2,1)} collective-permute-done((bf16[128,7168]{1,0:T(8,128)(2,1)}, bf16[128,7168]{1,0:T(8,128)(2,1)}, u32[]{:S(2)}, u32[]{:S(2)}) %collective-permute-start.6) | collective-permute-done | bytes 1835040 | tf_op jit(solution)/shard_map/ppermute | solution.py:107
  230.1 2.8 %copy.33 = bf16[1,128,7168]{2,1,0:T(8,128)(2,1)} copy(bf16[1,128,7168]{2,1,0:T(8,128)(2,1)} %bitcast.34) | data formatting | bytes 3670016
  (65 shorter events, 3.3 us)
Async XLA Ops:
  0.6 2.9 %copy-start = (bf16[1,1,16,48,1024]{4,3,2,1,0:T(8,128)(2,1)S(1)}, bf16[1,1,16,48,1024]{4,3,2,1,0:T(8,128)(2,1)}, u32[]{:S(2)}) copy-start(bf16[1,1,16,48,1024]{4,3,2,1,0:T(8,128)(2,1)} %param.13) | copy-start | bytes 4718596
  4.2 1.1 copy-start.2
  15.7 10.1 %collective-permute-start.3 = (bf16[8,48,3584]{2,1,0:T(8,128)(2,1)S(1)}, bf16[8,48,3584]{2,1,0:T(8,128)(2,1)S(1)}, u32[]{:S(2)}, u32[]{:S(2)}) collective-permute-start(bf16[8,48,3584]{2,1,0:T(8,128)(2,1)S(1)} %slice_bitcast_fusion), channel_id=1, source_target_pairs={{0,1},{1,0},{2,3},{3,2},{4,5},{5,4},{6,7},{7,6},{8,9},{9,8},{10,11... | collective-permute-start | bytes 8257544 | tf_op jit(solution)/shard_map/ppermute | solution.py:85
  25.2 5.3 %collective-permute-start.2 = (bf16[8,48,3584]{2,1,0:T(8,128)(2,1)S(1)}, bf16[8,48,3584]{2,1,0:T(8,128)(2,1)S(1)}, u32[]{:S(2)}, u32[]{:S(2)}) collective-permute-start(bf16[8,48,3584]{2,1,0:T(8,128)(2,1)S(1)} %slice_bitcast_fusion.2), channel_id=1, source_target_pairs={{0,1},{1,0},{2,3},{3,2},{4,5},{5,4},{6,7},{7,6},{8,9},{9,8},{10,11... | collective-permute-start | bytes 8257544 | tf_op jit(solution)/shard_map/ppermute | solution.py:85
  34.4 6.9 %copy-start.4 = (s32[1,128,2]{1,2,0:T(2,128)S(1)}, s32[1,128,2]{1,2,0:T(2,128)}, u32[]{:S(2)}) copy-start(s32[1,128,2]{1,2,0:T(2,128)} %param.11) | copy-start | bytes 3076
  34.4 6.9 %copy-start.5 = (s32[1,128,2]{1,2,0:T(2,128)S(1)}, s32[1,128,2]{1,2,0:T(2,128)}, u32[]{:S(2)}) copy-start(s32[1,128,2]{1,2,0:T(2,128)} %param.9) | copy-start | bytes 3076
  34.4 69.8 %all-to-all-start = ((bf16[8,48,7168]{2,1,0:T(8,128)(2,1)}), bf16[8,48,7168]{2,1,0:T(8,128)(2,1)}, u32[]{:S(2)}, u32[]{:S(2)}) async-start(bf16[8,48,7168]{2,1,0:T(8,128)(2,1)} %pad_maximum_fusion), calls=%async_computation | async-start | bytes 11010048 | tf_op jit(solution)/shard_map/all_to_all | solution.py:90
  41.4 62.7 %collective-permute-start.1 = (bf16[128,7168]{1,0:T(8,128)(2,1)}, bf16[128,7168]{1,0:T(8,128)(2,1)S(1)}, u32[]{:S(2)}, u32[]{:S(2)}) collective-permute-start(bf16[128,7168]{1,0:T(8,128)(2,1)} %bitcast.91), channel_id=1, source_target_pairs={{0,18},{2,16},{16,34},{18,32},{32,50},{34,48},{48,66},{50,64},{64,... | collective-permute-start | bytes 5505032 | tf_op jit(solution)/shard_map/ppermute | solution.py:73
  41.4 60.5 %collective-permute-start = (s32[128,4]{0,1:T(4,128)S(1)}, s32[128,4]{0,1:T(4,128)S(1)}, u32[]{:S(2)}, u32[]{:S(2)}) collective-permute-start(s32[128,4]{0,1:T(4,128)S(1)} %pad_add_fusion), channel_id=1, source_target_pairs={{0,2},{2,0},{1,3},{3,1},{4,6},{6,4},{5,7},{7,5},{8,10},{10,8},{9,1... | collective-permute-start | bytes 6152 | tf_op jit(solution)/shard_map/ppermute | solution.py:23
  176.3 7.9 %collective-permute-start.4 = (bf16[8,24,7168]{2,1,0:T(8,128)(2,1)}, bf16[8,24,7168]{2,1,0:T(8,128)(2,1)}, u32[]{:S(2)}, u32[]{:S(2)}) collective-permute-start(bf16[8,24,7168]{2,1,0:T(8,128)(2,1)} %get-tuple-element.17), channel_id=1, source_target_pairs={{0,1},{1,0},{2,3},{3,2},{4,5},{5,4},{6,7},{7,6},{8,9},{9,8},{10,11... | collective-permute-start | bytes 8257544 | tf_op jit(solution)/shard_map/ppermute | solution.py:100
  176.8 20.0 %collective-permute-start.5 = (bf16[8,24,7168]{2,1,0:T(8,128)(2,1)}, bf16[8,24,7168]{2,1,0:T(8,128)(2,1)}, u32[]{:S(2)}, u32[]{:S(2)}) collective-permute-start(bf16[8,24,7168]{2,1,0:T(8,128)(2,1)} %get-tuple-element.18), channel_id=1, source_target_pairs={{0,1},{1,0},{2,3},{3,2},{4,5},{5,4},{6,7},{7,6},{8,9},{9,8},{10,11... | collective-permute-start | bytes 8257544 | tf_op jit(solution)/shard_map/ppermute | solution.py:101
  179.1 17.7 %slice-start = ((s8[14680064]{0:T(1024)(128)(4,1)}), s8[4194304]{0:T(1024)(128)(4,1)S(1)}, s32[]{:S(2)}) async-start(s8[14680064]{0:T(1024)(128)(4,1)} %bitcast.89), calls=%async_computation.2 | async-start | bytes 8388608
  184.2 12.6 %copy-start.3 = (bf16[8,24,7168]{2,1,0:T(8,128)(2,1)S(1)}, bf16[8,24,7168]{2,1,0:T(8,128)(2,1)}, u32[]{:S(2)}) copy-start(bf16[8,24,7168]{2,1,0:T(8,128)(2,1)} %get-tuple-element.18) | copy-start | bytes 8257540
  184.2 12.6 %slice-start.1 = ((s8[14680064]{0:T(1024)(128)(4,1)}), s8[4194304]{0:T(1024)(128)(4,1)S(1)}, s32[]{:S(2)}) async-start(s8[14680064]{0:T(1024)(128)(4,1)} %bitcast.89), calls=%async_computation.3 | async-start | bytes 8388608
  184.2 12.6 %slice-start.2 = ((s8[14680064]{0:T(1024)(128)(4,1)}), s8[4194304]{0:T(1024)(128)(4,1)S(1)}, s32[]{:S(2)}) async-start(s8[14680064]{0:T(1024)(128)(4,1)} %bitcast.89), calls=%async_computation.4 | async-start | bytes 8388608
  184.2 12.6 %slice-start.3 = ((s8[14680064]{0:T(1024)(128)(4,1)}), s8[2097152]{0:T(1024)(128)(4,1)S(1)}, s32[]{:S(2)}) async-start(s8[14680064]{0:T(1024)(128)(4,1)} %bitcast.89), calls=%async_computation.5 | async-start | bytes 4194304
  184.2 45.9 %collective-permute-start.6 = (bf16[128,7168]{1,0:T(8,128)(2,1)}, bf16[128,7168]{1,0:T(8,128)(2,1)}, u32[]{:S(2)}, u32[]{:S(2)}) collective-permute-start(bf16[128,7168]{1,0:T(8,128)(2,1)} %fusion.4), channel_id=1, source_target_pairs={{0,114},{2,112},{16,2},{18,0},{32,18},{34,16},{48,34},{50,32},{64,... | collective-permute-start | bytes 5505032 | tf_op jit(solution)/shard_map/ppermute | solution.py:107
  205.2 27.7 %copy-start.1 = (bf16[1,1,16,48,1024]{4,3,2,1,0:T(8,128)(2,1)S(1)}, bf16[1,1,16,48,1024]{4,3,2,1,0:T(8,128)(2,1)}, u32[]{:S(2)}) copy-start(bf16[1,1,16,48,1024]{4,3,2,1,0:T(8,128)(2,1)} %param.13) | copy-start | bytes 4718596

commit v14 on v12

--- a/solution.py
+++ b/solution.py
@@ -89,14 +89,21 @@
         rows, returned = lax.optimization_barrier((rows, returned))
 
         fwd_table = slot_table(fwd_ids, experts, capacity).astype(jnp.bfloat16)
-        picked = jnp.einsum(
-            "ect,td->ecd", fwd_table, rows, preferred_element_type=jnp.float32
-        ).astype(jnp.bfloat16)
-        arrived = lax.all_to_all(picked, CHIPS, split_axis=0, concat_axis=0, tiled=True)
-
         half = capacity // 2
-        partner_a = lax.ppermute(arrived[:, :half], "core", [(0, 1), (1, 0)])
-        partner_b = lax.ppermute(arrived[:, half:], "core", [(0, 1), (1, 0)])
+        arrived_ab = [
+            lax.all_to_all(
+                jnp.einsum(
+                    "ect,td->ecd", table_half, rows, preferred_element_type=jnp.float32
+                ).astype(jnp.bfloat16),
+                CHIPS,
+                split_axis=0,
+                concat_axis=0,
+                tiled=True,
+            )
+            for table_half in (fwd_table[:, :half], fwd_table[:, half:])
+        ]
+        partner_a = lax.ppermute(arrived_ab[0], "core", [(0, 1), (1, 0)])
+        partner_b = lax.ppermute(arrived_ab[1], "core", [(0, 1), (1, 0)])
         bwd_table = slot_table(bwd_ids, experts, capacity).astype(jnp.bfloat16)
         grad_in = jnp.einsum(
             "ect,ecd->td", bwd_table, returned, preferred_element_type=jnp.float32
@@ -108,13 +115,13 @@
             [
                 jnp.einsum(
                     "scd,dh->sch",
-                    jnp.concatenate([arrived[:, :half], partner_a]),
+                    jnp.concatenate([arrived_ab[0], partner_a]),
                     weights,
                     preferred_element_type=jnp.float32,
                 ),
                 jnp.einsum(
                     "scd,dh->sch",
-                    jnp.concatenate([arrived[:, half:], partner_b]),
+                    jnp.concatenate([arrived_ab[1], partner_b]),
                     weights,
                     preferred_element_type=jnp.float32,
                 ),

time: 233 us -> 241 us (1.034)
  blocking collectives: 67.6 us -> 0 us
  waiting for transfers between devices: 86.7 us -> 148 us
  starting transfers between devices: 10.7 us -> 21.9 us
  local copies, waits for them, and re-layouts: 12.8 us -> 8.18 us
  matrix products: 44.3 us -> 48.4 us
  other arithmetic: 9.88 us -> 13.3 us
    all_to_all x1 -> x0, blocking collectives: 67.6 us -> none  [shards(): lax.all_to_all(picked, CHIPS, split_axis=0, concat_axis=0, tiled=True)]
    all_to_all x0 -> x2, waiting for transfers between devices: none -> 61.6 us  [shards(): lax.all_to_all(jnp.einsum('ect,td->ecd', table_half, rows, preferred_elem...]
    all_to_all x0 -> x2, starting transfers between devices: none -> 11.9 us  [shards(): lax.all_to_all(jnp.einsum('ect,td->ecd', table_half, rows, preferred_elem...]
    dot_general x3 -> x4, matrix products: 20.7 us -> 24.9 us  [the longest x1 11.2 us: shards(): jnp.einsum('scd,dh->sch', jnp.concatenate([arrived_ab[0], partner_a]), we...]
    slice x2 -> x1, local copies, waits for them, and re-layouts: 3.06 us -> 0.21 us  [the longest x1 2.85 us: shards(): arrived[:, :half]]
  transfers between devices with their start and end apart: 8 -> 10, of which waited for: 4 -> 6; matrix products, arithmetic and copies ran while one was open for 17% -> 18% of each run, Pallas kernels for 0% -> 0%
where the time goes in v14:
time: 241 us
  waiting for transfers between devices  148 us (61%)
  matrix products  48.4 us (20%)
  starting transfers between devices  21.9 us (9%)
  other arithmetic  13.3 us (6%)
  local copies, waits for them, and re-layouts  8.18 us (3%)
    all_to_all x2, waiting for transfers between devices, shards(): lax.all_to_all(jnp.einsum('ect,td->ecd', table_half, rows, preferred_elem...  61.6 us
    ppermute x1, waiting for transfers between devices, swap_ylo(): return lax.ppermute(block, 'ylo', [(0, 1), (1, 0)])  59.2 us
    ppermute x1, waiting for transfers between devices, shards(): grad_rows = lax.ppermute(grad_in, RING, ring_route(sections, -1))  23 us
    dot_general x2, matrix products, shards(): jnp.einsum('kech,dh->kecd', grad_pre, cols, preferred_element_type=jnp.fl...  18.4 us
    all_to_all x2, starting transfers between devices, shards(): lax.all_to_all(jnp.einsum('ect,td->ecd', table_half, rows, preferred_elem...  11.9 us
    dot_general x1, matrix products, shards(): jnp.einsum('scd,dh->sch', jnp.concatenate([arrived_ab[0], partner_a]), we...  11.2 us
    dot_general x1, matrix products, shards(): jnp.einsum('scd,dh->sch', jnp.concatenate([arrived_ab[1], partner_b]), we...  8.64 us
    all_to_all x1, starting transfers between devices, shards(): lax.all_to_all(pair_sum, CHIPS, split_axis=0, concat_axis=0, tiled=True)  6.91 us
  transfers between devices with their start and end apart: 10, of which 6 were waited for; matrix products, arithmetic and copies ran while one was open for 18% of the time, Pallas kernels for 0%

profile of v14, /device:TPU:30, one launch (start us, length us, event | category | flops | bytes accessed | tf_op | source)
XLA Modules:
  0.0 240.6 jit_solution(5739210816340584363)
XLA Ops:
  0.9 1.2 copy-done
  2.0 0.6 gather_fusion
  2.7 1.9 select_convert_fusion
  4.6 0.6 gather_fusion.1
  5.3 2.7 %fusion.29 = (bf16[16,48,512]{2,1,0:T(8,128)(2,1)S(1)}, bf16[16,48,512]{2,1,0:T(8,128)(2,1)S(1)}) fusion(f32[16,48,1024]{2,1,0:T(8,128)} %select_convert_fusion, bf16[16,48,512]{2,1,0:T(8,128)(2,1)S(1)} %gather_fusion.1, pred[16]{0:T(512)(128)(4,1)S(1)} %get-tuple-element.15), kind=kLoop, calls=%fused_computation.42 | loop fusion | flops 5898240 | bytes 5505040 | tf_op jit(solution)/shard_map/convert.9
  7.9 9.2 %fusion.11 = bf16[2,8,48,3584]{3,2,1,0:T(8,128)(2,1)S(1)} fusion(bf16[1,1,7168,1024]{3,2,1,0:T(8,128)(2,1)} %param.10, bf16[2,8,48,512]{3,2,1,0:T(8,128)(2,1)S(1)} %bitcast.87, bf16[2,8,48,512]{3,2,1,0:T(8,128)(2,1)S(1)} %bitcast.85), kind=kOutput, calls=%fused_computation.17 | convolution fusion | flops 5643042816 | bytes 14417920 | tf_op jit(solution)/shard_map/kech,dh->kecd/dot_general | solution.py:82
  17.4 9.2 %fusion.14 = bf16[2,8,48,3584]{3,2,1,0:T(8,128)(2,1)S(1)} fusion(bf16[1,1,7168,1024]{3,2,1,0:T(8,128)(2,1)} %param.10, bf16[2,8,48,512]{3,2,1,0:T(8,128)(2,1)S(1)} %bitcast.88, bf16[2,8,48,512]{3,2,1,0:T(8,128)(2,1)S(1)} %bitcast.86), kind=kOutput, calls=%fused_computation.18 | convolution fusion | flops 5643042816 | bytes 14417920 | tf_op jit(solution)/shard_map/kech,dh->kecd/dot_general | solution.py:82
  26.9 0.6 collective-permute-start.3
  27.4 0.7 fusion.24
  28.2 4.0 %collective-permute-done.3 = bf16[8,48,3584]{2,1,0:T(8,128)(2,1)S(1)} collective-permute-done((bf16[8,48,3584]{2,1,0:T(8,128)(2,1)S(1)}, bf16[8,48,3584]{2,1,0:T(8,128)(2,1)S(1)}, u32[]{:S(2)}, u32[]{:S(2)}) %collective-permute-start.3) | collective-permute-done | bytes 2752544 | tf_op jit(solution)/shard_map/ppermute | solution.py:85
  32.1 0.7 fusion.23
  32.9 3.1 %pad_maximum_fusion = bf16[8,48,7168]{2,1,0:T(8,128)(2,1)} fusion(bf16[8,48,3584]{2,1,0:T(8,128)(2,1)S(1)} %fusion.23, bf16[8,48,3584]{2,1,0:T(8,128)(2,1)S(1)} %fusion.24), kind=kLoop, calls=%fused_computation.19 | loop fusion | flops 11010048 | bytes 11010048 | tf_op jit(solution)/shard_map/concatenate | solution.py:87
  36.0 6.9 %all-to-all-start = ((bf16[8,48,7168]{2,1,0:T(8,128)(2,1)}), bf16[8,48,7168]{2,1,0:T(8,128)(2,1)}, u32[]{:S(2)}, u32[]{:S(2)}) async-start(bf16[8,48,7168]{2,1,0:T(8,128)(2,1)} %pad_maximum_fusion), calls=%async_computation | async-start | bytes 11010048 | tf_op jit(solution)/shard_map/all_to_all | solution.py:88
  42.9 1.4 collective-permute-start
  44.3 59.2 %collective-permute-done = s32[128,4]{0,1:T(4,128)S(1)} collective-permute-done((s32[128,4]{0,1:T(4,128)S(1)}, s32[128,4]{0,1:T(4,128)S(1)}, u32[]{:S(2)}, u32[]{:S(2)}) %collective-permute-start) | collective-permute-done | bytes 2080 | tf_op jit(solution)/shard_map/ppermute | solution.py:23
  103.9 0.6 reduce-window.14
  105.8 2.5 %convolution_convert_fusion.1 = bf16[8,24,7168]{2,1,0:T(8,128)(2,1)} fusion(bf16[128,7168]{1,0:T(8,128)(2,1)S(1)} %collective-permute-done.1, bf16[8,48,128]{2,1,0:T(8,128)(2,1)S(1)} %bitcast.89), kind=kOutput, calls=%fused_computation.8 | convolution fusion | flops 353697792 | bytes 4636672 | tf_op jit(solution)/shard_map/ect,td->ecd/dot_general | solution.py:95
  108.3 6.4 %all-to-all-start.1 = ((bf16[8,24,7168]{2,1,0:T(8,128)(2,1)}), bf16[8,24,7168]{2,1,0:T(8,128)(2,1)}, u32[]{:S(2)}, u32[]{:S(2)}) async-start(bf16[8,24,7168]{2,1,0:T(8,128)(2,1)} %convolution_convert_fusion.1), calls=%async_computation.1 | async-start | bytes 5505024 | tf_op jit(solution)/shard_map/all_to_all | solution.py:94
  114.7 2.5 %convolution_convert_fusion = bf16[8,24,7168]{2,1,0:T(8,128)(2,1)} fusion(bf16[128,7168]{1,0:T(8,128)(2,1)S(1)} %collective-permute-done.1, bf16[8,48,128]{2,1,0:T(8,128)(2,1)S(1)} %bitcast.90), kind=kOutput, calls=%fused_computation.7 | convolution fusion | flops 353697792 | bytes 4636672 | tf_op jit(solution)/shard_map/ect,td->ecd/dot_general | solution.py:95
  117.2 30.2 %all-to-all-done.1 = bf16[8,24,7168]{2,1,0:T(8,128)(2,1)} async-done(((bf16[8,24,7168]{2,1,0:T(8,128)(2,1)}), bf16[8,24,7168]{2,1,0:T(8,128)(2,1)}, u32[]{:S(2)}, u32[]{:S(2)}) %all-to-all-start.1) | async-done | bytes 2752544 | tf_op jit(solution)/shard_map/all_to_all | solution.py:94
  147.4 5.5 %all-to-all-start.2 = ((bf16[8,24,7168]{2,1,0:T(8,128)(2,1)}), bf16[8,24,7168]{2,1,0:T(8,128)(2,1)}, u32[]{:S(2)}, u32[]{:S(2)}) async-start(bf16[8,24,7168]{2,1,0:T(8,128)(2,1)} %convolution_convert_fusion), calls=%async_computation.2 | async-start | bytes 5505024 | tf_op jit(solution)/shard_map/all_to_all | solution.py:94
  153.4 31.4 %all-to-all-done.2 = bf16[8,24,7168]{2,1,0:T(8,128)(2,1)} async-done(((bf16[8,24,7168]{2,1,0:T(8,128)(2,1)}), bf16[8,24,7168]{2,1,0:T(8,128)(2,1)}, u32[]{:S(2)}, u32[]{:S(2)}) %all-to-all-start.2) | async-done | bytes 2752544 | tf_op jit(solution)/shard_map/all_to_all | solution.py:94
  184.8 0.6 reduce-window.16
  186.5 5.1 %fusion.4 = bf16[128,7168]{1,0:T(8,128)(2,1)} fusion(bf16[8,48,7168]{2,1,0:T(8,128)(2,1)} %all-to-all-done, bf16[128,8,48]{0,2,1:T(8,128)(2,1)S(1)} %copy.31), kind=kOutput, calls=%fused_computation.10 | convolution fusion | flops 705560576 | bytes 7438336 | tf_op jit(solution)/shard_map/ect,ecd->td/dot_general | solution.py:108
  191.6 1.1 collective-permute-start.6
  192.7 11.2 %fusion.2 = f32[16,24,1024]{2,1,0:T(8,128)S(1)} fusion(bf16[1,1,7168,1024]{3,2,1,0:T(8,128)(2,1)} %param.10, bf16[8,24,7168]{2,1,0:T(8,128)(2,1)} %collective-permute-done.4, bf16[8,24,7168]{2,1,0:T(8,128)(2,1)} %all-to-all-done.1), kind=kOutput, calls=%fused_computation.5 | convolution fusion | flops 5639897088 | bytes 21757952 | tf_op jit(solution)/shard_map/scd,dh->sch/dot_general | solution.py:116
  204.0 8.6 %fusion = f32[16,24,1024]{2,1,0:T(8,128)S(1)} fusion(bf16[1,1,7168,1024]{3,2,1,0:T(8,128)(2,1)S(1)} %bitcast.94, bf16[8,24,7168]{2,1,0:T(8,128)(2,1)} %collective-permute-done.5, bf16[8,24,7168]{2,1,0:T(8,128)(2,1)} %all-to-all-done.2), kind=kOutput, calls=%fused_computation.3 | convolution fusion | flops 5639897088 | bytes 21757952 | tf_op jit(solution)/shard_map/scd,dh->sch/dot_general | solution.py:122
  212.6 0.5 fusion.34
  213.2 0.6 gather_fusion.2
  213.8 1.0 broadcast_select_fusion
  214.8 23.0 %collective-permute-done.6 = bf16[128,7168]{1,0:T(8,128)(2,1)} collective-permute-done((bf16[128,7168]{1,0:T(8,128)(2,1)}, bf16[128,7168]{1,0:T(8,128)(2,1)}, u32[]{:S(2)}, u32[]{:S(2)}) %collective-permute-start.6) | collective-permute-done | bytes 1835040 | tf_op jit(solution)/shard_map/ppermute | solution.py:112
  237.7 2.8 %copy.33 = bf16[1,128,7168]{2,1,0:T(8,128)(2,1)} copy(bf16[1,128,7168]{2,1,0:T(8,128)(2,1)} %bitcast.34) | data formatting | bytes 3670016
  (66 shorter events, 4.0 us)
Async XLA Ops:
  0.6 1.4 copy-start
  2.7 1.9 copy-start.2
  17.4 10.1 %collective-permute-start.2 = (bf16[8,48,3584]{2,1,0:T(8,128)(2,1)S(1)}, bf16[8,48,3584]{2,1,0:T(8,128)(2,1)S(1)}, u32[]{:S(2)}, u32[]{:S(2)}) collective-permute-start(bf16[8,48,3584]{2,1,0:T(8,128)(2,1)S(1)} %slice_bitcast_fusion.2), channel_id=1, source_target_pairs={{0,1},{1,0},{2,3},{3,2},{4,5},{5,4},{6,7},{7,6},{8,9},{9,8},{10,11... | collective-permute-start | bytes 8257544 | tf_op jit(solution)/shard_map/ppermute | solution.py:85
  26.9 5.3 %collective-permute-start.3 = (bf16[8,48,3584]{2,1,0:T(8,128)(2,1)S(1)}, bf16[8,48,3584]{2,1,0:T(8,128)(2,1)S(1)}, u32[]{:S(2)}, u32[]{:S(2)}) collective-permute-start(bf16[8,48,3584]{2,1,0:T(8,128)(2,1)S(1)} %slice_bitcast_fusion), channel_id=1, source_target_pairs={{0,1},{1,0},{2,3},{3,2},{4,5},{5,4},{6,7},{7,6},{8,9},{9,8},{10,11... | collective-permute-start | bytes 8257544 | tf_op jit(solution)/shard_map/ppermute | solution.py:85
  36.0 6.9 %copy-start.3 = (s32[1,128,2]{1,2,0:T(2,128)S(1)}, s32[1,128,2]{1,2,0:T(2,128)}, u32[]{:S(2)}) copy-start(s32[1,128,2]{1,2,0:T(2,128)} %param.11) | copy-start | bytes 3076
  36.0 6.9 %copy-start.4 = (s32[1,128,2]{1,2,0:T(2,128)S(1)}, s32[1,128,2]{1,2,0:T(2,128)}, u32[]{:S(2)}) copy-start(s32[1,128,2]{1,2,0:T(2,128)} %param.9) | copy-start | bytes 3076
  36.0 69.8 %all-to-all-start = ((bf16[8,48,7168]{2,1,0:T(8,128)(2,1)}), bf16[8,48,7168]{2,1,0:T(8,128)(2,1)}, u32[]{:S(2)}, u32[]{:S(2)}) async-start(bf16[8,48,7168]{2,1,0:T(8,128)(2,1)} %pad_maximum_fusion), calls=%async_computation | async-start | bytes 11010048 | tf_op jit(solution)/shard_map/all_to_all | solution.py:88
  42.9 62.7 %collective-permute-start.1 = (bf16[128,7168]{1,0:T(8,128)(2,1)}, bf16[128,7168]{1,0:T(8,128)(2,1)S(1)}, u32[]{:S(2)}, u32[]{:S(2)}) collective-permute-start(bf16[128,7168]{1,0:T(8,128)(2,1)} %bitcast.95), channel_id=1, source_target_pairs={{0,18},{2,16},{16,34},{18,32},{32,50},{34,48},{48,66},{50,64},{64,... | collective-permute-start | bytes 5505032 | tf_op jit(solution)/shard_map/ppermute | solution.py:73
  42.9 60.5 %collective-permute-start = (s32[128,4]{0,1:T(4,128)S(1)}, s32[128,4]{0,1:T(4,128)S(1)}, u32[]{:S(2)}, u32[]{:S(2)}) collective-permute-start(s32[128,4]{0,1:T(4,128)S(1)} %pad_add_fusion), channel_id=1, source_target_pairs={{0,2},{2,0},{1,3},{3,1},{4,6},{6,4},{5,7},{7,5},{8,10},{10,8},{9,1... | collective-permute-start | bytes 6152 | tf_op jit(solution)/shard_map/ppermute | solution.py:23
  108.3 39.1 %all-to-all-start.1 = ((bf16[8,24,7168]{2,1,0:T(8,128)(2,1)}), bf16[8,24,7168]{2,1,0:T(8,128)(2,1)}, u32[]{:S(2)}, u32[]{:S(2)}) async-start(bf16[8,24,7168]{2,1,0:T(8,128)(2,1)} %convolution_convert_fusion.1), calls=%async_computation.1 | async-start | bytes 5505024 | tf_op jit(solution)/shard_map/all_to_all | solution.py:94
  147.4 37.3 %all-to-all-start.2 = ((bf16[8,24,7168]{2,1,0:T(8,128)(2,1)}), bf16[8,24,7168]{2,1,0:T(8,128)(2,1)}, u32[]{:S(2)}, u32[]{:S(2)}) async-start(bf16[8,24,7168]{2,1,0:T(8,128)(2,1)} %convolution_convert_fusion), calls=%async_computation.2 | async-start | bytes 5505024 | tf_op jit(solution)/shard_map/all_to_all | solution.py:94
  153.0 38.7 %collective-permute-start.4 = (bf16[8,24,7168]{2,1,0:T(8,128)(2,1)}, bf16[8,24,7168]{2,1,0:T(8,128)(2,1)}, u32[]{:S(2)}, u32[]{:S(2)}) collective-permute-start(bf16[8,24,7168]{2,1,0:T(8,128)(2,1)} %all-to-all-done.1), channel_id=1, source_target_pairs={{0,1},{1,0},{2,3},{3,2},{4,5},{5,4},{6,7},{7,6},{8,9},{9,8},{10,11... | collective-permute-start | bytes 8257544 | tf_op jit(solution)/shard_map/ppermute | solution.py:105
  184.8 19.2 %collective-permute-start.5 = (bf16[8,24,7168]{2,1,0:T(8,128)(2,1)}, bf16[8,24,7168]{2,1,0:T(8,128)(2,1)}, u32[]{:S(2)}, u32[]{:S(2)}) collective-permute-start(bf16[8,24,7168]{2,1,0:T(8,128)(2,1)} %all-to-all-done.2), channel_id=1, source_target_pairs={{0,1},{1,0},{2,3},{3,2},{4,5},{5,4},{6,7},{7,6},{8,9},{9,8},{10,11... | collective-permute-start | bytes 8257544 | tf_op jit(solution)/shard_map/ppermute | solution.py:106
  186.5 17.4 %slice-start = ((s8[14680064]{0:T(1024)(128)(4,1)}), s8[4194304]{0:T(1024)(128)(4,1)S(1)}, s32[]{:S(2)}) async-start(s8[14680064]{0:T(1024)(128)(4,1)} %bitcast.93), calls=%async_computation.3 | async-start | bytes 8388608
  191.6 12.3 %slice-start.1 = ((s8[14680064]{0:T(1024)(128)(4,1)}), s8[4194304]{0:T(1024)(128)(4,1)S(1)}, s32[]{:S(2)}) async-start(s8[14680064]{0:T(1024)(128)(4,1)} %bitcast.93), calls=%async_computation.4 | async-start | bytes 8388608
  191.6 12.3 %slice-start.2 = ((s8[14680064]{0:T(1024)(128)(4,1)}), s8[4194304]{0:T(1024)(128)(4,1)S(1)}, s32[]{:S(2)}) async-start(s8[14680064]{0:T(1024)(128)(4,1)} %bitcast.93), calls=%async_computation.5 | async-start | bytes 8388608
  191.6 12.3 %slice-start.3 = ((s8[14680064]{0:T(1024)(128)(4,1)}), s8[2097152]{0:T(1024)(128)(4,1)S(1)}, s32[]{:S(2)}) async-start(s8[14680064]{0:T(1024)(128)(4,1)} %bitcast.93), calls=%async_computation.6 | async-start | bytes 4194304
  191.6 46.1 %collective-permute-start.6 = (bf16[128,7168]{1,0:T(8,128)(2,1)}, bf16[128,7168]{1,0:T(8,128)(2,1)}, u32[]{:S(2)}, u32[]{:S(2)}) collective-permute-start(bf16[128,7168]{1,0:T(8,128)(2,1)} %fusion.4), channel_id=1, source_target_pairs={{0,114},{2,112},{16,2},{18,0},{32,18},{34,16},{48,34},{50,32},{64,... | collective-permute-start | bytes 5505032 | tf_op jit(solution)/shard_map/ppermute | solution.py:112
  213.1 27.4 %copy-start.1 = (bf16[1,1,16,48,1024]{4,3,2,1,0:T(8,128)(2,1)S(1)}, bf16[1,1,16,48,1024]{4,3,2,1,0:T(8,128)(2,1)}, u32[]{:S(2)}) copy-start(bf16[1,1,16,48,1024]{4,3,2,1,0:T(8,128)(2,1)} %param.13) | copy-start | bytes 4718596

commit v15 on v12

--- a/solution.py
+++ b/solution.py
@@ -94,9 +94,9 @@
         ).astype(jnp.bfloat16)
         arrived = lax.all_to_all(picked, CHIPS, split_axis=0, concat_axis=0, tiled=True)
 
-        half = capacity // 2
-        partner_a = lax.ppermute(arrived[:, :half], "core", [(0, 1), (1, 0)])
-        partner_b = lax.ppermute(arrived[:, half:], "core", [(0, 1), (1, 0)])
+        half = chips // 2
+        partner_a = lax.ppermute(arrived[:half], "core", [(0, 1), (1, 0)])
+        partner_b = lax.ppermute(arrived[half:], "core", [(0, 1), (1, 0)])
         bwd_table = slot_table(bwd_ids, experts, capacity).astype(jnp.bfloat16)
         grad_in = jnp.einsum(
             "ect,ecd->td", bwd_table, returned, preferred_element_type=jnp.float32
@@ -108,25 +108,26 @@
             [
                 jnp.einsum(
                     "scd,dh->sch",
-                    jnp.concatenate([arrived[:, :half], partner_a]),
+                    jnp.concatenate([arrived[:half], partner_a]),
                     weights,
                     preferred_element_type=jnp.float32,
                 ),
                 jnp.einsum(
                     "scd,dh->sch",
-                    jnp.concatenate([arrived[:, half:], partner_b]),
+                    jnp.concatenate([arrived[half:], partner_b]),
                     weights,
                     preferred_element_type=jnp.float32,
                 ),
             ],
-            axis=1,
+            axis=0,
         )
         hidden = (jax.nn.silu(projected[..., :hid_units]) * projected[..., hid_units:]).astype(
             jnp.bfloat16
         )
         blocks = jnp.arange(2 * experts, dtype=jnp.int32)
         chip_of = (blocks // 4) * 2 + (1 - (blocks // 2) % 2)
-        hidden = jnp.take(hidden, jnp.where(blocks % 2 == core, chip_of, chips + chip_of), axis=0)
+        place = (chip_of // half) * chips + jnp.where(blocks % 2 == core, 0, half) + chip_of % half
+        hidden = jnp.take(hidden, place, axis=0)
         hidden, grad_rows = lax.optimization_barrier((hidden, grad_rows))
         return (hidden[None, None], grad_rows[None])
 

time: 233 us -> 234 us (level)
  no operation moved by 1% of the time
where the time goes in v15:
time: 234 us; the launch traced here: 233 us
  waiting for transfers between devices  86.8 us (37%)
  blocking collectives  67.6 us (29%)
  matrix products  44.1 us (19%)
  local copies, waits for them, and re-layouts  13 us (6%)
  starting transfers between devices  10.7 us (5%)
  other arithmetic  9.91 us (4%)
    all_to_all x1, blocking collectives, shards(): lax.all_to_all(picked, CHIPS, split_axis=0, concat_axis=0, tiled=True)  67.6 us
    ppermute x1, waiting for transfers between devices, swap_ylo(): return lax.ppermute(block, 'ylo', [(0, 1), (1, 0)])  59.2 us
    ppermute x1, waiting for transfers between devices, shards(): grad_rows = lax.ppermute(grad_in, RING, ring_route(sections, -1))  23.4 us
    dot_general x2, matrix products, shards(): jnp.einsum('kech,dh->kecd', grad_pre, cols, preferred_element_type=jnp.fl...  18.4 us
    dot_general x1, matrix products, shards(): jnp.einsum('scd,dh->sch', jnp.concatenate([arrived[:half], partner_a]), w...  11.2 us
    dot_general x1, matrix products, shards(): jnp.einsum('scd,dh->sch', jnp.concatenate([arrived[half:], partner_b]), w...  7.76 us
    all_to_all x1, starting transfers between devices, shards(): lax.all_to_all(pair_sum, CHIPS, split_axis=0, concat_axis=0, tiled=True)  6.91 us
    dot_general x1, matrix products, shards(): jnp.einsum('ect,ecd->td', bwd_table, returned, preferred_element_type=jnp...  5.1 us
  transfers between devices with their start and end apart: 8, of which 4 were waited for; matrix products, arithmetic and copies ran while one was open for 17% of the time, Pallas kernels for 0%

profile of v15, /device:TPU:30, one launch (start us, length us, event | category | flops | bytes accessed | tf_op | source)
XLA Modules:
  0.0 233.1 jit_solution(12770946336312512663)
XLA Ops:
  0.9 2.7 %gather_fusion.1 = bf16[16,48,512]{2,1,0:T(8,128)(2,1)} fusion(bf16[16,48,512]{2,1,0:T(8,128)(2,1)} %bitcast.81, s32[1024]{0:T(1024)S(1)} %pad_clamp_fusion.2), kind=kCustom, calls=%fused_computation.clone | custom fusion | bytes 1572928 | tf_op jit(solution)/shard_map/jit(_take)/gather | solution.py:76
  3.6 0.6 gather_fusion
  4.2 0.3 select_convert_fusion
  4.5 0.8 copy-done.2
  5.4 0.9 fusion.28
  6.3 9.2 %fusion.14 = bf16[2,8,48,3584]{3,2,1,0:T(8,128)(2,1)S(1)} fusion(bf16[1,1,7168,1024]{3,2,1,0:T(8,128)(2,1)} %param.10, bf16[2,8,48,512]{3,2,1,0:T(8,128)(2,1)S(1)} %bitcast.85, bf16[2,8,48,512]{3,2,1,0:T(8,128)(2,1)S(1)} %bitcast.83), kind=kOutput, calls=%fused_computation.17 | convolution fusion | flops 5643042816 | bytes 14417920 | tf_op jit(solution)/shard_map/kech,dh->kecd/dot_general | solution.py:82
  15.8 9.2 %fusion.11 = bf16[2,8,48,3584]{3,2,1,0:T(8,128)(2,1)S(1)} fusion(bf16[1,1,7168,1024]{3,2,1,0:T(8,128)(2,1)} %param.10, bf16[2,8,48,512]{3,2,1,0:T(8,128)(2,1)S(1)} %bitcast.86, bf16[2,8,48,512]{3,2,1,0:T(8,128)(2,1)S(1)} %bitcast.84), kind=kOutput, calls=%fused_computation.16 | convolution fusion | flops 5643042816 | bytes 14417920 | tf_op jit(solution)/shard_map/kech,dh->kecd/dot_general | solution.py:82
  25.2 0.6 collective-permute-start.2
  25.7 0.7 fusion.23
  26.4 4.0 %collective-permute-done.2 = bf16[8,48,3584]{2,1,0:T(8,128)(2,1)S(1)} collective-permute-done((bf16[8,48,3584]{2,1,0:T(8,128)(2,1)S(1)}, bf16[8,48,3584]{2,1,0:T(8,128)(2,1)S(1)}, u32[]{:S(2)}, u32[]{:S(2)}) %collective-permute-start.2) | collective-permute-done | bytes 2752544 | tf_op jit(solution)/shard_map/ppermute | solution.py:85
  30.5 0.7 fusion.24
  31.2 3.2 %pad_maximum_fusion = bf16[8,48,7168]{2,1,0:T(8,128)(2,1)} fusion(bf16[8,48,3584]{2,1,0:T(8,128)(2,1)S(1)} %fusion.23, bf16[8,48,3584]{2,1,0:T(8,128)(2,1)S(1)} %fusion.24), kind=kLoop, calls=%fused_computation.18 | loop fusion | flops 11010048 | bytes 11010048 | tf_op jit(solution)/shard_map/concatenate | solution.py:87
  34.4 6.9 %all-to-all-start = ((bf16[8,48,7168]{2,1,0:T(8,128)(2,1)}), bf16[8,48,7168]{2,1,0:T(8,128)(2,1)}, u32[]{:S(2)}, u32[]{:S(2)}) async-start(bf16[8,48,7168]{2,1,0:T(8,128)(2,1)} %pad_maximum_fusion), calls=%async_computation | async-start | bytes 11010048 | tf_op jit(solution)/shard_map/all_to_all | solution.py:88
  41.4 1.3 collective-permute-start
  42.7 59.2 %collective-permute-done = s32[128,4]{0,1:T(4,128)S(1)} collective-permute-done((s32[128,4]{0,1:T(4,128)S(1)}, s32[128,4]{0,1:T(4,128)S(1)}, u32[]{:S(2)}, u32[]{:S(2)}) %collective-permute-start) | collective-permute-done | bytes 2080 | tf_op jit(solution)/shard_map/ppermute | solution.py:23
  102.3 0.6 reduce-window.14
  103.5 0.3 bitcast_reduce_fusion.1
  104.3 1.6 convolution_convert_fusion
  105.9 67.6 %all_to_all.10 = bf16[8,48,7168]{2,1,0:T(8,128)(2,1)S(1)} all-to-all(bf16[8,48,7168]{2,1,0:T(8,128)(2,1)S(1)} %convolution_convert_fusion), channel_id=1, replica_groups=mesh['x'=4,'yhi'=2,'z'=4,'ylo'=2,'core'=2] {'z','ylo'}, dimensions={0} | all-to-all | bytes 11010048 | tf_op jit(solution)/shard_map/all_to_all | solution.py:95
  173.5 3.0 %fusion.63 = (bf16[4,48,7168]{2,1,0:T(8,128)(2,1)}, bf16[4,48,7168]{2,1,0:T(8,128)(2,1)}) fusion(bf16[8,48,7168]{2,1,0:T(8,128)(2,1)S(1)} %all_to_all.10), kind=kLoop, calls=%fused_computation.130 | loop fusion | bytes 11010048 | tf_op jit(solution)/shard_map/slice | solution.py:111
  177.0 0.6 collective-permute-start.5
  177.6 0.6 reduce-window.16
  178.7 0.3 bitcast_reduce_fusion
  179.3 5.1 %fusion.4 = bf16[128,7168]{1,0:T(8,128)(2,1)} fusion(bf16[8,48,7168]{2,1,0:T(8,128)(2,1)} %all-to-all-done, bf16[128,8,48]{0,2,1:T(8,128)(2,1)S(1)} %copy.31), kind=kOutput, calls=%fused_computation.9 | convolution fusion | flops 705560576 | bytes 7438336 | tf_op jit(solution)/shard_map/ect,ecd->td/dot_general | solution.py:101
  184.4 1.2 collective-permute-start.6
  185.6 11.2 %fusion.2 = f32[8,48,1024]{2,1,0:T(8,128)S(1)} fusion(bf16[1,1,7168,1024]{3,2,1,0:T(8,128)(2,1)} %param.10, bf16[4,48,7168]{2,1,0:T(8,128)(2,1)} %collective-permute-done.4, bf16[4,48,7168]{2,1,0:T(8,128)(2,1)} %get-tuple-element.17), kind=kOutput, calls=%fused_computation.5 | convolution fusion | flops 5639897088 | bytes 21757952 | tf_op jit(solution)/shard_map/scd,dh->sch/dot_general | solution.py:109
  196.9 7.8 %fusion = f32[8,48,1024]{2,1,0:T(8,128)S(1)} fusion(bf16[1,1,7168,1024]{3,2,1,0:T(8,128)(2,1)S(1)} %bitcast.90, bf16[4,48,7168]{2,1,0:T(8,128)(2,1)} %collective-permute-done.5, bf16[4,48,7168]{2,1,0:T(8,128)(2,1)S(1)} %copy-done.3), kind=kOutput, calls=%fused_computation.3 | convolution fusion | flops 5639897088 | bytes 21757952 | tf_op jit(solution)/shard_map/scd,dh->sch/dot_general | solution.py:115
  204.7 0.5 fusion.33
  205.2 0.6 gather_fusion.2
  205.9 1.0 broadcast_select_fusion
  206.9 23.4 %collective-permute-done.6 = bf16[128,7168]{1,0:T(8,128)(2,1)} collective-permute-done((bf16[128,7168]{1,0:T(8,128)(2,1)}, bf16[128,7168]{1,0:T(8,128)(2,1)}, u32[]{:S(2)}, u32[]{:S(2)}) %collective-permute-start.6) | collective-permute-done | bytes 1835040 | tf_op jit(solution)/shard_map/ppermute | solution.py:105
  230.3 2.8 %copy.33 = bf16[1,128,7168]{2,1,0:T(8,128)(2,1)} copy(bf16[1,128,7168]{2,1,0:T(8,128)(2,1)} %bitcast.34) | data formatting | bytes 3670016
  (65 shorter events, 3.3 us)
Async XLA Ops:
  0.6 2.9 %copy-start = (bf16[1,1,16,48,1024]{4,3,2,1,0:T(8,128)(2,1)S(1)}, bf16[1,1,16,48,1024]{4,3,2,1,0:T(8,128)(2,1)}, u32[]{:S(2)}) copy-start(bf16[1,1,16,48,1024]{4,3,2,1,0:T(8,128)(2,1)} %param.13) | copy-start | bytes 4718596
  4.2 1.1 copy-start.2
  15.7 10.1 %collective-permute-start.3 = (bf16[8,48,3584]{2,1,0:T(8,128)(2,1)S(1)}, bf16[8,48,3584]{2,1,0:T(8,128)(2,1)S(1)}, u32[]{:S(2)}, u32[]{:S(2)}) collective-permute-start(bf16[8,48,3584]{2,1,0:T(8,128)(2,1)S(1)} %slice_bitcast_fusion), channel_id=1, source_target_pairs={{0,1},{1,0},{2,3},{3,2},{4,5},{5,4},{6,7},{7,6},{8,9},{9,8},{10,11... | collective-permute-start | bytes 8257544 | tf_op jit(solution)/shard_map/ppermute | solution.py:85
  25.2 5.3 %collective-permute-start.2 = (bf16[8,48,3584]{2,1,0:T(8,128)(2,1)S(1)}, bf16[8,48,3584]{2,1,0:T(8,128)(2,1)S(1)}, u32[]{:S(2)}, u32[]{:S(2)}) collective-permute-start(bf16[8,48,3584]{2,1,0:T(8,128)(2,1)S(1)} %slice_bitcast_fusion.2), channel_id=1, source_target_pairs={{0,1},{1,0},{2,3},{3,2},{4,5},{5,4},{6,7},{7,6},{8,9},{9,8},{10,11... | collective-permute-start | bytes 8257544 | tf_op jit(solution)/shard_map/ppermute | solution.py:85
  34.4 6.9 %copy-start.4 = (s32[1,128,2]{1,2,0:T(2,128)S(1)}, s32[1,128,2]{1,2,0:T(2,128)}, u32[]{:S(2)}) copy-start(s32[1,128,2]{1,2,0:T(2,128)} %param.11) | copy-start | bytes 3076
  34.4 6.9 %copy-start.5 = (s32[1,128,2]{1,2,0:T(2,128)S(1)}, s32[1,128,2]{1,2,0:T(2,128)}, u32[]{:S(2)}) copy-start(s32[1,128,2]{1,2,0:T(2,128)} %param.9) | copy-start | bytes 3076
  34.4 69.8 %all-to-all-start = ((bf16[8,48,7168]{2,1,0:T(8,128)(2,1)}), bf16[8,48,7168]{2,1,0:T(8,128)(2,1)}, u32[]{:S(2)}, u32[]{:S(2)}) async-start(bf16[8,48,7168]{2,1,0:T(8,128)(2,1)} %pad_maximum_fusion), calls=%async_computation | async-start | bytes 11010048 | tf_op jit(solution)/shard_map/all_to_all | solution.py:88
  41.4 62.7 %collective-permute-start.1 = (bf16[128,7168]{1,0:T(8,128)(2,1)}, bf16[128,7168]{1,0:T(8,128)(2,1)S(1)}, u32[]{:S(2)}, u32[]{:S(2)}) collective-permute-start(bf16[128,7168]{1,0:T(8,128)(2,1)} %bitcast.91), channel_id=1, source_target_pairs={{0,18},{2,16},{16,34},{18,32},{32,50},{34,48},{48,66},{50,64},{64,... | collective-permute-start | bytes 5505032 | tf_op jit(solution)/shard_map/ppermute | solution.py:73
  41.4 60.5 %collective-permute-start = (s32[128,4]{0,1:T(4,128)S(1)}, s32[128,4]{0,1:T(4,128)S(1)}, u32[]{:S(2)}, u32[]{:S(2)}) collective-permute-start(s32[128,4]{0,1:T(4,128)S(1)} %pad_add_fusion), channel_id=1, source_target_pairs={{0,2},{2,0},{1,3},{3,1},{4,6},{6,4},{5,7},{7,5},{8,10},{10,8},{9,1... | collective-permute-start | bytes 6152 | tf_op jit(solution)/shard_map/ppermute | solution.py:23
  176.5 7.9 %collective-permute-start.4 = (bf16[4,48,7168]{2,1,0:T(8,128)(2,1)}, bf16[4,48,7168]{2,1,0:T(8,128)(2,1)}, u32[]{:S(2)}, u32[]{:S(2)}) collective-permute-start(bf16[4,48,7168]{2,1,0:T(8,128)(2,1)} %get-tuple-element.17), channel_id=1, source_target_pairs={{0,1},{1,0},{2,3},{3,2},{4,5},{5,4},{6,7},{7,6},{8,9},{9,8},{10,11... | collective-permute-start | bytes 8257544 | tf_op jit(solution)/shard_map/ppermute | solution.py:98
  177.0 19.9 %collective-permute-start.5 = (bf16[4,48,7168]{2,1,0:T(8,128)(2,1)}, bf16[4,48,7168]{2,1,0:T(8,128)(2,1)}, u32[]{:S(2)}, u32[]{:S(2)}) collective-permute-start(bf16[4,48,7168]{2,1,0:T(8,128)(2,1)} %get-tuple-element.18), channel_id=1, source_target_pairs={{0,1},{1,0},{2,3},{3,2},{4,5},{5,4},{6,7},{7,6},{8,9},{9,8},{10,11... | collective-permute-start | bytes 8257544 | tf_op jit(solution)/shard_map/ppermute | solution.py:99
  179.3 17.6 %slice-start = ((s8[14680064]{0:T(1024)(128)(4,1)}), s8[4194304]{0:T(1024)(128)(4,1)S(1)}, s32[]{:S(2)}) async-start(s8[14680064]{0:T(1024)(128)(4,1)} %bitcast.89), calls=%async_computation.2 | async-start | bytes 8388608
  184.4 12.5 %copy-start.3 = (bf16[4,48,7168]{2,1,0:T(8,128)(2,1)S(1)}, bf16[4,48,7168]{2,1,0:T(8,128)(2,1)}, u32[]{:S(2)}) copy-start(bf16[4,48,7168]{2,1,0:T(8,128)(2,1)} %get-tuple-element.18) | copy-start | bytes 8257540
  184.4 12.5 %slice-start.1 = ((s8[14680064]{0:T(1024)(128)(4,1)}), s8[4194304]{0:T(1024)(128)(4,1)S(1)}, s32[]{:S(2)}) async-start(s8[14680064]{0:T(1024)(128)(4,1)} %bitcast.89), calls=%async_computation.3 | async-start | bytes 8388608
  184.4 12.5 %slice-start.2 = ((s8[14680064]{0:T(1024)(128)(4,1)}), s8[4194304]{0:T(1024)(128)(4,1)S(1)}, s32[]{:S(2)}) async-start(s8[14680064]{0:T(1024)(128)(4,1)} %bitcast.89), calls=%async_computation.4 | async-start | bytes 8388608
  184.4 12.5 %slice-start.3 = ((s8[14680064]{0:T(1024)(128)(4,1)}), s8[2097152]{0:T(1024)(128)(4,1)S(1)}, s32[]{:S(2)}) async-start(s8[14680064]{0:T(1024)(128)(4,1)} %bitcast.89), calls=%async_computation.5 | async-start | bytes 4194304
  184.4 45.9 %collective-permute-start.6 = (bf16[128,7168]{1,0:T(8,128)(2,1)}, bf16[128,7168]{1,0:T(8,128)(2,1)}, u32[]{:S(2)}, u32[]{:S(2)}) collective-permute-start(bf16[128,7168]{1,0:T(8,128)(2,1)} %fusion.4), channel_id=1, source_target_pairs={{0,114},{2,112},{16,2},{18,0},{32,18},{34,16},{48,34},{50,32},{64,... | collective-permute-start | bytes 5505032 | tf_op jit(solution)/shard_map/ppermute | solution.py:105
  205.2 27.9 %copy-start.1 = (bf16[1,1,16,48,1024]{4,3,2,1,0:T(8,128)(2,1)S(1)}, bf16[1,1,16,48,1024]{4,3,2,1,0:T(8,128)(2,1)}, u32[]{:S(2)}) copy-start(bf16[1,1,16,48,1024]{4,3,2,1,0:T(8,128)(2,1)} %param.13) | copy-start | bytes 4718596

commit v16 on v15

--- a/solution.py
+++ b/solution.py
@@ -98,11 +98,21 @@
         partner_a = lax.ppermute(arrived[:half], "core", [(0, 1), (1, 0)])
         partner_b = lax.ppermute(arrived[half:], "core", [(0, 1), (1, 0)])
         bwd_table = slot_table(bwd_ids, experts, capacity).astype(jnp.bfloat16)
-        grad_in = jnp.einsum(
-            "ect,ecd->td", bwd_table, returned, preferred_element_type=jnp.float32
-        ).astype(jnp.bfloat16)
-        grad_in, partner_a = lax.optimization_barrier((grad_in, partner_a))
-        grad_rows = lax.ppermute(grad_in, RING, ring_route(sections, -1))
+        grad_in = [
+            jnp.einsum(
+                "ect,ecd->td", bwd_table, returned[..., start : start + width],
+                preferred_element_type=jnp.float32,
+            ).astype(jnp.bfloat16)
+            for start in (0, width)
+        ]
+        first, partner_a = lax.optimization_barrier((grad_in[0], partner_a))
+        grad_rows = jnp.concatenate(
+            [
+                lax.ppermute(first, RING, ring_route(sections, -1)),
+                lax.ppermute(grad_in[1], RING, ring_route(sections, -1)),
+            ],
+            axis=-1,
+        )
 
         projected = jnp.concatenate(
             [

time: 234 us -> 232 us (level)
  waiting for transfers between devices: 86.8 us -> 80.2 us
  local copies, waits for them, and re-layouts: 13 us -> 10.1 us
  other arithmetic: 9.91 us -> 12.8 us
  starting transfers between devices: 10.7 us -> 13.2 us
    ppermute x1 -> x2, waiting for transfers between devices: 23.4 us -> 16.8 us  [the longest x1 16.8 us: shards(): lax.ppermute(first, RING, ring_route(sections, -1))]
    unnamed x23 -> x22, local copies, waits for them, and re-layouts: 4.12 us -> 1.28 us
    concatenate x0 -> x1, other arithmetic: none -> 2.84 us  [shards(): jnp.concatenate([lax.ppermute(first, RING, ring_route(sections, -1)), lax...]
    ppermute x1 -> x2, starting transfers between devices: 1.23 us -> 3.78 us  [the longest x1 2.85 us: shards(): lax.ppermute(first, RING, ring_route(sections, -1))]
    dot_general x1 -> x2, matrix products: 5.1 us -> 6.91 us  [shards(): jnp.einsum('ect,ecd->td', bwd_table, returned[..., start:start + width],...]
  transfers between devices with their start and end apart: 8 -> 9, of which waited for: 4 -> 4; matrix products, arithmetic and copies ran while one was open for 17% -> 18% of each run, Pallas kernels for 0% -> 0%
where the time goes in v16:
time: 232 us; the launch traced here: 231 us
  waiting for transfers between devices  80.2 us (35%)
  blocking collectives  67.6 us (29%)
  matrix products  46.1 us (20%)
  starting transfers between devices  13.2 us (6%)
  other arithmetic  12.8 us (6%)
  local copies, waits for them, and re-layouts  10.1 us (4%)
    all_to_all x1, blocking collectives, shards(): lax.all_to_all(picked, CHIPS, split_axis=0, concat_axis=0, tiled=True)  67.6 us
    ppermute x1, waiting for transfers between devices, swap_ylo(): return lax.ppermute(block, 'ylo', [(0, 1), (1, 0)])  59.2 us
    dot_general x2, matrix products, shards(): jnp.einsum('kech,dh->kecd', grad_pre, cols, preferred_element_type=jnp.fl...  18.4 us
    ppermute x1, waiting for transfers between devices, shards(): lax.ppermute(first, RING, ring_route(sections, -1))  16.8 us
    dot_general x1, matrix products, shards(): jnp.einsum('scd,dh->sch', jnp.concatenate([arrived[:half], partner_a]), w...  11.5 us
    dot_general x1, matrix products, shards(): jnp.einsum('scd,dh->sch', jnp.concatenate([arrived[half:], partner_b]), w...  7.75 us
    all_to_all x1, starting transfers between devices, shards(): lax.all_to_all(pair_sum, CHIPS, split_axis=0, concat_axis=0, tiled=True)  6.91 us
    dot_general x2, matrix products, shards(): jnp.einsum('ect,ecd->td', bwd_table, returned[..., start:start + width],...  6.91 us
  transfers between devices with their start and end apart: 9, of which 4 were waited for; matrix products, arithmetic and copies ran while one was open for 18% of the time, Pallas kernels for 0%

profile of v16, /device:TPU:30, one launch (start us, length us, event | category | flops | bytes accessed | tf_op | source)
XLA Modules:
  0.0 231.1 jit_solution(103107562732239709)
XLA Ops:
  0.9 2.7 %gather_fusion.1 = bf16[16,48,512]{2,1,0:T(8,128)(2,1)} fusion(bf16[16,48,512]{2,1,0:T(8,128)(2,1)} %bitcast.87, s32[1024]{0:T(1024)S(1)} %pad_clamp_fusion.2), kind=kCustom, calls=%fused_computation.clone | custom fusion | bytes 1572928 | tf_op jit(solution)/shard_map/jit(_take)/gather | solution.py:76
  3.6 0.6 gather_fusion
  4.5 0.8 copy-done.2
  5.4 0.9 fusion.31
  6.3 9.2 %fusion.13 = bf16[2,8,48,3584]{3,2,1,0:T(8,128)(2,1)S(1)} fusion(bf16[1,1,7168,1024]{3,2,1,0:T(8,128)(2,1)} %param.10, bf16[2,8,48,512]{3,2,1,0:T(8,128)(2,1)S(1)} %bitcast.91, bf16[2,8,48,512]{3,2,1,0:T(8,128)(2,1)S(1)} %bitcast.89), kind=kOutput, calls=%fused_computation.15 | convolution fusion | flops 5643042816 | bytes 14417920 | tf_op jit(solution)/shard_map/kech,dh->kecd/dot_general | solution.py:82
  15.8 9.2 %fusion.10 = bf16[2,8,48,3584]{3,2,1,0:T(8,128)(2,1)S(1)} fusion(bf16[1,1,7168,1024]{3,2,1,0:T(8,128)(2,1)} %param.10, bf16[2,8,48,512]{3,2,1,0:T(8,128)(2,1)S(1)} %bitcast.92, bf16[2,8,48,512]{3,2,1,0:T(8,128)(2,1)S(1)} %bitcast.90), kind=kOutput, calls=%fused_computation.14 | convolution fusion | flops 5643042816 | bytes 14417920 | tf_op jit(solution)/shard_map/kech,dh->kecd/dot_general | solution.py:82
  25.2 0.6 collective-permute-start.2
  25.7 0.7 fusion.22
  26.4 4.0 %collective-permute-done.2 = bf16[8,48,3584]{2,1,0:T(8,128)(2,1)S(1)} collective-permute-done((bf16[8,48,3584]{2,1,0:T(8,128)(2,1)S(1)}, bf16[8,48,3584]{2,1,0:T(8,128)(2,1)S(1)}, u32[]{:S(2)}, u32[]{:S(2)}) %collective-permute-start.2) | collective-permute-done | bytes 2752544 | tf_op jit(solution)/shard_map/ppermute | solution.py:85
  30.5 0.7 fusion.23
  31.2 3.2 %pad_maximum_fusion = bf16[8,48,7168]{2,1,0:T(8,128)(2,1)} fusion(bf16[8,48,3584]{2,1,0:T(8,128)(2,1)S(1)} %fusion.22, bf16[8,48,3584]{2,1,0:T(8,128)(2,1)S(1)} %fusion.23), kind=kLoop, calls=%fused_computation.16 | loop fusion | flops 11010048 | bytes 11010048 | tf_op jit(solution)/shard_map/concatenate | solution.py:87
  34.4 6.9 %all-to-all-start = ((bf16[8,48,7168]{2,1,0:T(8,128)(2,1)}), bf16[8,48,7168]{2,1,0:T(8,128)(2,1)}, u32[]{:S(2)}, u32[]{:S(2)}) async-start(bf16[8,48,7168]{2,1,0:T(8,128)(2,1)} %pad_maximum_fusion), calls=%async_computation | async-start | bytes 11010048 | tf_op jit(solution)/shard_map/all_to_all | solution.py:88
  41.4 1.3 collective-permute-start
  42.7 59.2 %collective-permute-done = s32[128,4]{0,1:T(4,128)S(1)} collective-permute-done((s32[128,4]{0,1:T(4,128)S(1)}, s32[128,4]{0,1:T(4,128)S(1)}, u32[]{:S(2)}, u32[]{:S(2)}) %collective-permute-start) | collective-permute-done | bytes 2080 | tf_op jit(solution)/shard_map/ppermute | solution.py:23
  102.3 0.6 reduce-window.14
  104.3 1.6 convolution_convert_fusion
  105.9 67.6 %all_to_all.10 = bf16[8,48,7168]{2,1,0:T(8,128)(2,1)S(1)} all-to-all(bf16[8,48,7168]{2,1,0:T(8,128)(2,1)S(1)} %convolution_convert_fusion), channel_id=1, replica_groups=mesh['x'=4,'yhi'=2,'z'=4,'ylo'=2,'core'=2] {'z','ylo'}, dimensions={0} | all-to-all | bytes 11010048 | tf_op jit(solution)/shard_map/all_to_all | solution.py:95
  173.5 3.0 %fusion.68 = (bf16[4,48,7168]{2,1,0:T(8,128)(2,1)}, bf16[4,48,7168]{2,1,0:T(8,128)(2,1)}) fusion(bf16[8,48,7168]{2,1,0:T(8,128)(2,1)S(1)} %all_to_all.10), kind=kLoop, calls=%fused_computation.137 | loop fusion | bytes 11010048 | tf_op jit(solution)/shard_map/slice | solution.py:121
  176.9 0.6 reduce-window.16
  177.4 0.6 collective-permute-start.5
  178.8 0.3 bitcast_reduce_fusion
  179.3 3.4 %fusion.25 = bf16[128,3584]{1,0:T(8,128)(2,1)} fusion(bf16[8,48,7168]{2,1,0:T(8,128)(2,1)} %all-to-all-done, bf16[128,8,48]{0,2,1:T(8,128)(2,1)S(1)} %copy.31), kind=kOutput, calls=%fused_computation.30 | convolution fusion | flops 352780288 | bytes 3768320 | tf_op jit(solution)/shard_map/ect,ecd->td/dot_general | solution.py:102
  182.7 0.9 collective-permute-start.7
  183.6 3.5 %fusion.24 = bf16[128,3584]{1,0:T(8,128)(2,1)} fusion(bf16[8,48,7168]{2,1,0:T(8,128)(2,1)} %all-to-all-done, bf16[128,8,48]{0,2,1:T(8,128)(2,1)S(1)} %copy.31), kind=kOutput, calls=%fused_computation.29 | convolution fusion | flops 352780288 | bytes 3768320 | tf_op jit(solution)/shard_map/ect,ecd->td/dot_general | solution.py:102
  187.2 2.8 %collective-permute-start.6 = (bf16[128,3584]{1,0:T(8,128)(2,1)}, bf16[128,3584]{1,0:T(8,128)(2,1)}, u32[]{:S(2)}, u32[]{:S(2)}) collective-permute-start(bf16[128,3584]{1,0:T(8,128)(2,1)} %fusion.24), channel_id=1, source_target_pairs={{0,114},{2,112},{16,2},{18,0},{32,18},{34,16},{48,34},{50,32},{64,... | collective-permute-start | bytes 2752520 | tf_op jit(solution)/shard_map/ppermute | solution.py:111
  190.0 11.5 %fusion.2 = f32[8,48,1024]{2,1,0:T(8,128)S(1)} fusion(bf16[1,1,7168,1024]{3,2,1,0:T(8,128)(2,1)} %param.10, bf16[4,48,7168]{2,1,0:T(8,128)(2,1)} %collective-permute-done.4, bf16[4,48,7168]{2,1,0:T(8,128)(2,1)} %get-tuple-element.17), kind=kOutput, calls=%fused_computation.5 | convolution fusion | flops 5639897088 | bytes 21757952 | tf_op jit(solution)/shard_map/scd,dh->sch/dot_general | solution.py:119
  201.5 7.8 %fusion = f32[8,48,1024]{2,1,0:T(8,128)S(1)} fusion(bf16[1,1,7168,1024]{3,2,1,0:T(8,128)(2,1)S(1)} %bitcast.96, bf16[4,48,7168]{2,1,0:T(8,128)(2,1)} %collective-permute-done.5, bf16[4,48,7168]{2,1,0:T(8,128)(2,1)S(1)} %copy-done.3), kind=kOutput, calls=%fused_computation.3 | convolution fusion | flops 5639897088 | bytes 21757952 | tf_op jit(solution)/shard_map/scd,dh->sch/dot_general | solution.py:125
  209.3 0.5 fusion.36
  209.8 0.6 gather_fusion.2
  210.4 1.0 broadcast_select_fusion
  211.5 16.8 %collective-permute-done.6 = bf16[128,3584]{1,0:T(8,128)(2,1)} collective-permute-done((bf16[128,3584]{1,0:T(8,128)(2,1)}, bf16[128,3584]{1,0:T(8,128)(2,1)}, u32[]{:S(2)}, u32[]{:S(2)}) %collective-permute-start.6) | collective-permute-done | bytes 917536 | tf_op jit(solution)/shard_map/ppermute | solution.py:111
  228.2 2.8 %pad_maximum_fusion.1 = bf16[128,7168]{1,0:T(8,128)(2,1)} fusion(bf16[128,3584]{1,0:T(8,128)(2,1)} %collective-permute-done.7, bf16[128,3584]{1,0:T(8,128)(2,1)} %collective-permute-done.6), kind=kLoop, calls=%fused_computation.41 | loop fusion | flops 3670016 | bytes 3670016 | tf_op jit(solution)/shard_map/concatenate | solution.py:109
  (68 shorter events, 3.9 us)
Async XLA Ops:
  0.6 2.9 %copy-start = (bf16[1,1,16,48,1024]{4,3,2,1,0:T(8,128)(2,1)S(1)}, bf16[1,1,16,48,1024]{4,3,2,1,0:T(8,128)(2,1)}, u32[]{:S(2)}) copy-start(bf16[1,1,16,48,1024]{4,3,2,1,0:T(8,128)(2,1)} %param.13) | copy-start | bytes 4718596
  4.2 1.1 copy-start.2
  15.7 10.1 %collective-permute-start.3 = (bf16[8,48,3584]{2,1,0:T(8,128)(2,1)S(1)}, bf16[8,48,3584]{2,1,0:T(8,128)(2,1)S(1)}, u32[]{:S(2)}, u32[]{:S(2)}) collective-permute-start(bf16[8,48,3584]{2,1,0:T(8,128)(2,1)S(1)} %slice_bitcast_fusion), channel_id=1, source_target_pairs={{0,1},{1,0},{2,3},{3,2},{4,5},{5,4},{6,7},{7,6},{8,9},{9,8},{10,11... | collective-permute-start | bytes 8257544 | tf_op jit(solution)/shard_map/ppermute | solution.py:85
  25.2 5.3 %collective-permute-start.2 = (bf16[8,48,3584]{2,1,0:T(8,128)(2,1)S(1)}, bf16[8,48,3584]{2,1,0:T(8,128)(2,1)S(1)}, u32[]{:S(2)}, u32[]{:S(2)}) collective-permute-start(bf16[8,48,3584]{2,1,0:T(8,128)(2,1)S(1)} %slice_bitcast_fusion.2), channel_id=1, source_target_pairs={{0,1},{1,0},{2,3},{3,2},{4,5},{5,4},{6,7},{7,6},{8,9},{9,8},{10,11... | collective-permute-start | bytes 8257544 | tf_op jit(solution)/shard_map/ppermute | solution.py:85
  34.4 6.9 %copy-start.4 = (s32[1,128,2]{1,2,0:T(2,128)S(1)}, s32[1,128,2]{1,2,0:T(2,128)}, u32[]{:S(2)}) copy-start(s32[1,128,2]{1,2,0:T(2,128)} %param.11) | copy-start | bytes 3076
  34.4 6.9 %copy-start.5 = (s32[1,128,2]{1,2,0:T(2,128)S(1)}, s32[1,128,2]{1,2,0:T(2,128)}, u32[]{:S(2)}) copy-start(s32[1,128,2]{1,2,0:T(2,128)} %param.9) | copy-start | bytes 3076
  34.4 69.8 %all-to-all-start = ((bf16[8,48,7168]{2,1,0:T(8,128)(2,1)}), bf16[8,48,7168]{2,1,0:T(8,128)(2,1)}, u32[]{:S(2)}, u32[]{:S(2)}) async-start(bf16[8,48,7168]{2,1,0:T(8,128)(2,1)} %pad_maximum_fusion), calls=%async_computation | async-start | bytes 11010048 | tf_op jit(solution)/shard_map/all_to_all | solution.py:88
  41.3 62.7 %collective-permute-start.1 = (bf16[128,7168]{1,0:T(8,128)(2,1)}, bf16[128,7168]{1,0:T(8,128)(2,1)S(1)}, u32[]{:S(2)}, u32[]{:S(2)}) collective-permute-start(bf16[128,7168]{1,0:T(8,128)(2,1)} %bitcast.97), channel_id=1, source_target_pairs={{0,18},{2,16},{16,34},{18,32},{32,50},{34,48},{48,66},{50,64},{64,... | collective-permute-start | bytes 5505032 | tf_op jit(solution)/shard_map/ppermute | solution.py:73
  41.4 60.5 %collective-permute-start = (s32[128,4]{0,1:T(4,128)S(1)}, s32[128,4]{0,1:T(4,128)S(1)}, u32[]{:S(2)}, u32[]{:S(2)}) collective-permute-start(s32[128,4]{0,1:T(4,128)S(1)} %pad_add_fusion), channel_id=1, source_target_pairs={{0,2},{2,0},{1,3},{3,1},{4,6},{6,4},{5,7},{7,5},{8,10},{10,8},{9,1... | collective-permute-start | bytes 6152 | tf_op jit(solution)/shard_map/ppermute | solution.py:23
  176.5 10.6 %collective-permute-start.4 = (bf16[4,48,7168]{2,1,0:T(8,128)(2,1)}, bf16[4,48,7168]{2,1,0:T(8,128)(2,1)}, u32[]{:S(2)}, u32[]{:S(2)}) collective-permute-start(bf16[4,48,7168]{2,1,0:T(8,128)(2,1)} %get-tuple-element.17), channel_id=1, source_target_pairs={{0,1},{1,0},{2,3},{3,2},{4,5},{5,4},{6,7},{7,6},{8,9},{9,8},{10,11... | collective-permute-start | bytes 8257544 | tf_op jit(solution)/shard_map/ppermute | solution.py:98
  177.4 24.0 %collective-permute-start.5 = (bf16[4,48,7168]{2,1,0:T(8,128)(2,1)}, bf16[4,48,7168]{2,1,0:T(8,128)(2,1)}, u32[]{:S(2)}, u32[]{:S(2)}) collective-permute-start(bf16[4,48,7168]{2,1,0:T(8,128)(2,1)} %get-tuple-element.18), channel_id=1, source_target_pairs={{0,1},{1,0},{2,3},{3,2},{4,5},{5,4},{6,7},{7,6},{8,9},{9,8},{10,11... | collective-permute-start | bytes 8257544 | tf_op jit(solution)/shard_map/ppermute | solution.py:99
  182.7 28.8 %collective-permute-start.7 = (bf16[128,3584]{1,0:T(8,128)(2,1)}, bf16[128,3584]{1,0:T(8,128)(2,1)}, u32[]{:S(2)}, u32[]{:S(2)}) collective-permute-start(bf16[128,3584]{1,0:T(8,128)(2,1)} %fusion.25), channel_id=1, source_target_pairs={{0,114},{2,112},{16,2},{18,0},{32,18},{34,16},{48,34},{50,32},{64,... | collective-permute-start | bytes 2752520 | tf_op jit(solution)/shard_map/ppermute | solution.py:112
  183.6 17.9 %slice-start = ((s8[14680064]{0:T(1024)(128)(4,1)}), s8[4194304]{0:T(1024)(128)(4,1)S(1)}, s32[]{:S(2)}) async-start(s8[14680064]{0:T(1024)(128)(4,1)} %bitcast.95), calls=%async_computation.2 | async-start | bytes 8388608
  187.1 14.4 %copy-start.3 = (bf16[4,48,7168]{2,1,0:T(8,128)(2,1)S(1)}, bf16[4,48,7168]{2,1,0:T(8,128)(2,1)}, u32[]{:S(2)}) copy-start(bf16[4,48,7168]{2,1,0:T(8,128)(2,1)} %get-tuple-element.18) | copy-start | bytes 8257540
  187.1 14.4 %slice-start.1 = ((s8[14680064]{0:T(1024)(128)(4,1)}), s8[4194304]{0:T(1024)(128)(4,1)S(1)}, s32[]{:S(2)}) async-start(s8[14680064]{0:T(1024)(128)(4,1)} %bitcast.95), calls=%async_computation.3 | async-start | bytes 8388608
  187.1 14.4 %slice-start.2 = ((s8[14680064]{0:T(1024)(128)(4,1)}), s8[4194304]{0:T(1024)(128)(4,1)S(1)}, s32[]{:S(2)}) async-start(s8[14680064]{0:T(1024)(128)(4,1)} %bitcast.95), calls=%async_computation.4 | async-start | bytes 8388608
  187.1 14.4 %slice-start.3 = ((s8[14680064]{0:T(1024)(128)(4,1)}), s8[2097152]{0:T(1024)(128)(4,1)S(1)}, s32[]{:S(2)}) async-start(s8[14680064]{0:T(1024)(128)(4,1)} %bitcast.95), calls=%async_computation.5 | async-start | bytes 4194304
  187.2 41.1 %collective-permute-start.6 = (bf16[128,3584]{1,0:T(8,128)(2,1)}, bf16[128,3584]{1,0:T(8,128)(2,1)}, u32[]{:S(2)}, u32[]{:S(2)}) collective-permute-start(bf16[128,3584]{1,0:T(8,128)(2,1)} %fusion.24), channel_id=1, source_target_pairs={{0,114},{2,112},{16,2},{18,0},{32,18},{34,16},{48,34},{50,32},{64,... | collective-permute-start | bytes 2752520 | tf_op jit(solution)/shard_map/ppermute | solution.py:111
  209.8 21.2 %copy-start.1 = (bf16[1,1,16,48,1024]{4,3,2,1,0:T(8,128)(2,1)S(1)}, bf16[1,1,16,48,1024]{4,3,2,1,0:T(8,128)(2,1)}, u32[]{:S(2)}) copy-start(bf16[1,1,16,48,1024]{4,3,2,1,0:T(8,128)(2,1)} %param.13) | copy-start | bytes 4718596

commit v17 on v16

--- a/solution.py
+++ b/solution.py
@@ -98,20 +98,17 @@
         partner_a = lax.ppermute(arrived[:half], "core", [(0, 1), (1, 0)])
         partner_b = lax.ppermute(arrived[half:], "core", [(0, 1), (1, 0)])
         bwd_table = slot_table(bwd_ids, experts, capacity).astype(jnp.bfloat16)
+        piece = model_width // 4
         grad_in = [
             jnp.einsum(
-                "ect,ecd->td", bwd_table, returned[..., start : start + width],
+                "ect,ecd->td", bwd_table, returned[..., start : start + piece],
                 preferred_element_type=jnp.float32,
             ).astype(jnp.bfloat16)
-            for start in (0, width)
+            for start in range(0, model_width, piece)
         ]
-        first, partner_a = lax.optimization_barrier((grad_in[0], partner_a))
+        grad_in[0], partner_a = lax.optimization_barrier((grad_in[0], partner_a))
         grad_rows = jnp.concatenate(
-            [
-                lax.ppermute(first, RING, ring_route(sections, -1)),
-                lax.ppermute(grad_in[1], RING, ring_route(sections, -1)),
-            ],
-            axis=-1,
+            [lax.ppermute(g, RING, ring_route(sections, -1)) for g in grad_in], axis=-1
         )
 
         projected = jnp.concatenate(

time: 232 us -> 231 us (level)
  waiting for transfers between devices: 80.2 us -> 72.7 us
  matrix products: 46.1 us -> 49.6 us
  starting transfers between devices: 13.2 us -> 16.5 us
    ppermute x2 -> x4, waiting for transfers between devices: 16.8 us -> 9.26 us  [shards(): lax.ppermute(g, RING, ring_route(sections, -1))]
    dot_general x2 -> x4, matrix products: 6.91 us -> 10.4 us  [shards(): jnp.einsum('ect,ecd->td', bwd_table, returned[..., start:start + piece],...]
    ppermute x2 -> x4, starting transfers between devices: 3.78 us -> 6.98 us  [shards(): lax.ppermute(g, RING, ring_route(sections, -1))]
  transfers between devices with their start and end apart: 9 -> 11, of which waited for: 4 -> 5; matrix products, arithmetic and copies ran while one was open for 18% -> 20% of each run, Pallas kernels for 0% -> 0%
where the time goes in v17:
time: 231 us; the launch traced here: 230 us
  waiting for transfers between devices  72.7 us (31%)
  blocking collectives  67.6 us (29%)
  matrix products  49.6 us (21%)
  starting transfers between devices  16.5 us (7%)
  other arithmetic  12.8 us (6%)
  local copies, waits for them, and re-layouts  10.1 us (4%)
    all_to_all x1, blocking collectives, shards(): lax.all_to_all(picked, CHIPS, split_axis=0, concat_axis=0, tiled=True)  67.6 us
    ppermute x1, waiting for transfers between devices, swap_ylo(): return lax.ppermute(block, 'ylo', [(0, 1), (1, 0)])  59.2 us
    dot_general x2, matrix products, shards(): jnp.einsum('kech,dh->kecd', grad_pre, cols, preferred_element_type=jnp.fl...  18.4 us
    dot_general x1, matrix products, shards(): jnp.einsum('scd,dh->sch', jnp.concatenate([arrived[:half], partner_a]), w...  11.5 us
    dot_general x4, matrix products, shards(): jnp.einsum('ect,ecd->td', bwd_table, returned[..., start:start + piece],...  10.4 us
    ppermute x4, waiting for transfers between devices, shards(): lax.ppermute(g, RING, ring_route(sections, -1))  9.26 us
    dot_general x1, matrix products, shards(): jnp.einsum('scd,dh->sch', jnp.concatenate([arrived[half:], partner_b]), w...  7.75 us
    ppermute x4, starting transfers between devices, shards(): lax.ppermute(g, RING, ring_route(sections, -1))  6.98 us
  transfers between devices with their start and end apart: 11, of which 5 were waited for; matrix products, arithmetic and copies ran while one was open for 20% of the time, Pallas kernels for 0%

profile of v17, /device:TPU:30, one launch (start us, length us, event | category | flops | bytes accessed | tf_op | source)
XLA Modules:
  0.0 230.3 jit_solution(6590327760775264695)
XLA Ops:
  0.9 2.7 %gather_fusion.1 = bf16[16,48,512]{2,1,0:T(8,128)(2,1)} fusion(bf16[16,48,512]{2,1,0:T(8,128)(2,1)} %bitcast.99, s32[1024]{0:T(1024)S(1)} %pad_clamp_fusion.2), kind=kCustom, calls=%fused_computation.clone | custom fusion | bytes 1572928 | tf_op jit(solution)/shard_map/jit(_take)/gather | solution.py:76
  3.6 0.6 gather_fusion
  4.5 0.8 copy-done.2
  5.4 0.9 fusion.31
  6.3 9.2 %fusion.13 = bf16[2,8,48,3584]{3,2,1,0:T(8,128)(2,1)S(1)} fusion(bf16[1,1,7168,1024]{3,2,1,0:T(8,128)(2,1)} %param.10, bf16[2,8,48,512]{3,2,1,0:T(8,128)(2,1)S(1)} %bitcast.103, bf16[2,8,48,512]{3,2,1,0:T(8,128)(2,1)S(1)} %bitcast.101), kind=kOutput, calls=%fused_computation.15 | convolution fusion | flops 5643042816 | bytes 14417920 | tf_op jit(solution)/shard_map/kech,dh->kecd/dot_general | solution.py:82
  15.8 9.2 %fusion.10 = bf16[2,8,48,3584]{3,2,1,0:T(8,128)(2,1)S(1)} fusion(bf16[1,1,7168,1024]{3,2,1,0:T(8,128)(2,1)} %param.10, bf16[2,8,48,512]{3,2,1,0:T(8,128)(2,1)S(1)} %bitcast.104, bf16[2,8,48,512]{3,2,1,0:T(8,128)(2,1)S(1)} %bitcast.102), kind=kOutput, calls=%fused_computation.14 | convolution fusion | flops 5643042816 | bytes 14417920 | tf_op jit(solution)/shard_map/kech,dh->kecd/dot_general | solution.py:82
  25.7 0.7 fusion.22
  26.4 4.0 %collective-permute-done.2 = bf16[8,48,3584]{2,1,0:T(8,128)(2,1)S(1)} collective-permute-done((bf16[8,48,3584]{2,1,0:T(8,128)(2,1)S(1)}, bf16[8,48,3584]{2,1,0:T(8,128)(2,1)S(1)}, u32[]{:S(2)}, u32[]{:S(2)}) %collective-permute-start.2) | collective-permute-done | bytes 2752544 | tf_op jit(solution)/shard_map/ppermute | solution.py:85
  30.5 0.7 fusion.23
  31.2 3.2 %pad_maximum_fusion = bf16[8,48,7168]{2,1,0:T(8,128)(2,1)} fusion(bf16[8,48,3584]{2,1,0:T(8,128)(2,1)S(1)} %fusion.22, bf16[8,48,3584]{2,1,0:T(8,128)(2,1)S(1)} %fusion.23), kind=kLoop, calls=%fused_computation.16 | loop fusion | flops 11010048 | bytes 11010048 | tf_op jit(solution)/shard_map/concatenate | solution.py:87
  34.4 6.9 %all-to-all-start = ((bf16[8,48,7168]{2,1,0:T(8,128)(2,1)}), bf16[8,48,7168]{2,1,0:T(8,128)(2,1)}, u32[]{:S(2)}, u32[]{:S(2)}) async-start(bf16[8,48,7168]{2,1,0:T(8,128)(2,1)} %pad_maximum_fusion), calls=%async_computation | async-start | bytes 11010048 | tf_op jit(solution)/shard_map/all_to_all | solution.py:88
  41.4 1.3 collective-permute-start
  42.7 59.2 %collective-permute-done = s32[128,4]{0,1:T(4,128)S(1)} collective-permute-done((s32[128,4]{0,1:T(4,128)S(1)}, s32[128,4]{0,1:T(4,128)S(1)}, u32[]{:S(2)}, u32[]{:S(2)}) %collective-permute-start) | collective-permute-done | bytes 2080 | tf_op jit(solution)/shard_map/ppermute | solution.py:23
  102.4 0.6 reduce-window.14
  104.3 1.6 convolution_convert_fusion
  105.9 67.6 %all_to_all.10 = bf16[8,48,7168]{2,1,0:T(8,128)(2,1)S(1)} all-to-all(bf16[8,48,7168]{2,1,0:T(8,128)(2,1)S(1)} %convolution_convert_fusion), channel_id=1, replica_groups=mesh['x'=4,'yhi'=2,'z'=4,'ylo'=2,'core'=2] {'z','ylo'}, dimensions={0} | all-to-all | bytes 11010048 | tf_op jit(solution)/shard_map/all_to_all | solution.py:95
  173.5 3.0 %fusion.72 = (bf16[4,48,7168]{2,1,0:T(8,128)(2,1)}, bf16[4,48,7168]{2,1,0:T(8,128)(2,1)}) fusion(bf16[8,48,7168]{2,1,0:T(8,128)(2,1)S(1)} %all_to_all.10), kind=kLoop, calls=%fused_computation.143 | loop fusion | bytes 11010048 | tf_op jit(solution)/shard_map/slice | solution.py:118
  177.0 0.6 reduce-window.16
  179.3 2.5 %fusion.25 = bf16[128,1792]{1,0:T(8,128)(2,1)} fusion(bf16[8,48,7168]{2,1,0:T(8,128)(2,1)} %all-to-all-done, bf16[128,8,48]{0,2,1:T(8,128)(2,1)S(1)} %copy.31), kind=kOutput, calls=%fused_computation.38 | convolution fusion | flops 176390144 | bytes 1933312 | tf_op jit(solution)/shard_map/ect,ecd->td/dot_general | solution.py:103
  181.8 1.0 collective-permute-start.7
  182.8 2.6 %fusion.26 = bf16[128,1792]{1,0:T(8,128)(2,1)} fusion(bf16[8,48,7168]{2,1,0:T(8,128)(2,1)} %all-to-all-done, bf16[128,8,48]{0,2,1:T(8,128)(2,1)S(1)} %copy.31), kind=kOutput, calls=%fused_computation.39 | convolution fusion | flops 176390144 | bytes 1933312 | tf_op jit(solution)/shard_map/ect,ecd->td/dot_general | solution.py:103
  185.4 2.5 %collective-permute-start.8 = (bf16[128,1792]{1,0:T(8,128)(2,1)}, bf16[128,1792]{1,0:T(8,128)(2,1)}, u32[]{:S(2)}, u32[]{:S(2)}) collective-permute-start(bf16[128,1792]{1,0:T(8,128)(2,1)} %fusion.26), channel_id=1, source_target_pairs={{0,114},{2,112},{16,2},{18,0},{32,18},{34,16},{48,34},{50,32},{64,... | collective-permute-start | bytes 1376264 | tf_op jit(solution)/shard_map/ppermute | solution.py:111
  187.9 2.5 %fusion.27 = bf16[128,1792]{1,0:T(8,128)(2,1)} fusion(bf16[8,48,7168]{2,1,0:T(8,128)(2,1)} %all-to-all-done, bf16[128,8,48]{0,2,1:T(8,128)(2,1)S(1)} %copy.31), kind=kOutput, calls=%fused_computation.40 | convolution fusion | flops 176390144 | bytes 1933312 | tf_op jit(solution)/shard_map/ect,ecd->td/dot_general | solution.py:103
  190.5 0.9 collective-permute-start.9
  191.4 2.7 %fusion.24 = bf16[128,1792]{1,0:T(8,128)(2,1)} fusion(bf16[8,48,7168]{2,1,0:T(8,128)(2,1)} %all-to-all-done, bf16[128,8,48]{0,2,1:T(8,128)(2,1)S(1)} %copy.31), kind=kOutput, calls=%fused_computation.37 | convolution fusion | flops 176390144 | bytes 1933312 | tf_op jit(solution)/shard_map/ect,ecd->td/dot_general | solution.py:103
  194.1 2.5 %collective-permute-start.6 = (bf16[128,1792]{1,0:T(8,128)(2,1)}, bf16[128,1792]{1,0:T(8,128)(2,1)}, u32[]{:S(2)}, u32[]{:S(2)}) collective-permute-start(bf16[128,1792]{1,0:T(8,128)(2,1)} %fusion.24), channel_id=1, source_target_pairs={{0,114},{2,112},{16,2},{18,0},{32,18},{34,16},{48,34},{50,32},{64,... | collective-permute-start | bytes 1376264 | tf_op jit(solution)/shard_map/ppermute | solution.py:111
  196.7 11.5 %fusion.2 = f32[8,48,1024]{2,1,0:T(8,128)S(1)} fusion(bf16[1,1,7168,1024]{3,2,1,0:T(8,128)(2,1)} %param.10, bf16[4,48,7168]{2,1,0:T(8,128)(2,1)} %collective-permute-done.4, bf16[4,48,7168]{2,1,0:T(8,128)(2,1)} %get-tuple-element.17), kind=kOutput, calls=%fused_computation.5 | convolution fusion | flops 5639897088 | bytes 21757952 | tf_op jit(solution)/shard_map/scd,dh->sch/dot_general | solution.py:116
  208.2 7.8 %fusion = f32[8,48,1024]{2,1,0:T(8,128)S(1)} fusion(bf16[1,1,7168,1024]{3,2,1,0:T(8,128)(2,1)S(1)} %bitcast.108, bf16[4,48,7168]{2,1,0:T(8,128)(2,1)} %collective-permute-done.5, bf16[4,48,7168]{2,1,0:T(8,128)(2,1)S(1)} %copy-done.3), kind=kOutput, calls=%fused_computation.3 | convolution fusion | flops 5639897088 | bytes 21757952 | tf_op jit(solution)/shard_map/scd,dh->sch/dot_general | solution.py:122
  216.5 0.6 gather_fusion.2
  217.1 1.0 broadcast_select_fusion
  218.5 8.9 %collective-permute-done.6 = bf16[128,1792]{1,0:T(8,128)(2,1)} collective-permute-done((bf16[128,1792]{1,0:T(8,128)(2,1)}, bf16[128,1792]{1,0:T(8,128)(2,1)}, u32[]{:S(2)}, u32[]{:S(2)}) %collective-permute-start.6) | collective-permute-done | bytes 458784 | tf_op jit(solution)/shard_map/ppermute | solution.py:111
  227.4 2.8 %pad_maximum_fusion.1 = bf16[128,7168]{1,0:T(8,128)(2,1)} fusion(bf16[128,1792]{1,0:T(8,128)(2,1)} %collective-permute-done.9, bf16[128,1792]{1,0:T(8,128)(2,1)} %collective-permute-done.8, bf16[128,1792]{1,0:T(8,128)(2,1)} %collective-permute-done.7, bf16[128,1792]{1,0:T(8,128)(2,1)} %collective-permute-done.6), kind=kLoop, calls=%fused_computation.43 | loop fusion | flops 7340032 | bytes 3670016 | tf_op jit(solution)/shard_map/concatenate | solution.py:110
  (74 shorter events, 6.3 us)
Async XLA Ops:
  0.6 2.9 %copy-start = (bf16[1,1,16,48,1024]{4,3,2,1,0:T(8,128)(2,1)S(1)}, bf16[1,1,16,48,1024]{4,3,2,1,0:T(8,128)(2,1)}, u32[]{:S(2)}) copy-start(bf16[1,1,16,48,1024]{4,3,2,1,0:T(8,128)(2,1)} %param.13) | copy-start | bytes 4718596
  4.2 1.1 copy-start.2
  15.7 10.1 %collective-permute-start.3 = (bf16[8,48,3584]{2,1,0:T(8,128)(2,1)S(1)}, bf16[8,48,3584]{2,1,0:T(8,128)(2,1)S(1)}, u32[]{:S(2)}, u32[]{:S(2)}) collective-permute-start(bf16[8,48,3584]{2,1,0:T(8,128)(2,1)S(1)} %slice_bitcast_fusion), channel_id=1, source_target_pairs={{0,1},{1,0},{2,3},{3,2},{4,5},{5,4},{6,7},{7,6},{8,9},{9,8},{10,11... | collective-permute-start | bytes 8257544 | tf_op jit(solution)/shard_map/ppermute | solution.py:85
  25.2 5.3 %collective-permute-start.2 = (bf16[8,48,3584]{2,1,0:T(8,128)(2,1)S(1)}, bf16[8,48,3584]{2,1,0:T(8,128)(2,1)S(1)}, u32[]{:S(2)}, u32[]{:S(2)}) collective-permute-start(bf16[8,48,3584]{2,1,0:T(8,128)(2,1)S(1)} %slice_bitcast_fusion.2), channel_id=1, source_target_pairs={{0,1},{1,0},{2,3},{3,2},{4,5},{5,4},{6,7},{7,6},{8,9},{9,8},{10,11... | collective-permute-start | bytes 8257544 | tf_op jit(solution)/shard_map/ppermute | solution.py:85
  34.4 6.9 %copy-start.4 = (s32[1,128,2]{1,2,0:T(2,128)S(1)}, s32[1,128,2]{1,2,0:T(2,128)}, u32[]{:S(2)}) copy-start(s32[1,128,2]{1,2,0:T(2,128)} %param.11) | copy-start | bytes 3076
  34.4 6.9 %copy-start.5 = (s32[1,128,2]{1,2,0:T(2,128)S(1)}, s32[1,128,2]{1,2,0:T(2,128)}, u32[]{:S(2)}) copy-start(s32[1,128,2]{1,2,0:T(2,128)} %param.9) | copy-start | bytes 3076
  34.4 69.8 %all-to-all-start = ((bf16[8,48,7168]{2,1,0:T(8,128)(2,1)}), bf16[8,48,7168]{2,1,0:T(8,128)(2,1)}, u32[]{:S(2)}, u32[]{:S(2)}) async-start(bf16[8,48,7168]{2,1,0:T(8,128)(2,1)} %pad_maximum_fusion), calls=%async_computation | async-start | bytes 11010048 | tf_op jit(solution)/shard_map/all_to_all | solution.py:88
  41.4 62.7 %collective-permute-start.1 = (bf16[128,7168]{1,0:T(8,128)(2,1)}, bf16[128,7168]{1,0:T(8,128)(2,1)S(1)}, u32[]{:S(2)}, u32[]{:S(2)}) collective-permute-start(bf16[128,7168]{1,0:T(8,128)(2,1)} %bitcast.109), channel_id=1, source_target_pairs={{0,18},{2,16},{16,34},{18,32},{32,50},{34,48},{48,66},{50,64},{64,... | collective-permute-start | bytes 5505032 | tf_op jit(solution)/shard_map/ppermute | solution.py:73
  41.4 60.5 %collective-permute-start = (s32[128,4]{0,1:T(4,128)S(1)}, s32[128,4]{0,1:T(4,128)S(1)}, u32[]{:S(2)}, u32[]{:S(2)}) collective-permute-start(s32[128,4]{0,1:T(4,128)S(1)} %pad_add_fusion), channel_id=1, source_target_pairs={{0,2},{2,0},{1,3},{3,1},{4,6},{6,4},{5,7},{7,5},{8,10},{10,8},{9,1... | collective-permute-start | bytes 6152 | tf_op jit(solution)/shard_map/ppermute | solution.py:23
  176.5 17.6 %collective-permute-start.4 = (bf16[4,48,7168]{2,1,0:T(8,128)(2,1)}, bf16[4,48,7168]{2,1,0:T(8,128)(2,1)}, u32[]{:S(2)}, u32[]{:S(2)}) collective-permute-start(bf16[4,48,7168]{2,1,0:T(8,128)(2,1)} %get-tuple-element.17), channel_id=1, source_target_pairs={{0,1},{1,0},{2,3},{3,2},{4,5},{5,4},{6,7},{7,6},{8,9},{9,8},{10,11... | collective-permute-start | bytes 8257544 | tf_op jit(solution)/shard_map/ppermute | solution.py:98
  178.1 30.1 %collective-permute-start.5 = (bf16[4,48,7168]{2,1,0:T(8,128)(2,1)}, bf16[4,48,7168]{2,1,0:T(8,128)(2,1)}, u32[]{:S(2)}, u32[]{:S(2)}) collective-permute-start(bf16[4,48,7168]{2,1,0:T(8,128)(2,1)} %get-tuple-element.18), channel_id=1, source_target_pairs={{0,1},{1,0},{2,3},{3,2},{4,5},{5,4},{6,7},{7,6},{8,9},{9,8},{10,11... | collective-permute-start | bytes 8257544 | tf_op jit(solution)/shard_map/ppermute | solution.py:99
  181.8 36.3 %collective-permute-start.7 = (bf16[128,1792]{1,0:T(8,128)(2,1)}, bf16[128,1792]{1,0:T(8,128)(2,1)}, u32[]{:S(2)}, u32[]{:S(2)}) collective-permute-start(bf16[128,1792]{1,0:T(8,128)(2,1)} %fusion.25), channel_id=1, source_target_pairs={{0,114},{2,112},{16,2},{18,0},{32,18},{34,16},{48,34},{50,32},{64,... | collective-permute-start | bytes 1376264 | tf_op jit(solution)/shard_map/ppermute | solution.py:111
  185.4 32.8 %collective-permute-start.8 = (bf16[128,1792]{1,0:T(8,128)(2,1)}, bf16[128,1792]{1,0:T(8,128)(2,1)}, u32[]{:S(2)}, u32[]{:S(2)}) collective-permute-start(bf16[128,1792]{1,0:T(8,128)(2,1)} %fusion.26), channel_id=1, source_target_pairs={{0,114},{2,112},{16,2},{18,0},{32,18},{34,16},{48,34},{50,32},{64,... | collective-permute-start | bytes 1376264 | tf_op jit(solution)/shard_map/ppermute | solution.py:111
  190.5 28.1 %collective-permute-start.9 = (bf16[128,1792]{1,0:T(8,128)(2,1)}, bf16[128,1792]{1,0:T(8,128)(2,1)}, u32[]{:S(2)}, u32[]{:S(2)}) collective-permute-start(bf16[128,1792]{1,0:T(8,128)(2,1)} %fusion.27), channel_id=1, source_target_pairs={{0,114},{2,112},{16,2},{18,0},{32,18},{34,16},{48,34},{50,32},{64,... | collective-permute-start | bytes 1376264 | tf_op jit(solution)/shard_map/ppermute | solution.py:111
  191.4 16.8 %slice-start = ((s8[14680064]{0:T(1024)(128)(4,1)}), s8[4194304]{0:T(1024)(128)(4,1)S(1)}, s32[]{:S(2)}) async-start(s8[14680064]{0:T(1024)(128)(4,1)} %bitcast.107), calls=%async_computation.2 | async-start | bytes 8388608
  194.1 14.1 %copy-start.3 = (bf16[4,48,7168]{2,1,0:T(8,128)(2,1)S(1)}, bf16[4,48,7168]{2,1,0:T(8,128)(2,1)}, u32[]{:S(2)}) copy-start(bf16[4,48,7168]{2,1,0:T(8,128)(2,1)} %get-tuple-element.18) | copy-start | bytes 8257540
  194.1 14.1 %slice-start.1 = ((s8[14680064]{0:T(1024)(128)(4,1)}), s8[4194304]{0:T(1024)(128)(4,1)S(1)}, s32[]{:S(2)}) async-start(s8[14680064]{0:T(1024)(128)(4,1)} %bitcast.107), calls=%async_computation.3 | async-start | bytes 8388608
  194.1 14.1 %slice-start.2 = ((s8[14680064]{0:T(1024)(128)(4,1)}), s8[4194304]{0:T(1024)(128)(4,1)S(1)}, s32[]{:S(2)}) async-start(s8[14680064]{0:T(1024)(128)(4,1)} %bitcast.107), calls=%async_computation.4 | async-start | bytes 8388608
  194.1 14.1 %slice-start.3 = ((s8[14680064]{0:T(1024)(128)(4,1)}), s8[2097152]{0:T(1024)(128)(4,1)S(1)}, s32[]{:S(2)}) async-start(s8[14680064]{0:T(1024)(128)(4,1)} %bitcast.107), calls=%async_computation.5 | async-start | bytes 4194304
  194.1 33.3 %collective-permute-start.6 = (bf16[128,1792]{1,0:T(8,128)(2,1)}, bf16[128,1792]{1,0:T(8,128)(2,1)}, u32[]{:S(2)}, u32[]{:S(2)}) collective-permute-start(bf16[128,1792]{1,0:T(8,128)(2,1)} %fusion.24), channel_id=1, source_target_pairs={{0,114},{2,112},{16,2},{18,0},{32,18},{34,16},{48,34},{50,32},{64,... | collective-permute-start | bytes 1376264 | tf_op jit(solution)/shard_map/ppermute | solution.py:111
  216.5 13.7 %copy-start.1 = (bf16[1,1,16,48,1024]{4,3,2,1,0:T(8,128)(2,1)S(1)}, bf16[1,1,16,48,1024]{4,3,2,1,0:T(8,128)(2,1)}, u32[]{:S(2)}) copy-start(bf16[1,1,16,48,1024]{4,3,2,1,0:T(8,128)(2,1)} %param.13) | copy-start | bytes 4718596

commit v18 on v16

--- a/solution.py
+++ b/solution.py
@@ -105,11 +105,11 @@
             ).astype(jnp.bfloat16)
             for start in (0, width)
         ]
-        first, partner_a = lax.optimization_barrier((grad_in[0], partner_a))
+        second, partner_a = lax.optimization_barrier((grad_in[1], partner_a))
         grad_rows = jnp.concatenate(
             [
-                lax.ppermute(first, RING, ring_route(sections, -1)),
-                lax.ppermute(grad_in[1], RING, ring_route(sections, -1)),
+                lax.ppermute(grad_in[0], RING, ring_route(sections, -1)),
+                lax.ppermute(second, RING, ring_route(sections, -1)),
             ],
             axis=-1,
         )

time: 232 us -> 232 us (level)
  no operation moved by 1% of the time
where the time goes in v18:
time: 232 us; the launch traced here: 231 us
  waiting for transfers between devices  80.2 us (35%)
  blocking collectives  67.6 us (29%)
  matrix products  46.1 us (20%)
  starting transfers between devices  13.2 us (6%)
  other arithmetic  12.8 us (6%)
  local copies, waits for them, and re-layouts  10.1 us (4%)
    all_to_all x1, blocking collectives, shards(): lax.all_to_all(picked, CHIPS, split_axis=0, concat_axis=0, tiled=True)  67.6 us
    ppermute x1, waiting for transfers between devices, swap_ylo(): return lax.ppermute(block, 'ylo', [(0, 1), (1, 0)])  59.2 us
    dot_general x2, matrix products, shards(): jnp.einsum('kech,dh->kecd', grad_pre, cols, preferred_element_type=jnp.fl...  18.4 us
    ppermute x1, waiting for transfers between devices, shards(): lax.ppermute(second, RING, ring_route(sections, -1))  16.8 us
    dot_general x1, matrix products, shards(): jnp.einsum('scd,dh->sch', jnp.concatenate([arrived[:half], partner_a]), w...  11.5 us
    dot_general x1, matrix products, shards(): jnp.einsum('scd,dh->sch', jnp.concatenate([arrived[half:], partner_b]), w...  7.76 us
    all_to_all x1, starting transfers between devices, shards(): lax.all_to_all(pair_sum, CHIPS, split_axis=0, concat_axis=0, tiled=True)  6.91 us
    dot_general x2, matrix products, shards(): jnp.einsum('ect,ecd->td', bwd_table, returned[..., start:start + width],...  6.91 us
  transfers between devices with their start and end apart: 9, of which 4 were waited for; matrix products, arithmetic and copies ran while one was open for 18% of the time, Pallas kernels for 0%

profile of v18, /device:TPU:30, one launch (start us, length us, event | category | flops | bytes accessed | tf_op | source)
XLA Modules:
  0.0 231.1 jit_solution(10544883435703064824)
XLA Ops:
  0.9 2.7 %gather_fusion.1 = bf16[16,48,512]{2,1,0:T(8,128)(2,1)} fusion(bf16[16,48,512]{2,1,0:T(8,128)(2,1)} %bitcast.87, s32[1024]{0:T(1024)S(1)} %pad_clamp_fusion.2), kind=kCustom, calls=%fused_computation.clone | custom fusion | bytes 1572928 | tf_op jit(solution)/shard_map/jit(_take)/gather | solution.py:76
  3.6 0.6 gather_fusion
  4.5 0.8 copy-done.2
  5.4 0.9 fusion.31
  6.3 9.2 %fusion.13 = bf16[2,8,48,3584]{3,2,1,0:T(8,128)(2,1)S(1)} fusion(bf16[1,1,7168,1024]{3,2,1,0:T(8,128)(2,1)} %param.10, bf16[2,8,48,512]{3,2,1,0:T(8,128)(2,1)S(1)} %bitcast.91, bf16[2,8,48,512]{3,2,1,0:T(8,128)(2,1)S(1)} %bitcast.89), kind=kOutput, calls=%fused_computation.15 | convolution fusion | flops 5643042816 | bytes 14417920 | tf_op jit(solution)/shard_map/kech,dh->kecd/dot_general | solution.py:82
  15.8 9.2 %fusion.10 = bf16[2,8,48,3584]{3,2,1,0:T(8,128)(2,1)S(1)} fusion(bf16[1,1,7168,1024]{3,2,1,0:T(8,128)(2,1)} %param.10, bf16[2,8,48,512]{3,2,1,0:T(8,128)(2,1)S(1)} %bitcast.92, bf16[2,8,48,512]{3,2,1,0:T(8,128)(2,1)S(1)} %bitcast.90), kind=kOutput, calls=%fused_computation.14 | convolution fusion | flops 5643042816 | bytes 14417920 | tf_op jit(solution)/shard_map/kech,dh->kecd/dot_general | solution.py:82
  25.2 0.6 collective-permute-start.2
  25.7 0.7 fusion.22
  26.4 4.0 %collective-permute-done.2 = bf16[8,48,3584]{2,1,0:T(8,128)(2,1)S(1)} collective-permute-done((bf16[8,48,3584]{2,1,0:T(8,128)(2,1)S(1)}, bf16[8,48,3584]{2,1,0:T(8,128)(2,1)S(1)}, u32[]{:S(2)}, u32[]{:S(2)}) %collective-permute-start.2) | collective-permute-done | bytes 2752544 | tf_op jit(solution)/shard_map/ppermute | solution.py:85
  30.5 0.7 fusion.23
  31.2 3.2 %pad_maximum_fusion = bf16[8,48,7168]{2,1,0:T(8,128)(2,1)} fusion(bf16[8,48,3584]{2,1,0:T(8,128)(2,1)S(1)} %fusion.22, bf16[8,48,3584]{2,1,0:T(8,128)(2,1)S(1)} %fusion.23), kind=kLoop, calls=%fused_computation.16 | loop fusion | flops 11010048 | bytes 11010048 | tf_op jit(solution)/shard_map/concatenate | solution.py:87
  34.4 6.9 %all-to-all-start = ((bf16[8,48,7168]{2,1,0:T(8,128)(2,1)}), bf16[8,48,7168]{2,1,0:T(8,128)(2,1)}, u32[]{:S(2)}, u32[]{:S(2)}) async-start(bf16[8,48,7168]{2,1,0:T(8,128)(2,1)} %pad_maximum_fusion), calls=%async_computation | async-start | bytes 11010048 | tf_op jit(solution)/shard_map/all_to_all | solution.py:88
  41.4 1.3 collective-permute-start
  42.7 59.2 %collective-permute-done = s32[128,4]{0,1:T(4,128)S(1)} collective-permute-done((s32[128,4]{0,1:T(4,128)S(1)}, s32[128,4]{0,1:T(4,128)S(1)}, u32[]{:S(2)}, u32[]{:S(2)}) %collective-permute-start) | collective-permute-done | bytes 2080 | tf_op jit(solution)/shard_map/ppermute | solution.py:23
  102.3 0.6 reduce-window.14
  104.3 1.6 convolution_convert_fusion
  105.9 67.6 %all_to_all.10 = bf16[8,48,7168]{2,1,0:T(8,128)(2,1)S(1)} all-to-all(bf16[8,48,7168]{2,1,0:T(8,128)(2,1)S(1)} %convolution_convert_fusion), channel_id=1, replica_groups=mesh['x'=4,'yhi'=2,'z'=4,'ylo'=2,'core'=2] {'z','ylo'}, dimensions={0} | all-to-all | bytes 11010048 | tf_op jit(solution)/shard_map/all_to_all | solution.py:95
  173.5 3.0 %fusion.68 = (bf16[4,48,7168]{2,1,0:T(8,128)(2,1)}, bf16[4,48,7168]{2,1,0:T(8,128)(2,1)}) fusion(bf16[8,48,7168]{2,1,0:T(8,128)(2,1)S(1)} %all_to_all.10), kind=kLoop, calls=%fused_computation.137 | loop fusion | bytes 11010048 | tf_op jit(solution)/shard_map/slice | solution.py:121
  176.9 0.6 reduce-window.16
  177.4 0.6 collective-permute-start.5
  178.8 0.3 bitcast_reduce_fusion
  179.3 3.4 %fusion.25 = bf16[128,3584]{1,0:T(8,128)(2,1)} fusion(bf16[8,48,7168]{2,1,0:T(8,128)(2,1)} %all-to-all-done, bf16[128,8,48]{0,2,1:T(8,128)(2,1)S(1)} %copy.31), kind=kOutput, calls=%fused_computation.30 | convolution fusion | flops 352780288 | bytes 3768320 | tf_op jit(solution)/shard_map/ect,ecd->td/dot_general | solution.py:102
  182.7 0.9 collective-permute-start.6
  183.6 3.5 %fusion.24 = bf16[128,3584]{1,0:T(8,128)(2,1)} fusion(bf16[8,48,7168]{2,1,0:T(8,128)(2,1)} %all-to-all-done, bf16[128,8,48]{0,2,1:T(8,128)(2,1)S(1)} %copy.31), kind=kOutput, calls=%fused_computation.29 | convolution fusion | flops 352780288 | bytes 3768320 | tf_op jit(solution)/shard_map/ect,ecd->td/dot_general | solution.py:102
  187.2 2.8 %collective-permute-start.7 = (bf16[128,3584]{1,0:T(8,128)(2,1)}, bf16[128,3584]{1,0:T(8,128)(2,1)}, u32[]{:S(2)}, u32[]{:S(2)}) collective-permute-start(bf16[128,3584]{1,0:T(8,128)(2,1)} %fusion.24), channel_id=1, source_target_pairs={{0,114},{2,112},{16,2},{18,0},{32,18},{34,16},{48,34},{50,32},{64,... | collective-permute-start | bytes 2752520 | tf_op jit(solution)/shard_map/ppermute | solution.py:112
  190.0 11.5 %fusion.2 = f32[8,48,1024]{2,1,0:T(8,128)S(1)} fusion(bf16[1,1,7168,1024]{3,2,1,0:T(8,128)(2,1)} %param.10, bf16[4,48,7168]{2,1,0:T(8,128)(2,1)} %collective-permute-done.4, bf16[4,48,7168]{2,1,0:T(8,128)(2,1)} %get-tuple-element.17), kind=kOutput, calls=%fused_computation.5 | convolution fusion | flops 5639897088 | bytes 21757952 | tf_op jit(solution)/shard_map/scd,dh->sch/dot_general | solution.py:119
  201.5 7.8 %fusion = f32[8,48,1024]{2,1,0:T(8,128)S(1)} fusion(bf16[1,1,7168,1024]{3,2,1,0:T(8,128)(2,1)S(1)} %bitcast.96, bf16[4,48,7168]{2,1,0:T(8,128)(2,1)} %collective-permute-done.5, bf16[4,48,7168]{2,1,0:T(8,128)(2,1)S(1)} %copy-done.3), kind=kOutput, calls=%fused_computation.3 | convolution fusion | flops 5639897088 | bytes 21757952 | tf_op jit(solution)/shard_map/scd,dh->sch/dot_general | solution.py:125
  209.3 0.5 fusion.36
  209.8 0.6 gather_fusion.2
  210.5 1.0 broadcast_select_fusion
  211.5 16.8 %collective-permute-done.7 = bf16[128,3584]{1,0:T(8,128)(2,1)} collective-permute-done((bf16[128,3584]{1,0:T(8,128)(2,1)}, bf16[128,3584]{1,0:T(8,128)(2,1)}, u32[]{:S(2)}, u32[]{:S(2)}) %collective-permute-start.7) | collective-permute-done | bytes 917536 | tf_op jit(solution)/shard_map/ppermute | solution.py:112
  228.3 2.8 %pad_maximum_fusion.1 = bf16[128,7168]{1,0:T(8,128)(2,1)} fusion(bf16[128,3584]{1,0:T(8,128)(2,1)} %collective-permute-done.7, bf16[128,3584]{1,0:T(8,128)(2,1)} %collective-permute-done.6), kind=kLoop, calls=%fused_computation.41 | loop fusion | flops 3670016 | bytes 3670016 | tf_op jit(solution)/shard_map/concatenate | solution.py:109
  (68 shorter events, 3.9 us)
Async XLA Ops:
  0.6 2.9 %copy-start = (bf16[1,1,16,48,1024]{4,3,2,1,0:T(8,128)(2,1)S(1)}, bf16[1,1,16,48,1024]{4,3,2,1,0:T(8,128)(2,1)}, u32[]{:S(2)}) copy-start(bf16[1,1,16,48,1024]{4,3,2,1,0:T(8,128)(2,1)} %param.13) | copy-start | bytes 4718596
  4.2 1.1 copy-start.2
  15.7 10.1 %collective-permute-start.3 = (bf16[8,48,3584]{2,1,0:T(8,128)(2,1)S(1)}, bf16[8,48,3584]{2,1,0:T(8,128)(2,1)S(1)}, u32[]{:S(2)}, u32[]{:S(2)}) collective-permute-start(bf16[8,48,3584]{2,1,0:T(8,128)(2,1)S(1)} %slice_bitcast_fusion), channel_id=1, source_target_pairs={{0,1},{1,0},{2,3},{3,2},{4,5},{5,4},{6,7},{7,6},{8,9},{9,8},{10,11... | collective-permute-start | bytes 8257544 | tf_op jit(solution)/shard_map/ppermute | solution.py:85
  25.2 5.3 %collective-permute-start.2 = (bf16[8,48,3584]{2,1,0:T(8,128)(2,1)S(1)}, bf16[8,48,3584]{2,1,0:T(8,128)(2,1)S(1)}, u32[]{:S(2)}, u32[]{:S(2)}) collective-permute-start(bf16[8,48,3584]{2,1,0:T(8,128)(2,1)S(1)} %slice_bitcast_fusion.2), channel_id=1, source_target_pairs={{0,1},{1,0},{2,3},{3,2},{4,5},{5,4},{6,7},{7,6},{8,9},{9,8},{10,11... | collective-permute-start | bytes 8257544 | tf_op jit(solution)/shard_map/ppermute | solution.py:85
  34.4 6.9 %copy-start.4 = (s32[1,128,2]{1,2,0:T(2,128)S(1)}, s32[1,128,2]{1,2,0:T(2,128)}, u32[]{:S(2)}) copy-start(s32[1,128,2]{1,2,0:T(2,128)} %param.11) | copy-start | bytes 3076
  34.4 6.9 %copy-start.5 = (s32[1,128,2]{1,2,0:T(2,128)S(1)}, s32[1,128,2]{1,2,0:T(2,128)}, u32[]{:S(2)}) copy-start(s32[1,128,2]{1,2,0:T(2,128)} %param.9) | copy-start | bytes 3076
  34.4 69.8 %all-to-all-start = ((bf16[8,48,7168]{2,1,0:T(8,128)(2,1)}), bf16[8,48,7168]{2,1,0:T(8,128)(2,1)}, u32[]{:S(2)}, u32[]{:S(2)}) async-start(bf16[8,48,7168]{2,1,0:T(8,128)(2,1)} %pad_maximum_fusion), calls=%async_computation | async-start | bytes 11010048 | tf_op jit(solution)/shard_map/all_to_all | solution.py:88
  41.3 62.7 %collective-permute-start.1 = (bf16[128,7168]{1,0:T(8,128)(2,1)}, bf16[128,7168]{1,0:T(8,128)(2,1)S(1)}, u32[]{:S(2)}, u32[]{:S(2)}) collective-permute-start(bf16[128,7168]{1,0:T(8,128)(2,1)} %bitcast.97), channel_id=1, source_target_pairs={{0,18},{2,16},{16,34},{18,32},{32,50},{34,48},{48,66},{50,64},{64,... | collective-permute-start | bytes 5505032 | tf_op jit(solution)/shard_map/ppermute | solution.py:73
  41.4 60.5 %collective-permute-start = (s32[128,4]{0,1:T(4,128)S(1)}, s32[128,4]{0,1:T(4,128)S(1)}, u32[]{:S(2)}, u32[]{:S(2)}) collective-permute-start(s32[128,4]{0,1:T(4,128)S(1)} %pad_add_fusion), channel_id=1, source_target_pairs={{0,2},{2,0},{1,3},{3,1},{4,6},{6,4},{5,7},{7,5},{8,10},{10,8},{9,1... | collective-permute-start | bytes 6152 | tf_op jit(solution)/shard_map/ppermute | solution.py:23
  176.5 10.6 %collective-permute-start.4 = (bf16[4,48,7168]{2,1,0:T(8,128)(2,1)}, bf16[4,48,7168]{2,1,0:T(8,128)(2,1)}, u32[]{:S(2)}, u32[]{:S(2)}) collective-permute-start(bf16[4,48,7168]{2,1,0:T(8,128)(2,1)} %get-tuple-element.17), channel_id=1, source_target_pairs={{0,1},{1,0},{2,3},{3,2},{4,5},{5,4},{6,7},{7,6},{8,9},{9,8},{10,11... | collective-permute-start | bytes 8257544 | tf_op jit(solution)/shard_map/ppermute | solution.py:98
  177.4 24.0 %collective-permute-start.5 = (bf16[4,48,7168]{2,1,0:T(8,128)(2,1)}, bf16[4,48,7168]{2,1,0:T(8,128)(2,1)}, u32[]{:S(2)}, u32[]{:S(2)}) collective-permute-start(bf16[4,48,7168]{2,1,0:T(8,128)(2,1)} %get-tuple-element.18), channel_id=1, source_target_pairs={{0,1},{1,0},{2,3},{3,2},{4,5},{5,4},{6,7},{7,6},{8,9},{9,8},{10,11... | collective-permute-start | bytes 8257544 | tf_op jit(solution)/shard_map/ppermute | solution.py:99
  182.7 28.8 %collective-permute-start.6 = (bf16[128,3584]{1,0:T(8,128)(2,1)}, bf16[128,3584]{1,0:T(8,128)(2,1)}, u32[]{:S(2)}, u32[]{:S(2)}) collective-permute-start(bf16[128,3584]{1,0:T(8,128)(2,1)} %fusion.25), channel_id=1, source_target_pairs={{0,114},{2,112},{16,2},{18,0},{32,18},{34,16},{48,34},{50,32},{64,... | collective-permute-start | bytes 2752520 | tf_op jit(solution)/shard_map/ppermute | solution.py:111
  183.6 17.9 %slice-start = ((s8[14680064]{0:T(1024)(128)(4,1)}), s8[4194304]{0:T(1024)(128)(4,1)S(1)}, s32[]{:S(2)}) async-start(s8[14680064]{0:T(1024)(128)(4,1)} %bitcast.95), calls=%async_computation.2 | async-start | bytes 8388608
  187.1 14.4 %copy-start.3 = (bf16[4,48,7168]{2,1,0:T(8,128)(2,1)S(1)}, bf16[4,48,7168]{2,1,0:T(8,128)(2,1)}, u32[]{:S(2)}) copy-start(bf16[4,48,7168]{2,1,0:T(8,128)(2,1)} %get-tuple-element.18) | copy-start | bytes 8257540
  187.1 14.4 %slice-start.1 = ((s8[14680064]{0:T(1024)(128)(4,1)}), s8[4194304]{0:T(1024)(128)(4,1)S(1)}, s32[]{:S(2)}) async-start(s8[14680064]{0:T(1024)(128)(4,1)} %bitcast.95), calls=%async_computation.3 | async-start | bytes 8388608
  187.1 14.4 %slice-start.2 = ((s8[14680064]{0:T(1024)(128)(4,1)}), s8[4194304]{0:T(1024)(128)(4,1)S(1)}, s32[]{:S(2)}) async-start(s8[14680064]{0:T(1024)(128)(4,1)} %bitcast.95), calls=%async_computation.4 | async-start | bytes 8388608
  187.1 14.4 %slice-start.3 = ((s8[14680064]{0:T(1024)(128)(4,1)}), s8[2097152]{0:T(1024)(128)(4,1)S(1)}, s32[]{:S(2)}) async-start(s8[14680064]{0:T(1024)(128)(4,1)} %bitcast.95), calls=%async_computation.5 | async-start | bytes 4194304
  187.2 41.1 %collective-permute-start.7 = (bf16[128,3584]{1,0:T(8,128)(2,1)}, bf16[128,3584]{1,0:T(8,128)(2,1)}, u32[]{:S(2)}, u32[]{:S(2)}) collective-permute-start(bf16[128,3584]{1,0:T(8,128)(2,1)} %fusion.24), channel_id=1, source_target_pairs={{0,114},{2,112},{16,2},{18,0},{32,18},{34,16},{48,34},{50,32},{64,... | collective-permute-start | bytes 2752520 | tf_op jit(solution)/shard_map/ppermute | solution.py:112
  209.8 21.3 %copy-start.1 = (bf16[1,1,16,48,1024]{4,3,2,1,0:T(8,128)(2,1)S(1)}, bf16[1,1,16,48,1024]{4,3,2,1,0:T(8,128)(2,1)}, u32[]{:S(2)}) copy-start(bf16[1,1,16,48,1024]{4,3,2,1,0:T(8,128)(2,1)} %param.13) | copy-start | bytes 4718596
